TPU v7x, 128 devices: a whole 4x4x4 slice. The times are simulated.
128 devices in a mesh: img: 8 (over y, core), fsdp: 16 (over x, z).
Axes of the slice: x: 4, y: 4, z: 4, core: 2. Of those that a mesh axis runs over, the one named last changes fastest.
Arguments:
- text_states: bfloat16 [4096, 8192], P('img', 'fsdp'), may hold values from -100 to 100, as said below
- text_gain: float32 [8192], P('fsdp'), may hold values from 0.1 to 1.9
- gate_scale: float32 [8192], P('fsdp'), may hold values from 0.3 to 1.5
- live_counts: int32 [8], P('img'), may hold values from 1 to 512, 3072 in all
- token_slot: int32 [8, 512], P('img'), may hold values from 0 to 7, never falling along the last dimension, each value on 1 to 256 neighbouring positions
- wanted_images: int32 [8, 8], replicated, may hold values from 0 to 31, as said below
- patches: bfloat16 [32, 256, 1280], P('img', None, 'fsdp'), may hold values from -100 to 100, as said below
- latent_init: bfloat16 [64, 1280], replicated, may hold values from -100 to 100, as said below
- context_gain: float32 [1280], replicated, may hold values from 0.1 to 1.9
- latent_gain: float32 [1280], replicated, may hold values from 0.1 to 1.9
- res_query: bfloat16 [1280, 1536], P(None, 'fsdp'), may hold values from -0.15625 to 0.15625
- res_key: bfloat16 [1280, 1536], P(None, 'fsdp'), may hold values from -0.15625 to 0.15625
- res_value: bfloat16 [1280, 1536], P(None, 'fsdp'), may hold values from -0.15625 to 0.15625
- res_out: bfloat16 [1536, 1280], P('fsdp'), may hold values from -0.21875 to 0.21875
- final_gain: float32 [1280], P('fsdp'), may hold values from 0.1 to 1.9
- cross_query: bfloat16 [8192, 8192], P('fsdp'), may hold values from -0.09375 to 0.09375
- cross_key: bfloat16 [1280, 8192], P('fsdp'), may hold values from -0.25 to 0.25
- cross_value: bfloat16 [1280, 8192], P('fsdp'), may hold values from -0.25 to 0.25
- cross_out: bfloat16 [8192, 8192], P('fsdp'), may hold values from -0.09375 to 0.09375
Outputs:
- layer_output: float32 [4096, 8192], P('img', 'fsdp')
Inputs may be any that keep to these rules, and one draw needn't show every extreme that they name: `wanted_images`: image i is held by owner i // 4 along img. A row lists 8 distinct images; every owner that appears in a row has exactly 2 of its images there. `token_slot`: along a shard's tokens the slot never falls, and every slot of the shard is used. Tokens of shard s at positions live_counts[s] and beyond are padding. `text_states`: real values. `patches`: real values. `latent_init`: real values.
All inputs are finite; a program needn't handle non-finite values.
Results may differ from a plain program's by a relative error of at most 0.0075.
Values may be sent and summed in bfloat16 or wider, within the bound.
No kernel may reach another device: no remote copies, remote signals or barrier semaphores. Data moves between devices by JAX's collectives and lax.ppermute only.
A program may use at most 128 MiB of HBM per device.

v0:
```python
import jax
import jax.numpy as jnp
from jax import lax
from jax.sharding import PartitionSpec as P

D = 8192
HEAD = 128
RHD = 96
PAIR = 2


eps_norm = 1e-05
eps_rms = 1e-06


def layer_norm(values, gain_vec):
    values = values.astype(jnp.float32)
    row_mean = jnp.mean(values, -1, keepdims=True)
    spread = jnp.mean(values * values, -1, keepdims=True) - row_mean * row_mean
    return (values - row_mean) * lax.rsqrt(spread + eps_norm) * gain_vec


def route_tables(wanted_images, per_owner, pair_slots):
    owners = wanted_images // per_owner
    slot_total = wanted_images.shape[1]
    positions = jnp.arange(slot_total, dtype=jnp.int32)
    before = (owners[:, :, None] == owners[:, None, :]) & (
        positions[None, None, :] < positions[None, :, None]
    )
    slot_rank = jnp.sum(before.astype(jnp.int32), axis=2)
    rank_hot = (
        slot_rank[:, :, None] == jnp.arange(pair_slots, dtype=jnp.int32)[None, None, :]
    ).astype(jnp.float32)
    return (owners, rank_hot)


def pack_rows(row_data, wanted_images, my_shard, per_owner, pair_slots):
    owners, rank_hot = route_tables(wanted_images, per_owner, pair_slots)
    is_mine = (owners == my_shard).astype(jnp.float32)
    local_hot = (
        (wanted_images % per_owner)[:, :, None]
        == jnp.arange(per_owner, dtype=jnp.int32)[None, None, :]
    ).astype(jnp.float32)
    picker = jnp.einsum("scp,sci->spi", rank_hot * is_mine[:, :, None], local_hot).astype(
        jnp.bfloat16
    )
    return jnp.einsum("spi,if->spf", picker, row_data, preferred_element_type=jnp.float32).astype(
        jnp.bfloat16
    )


def unpack_rows(received, wanted_images, my_shard, per_owner, pair_slots):
    owners, rank_hot = route_tables(wanted_images, per_owner, pair_slots)
    owner_row = lax.dynamic_slice_in_dim(owners, my_shard, 1, 0)[0]
    rank_row = lax.dynamic_slice_in_dim(rank_hot, my_shard, 1, 0)[0]
    source_hot = (
        owner_row[:, None] == jnp.arange(received.shape[0], dtype=jnp.int32)[None, :]
    ).astype(jnp.float32)
    taker = (source_hot[:, :, None] * rank_row[:, None, :]).astype(jnp.bfloat16)
    return jnp.einsum("cop,opf->cf", taker, received, preferred_element_type=jnp.float32).astype(
        jnp.bfloat16
    )


def keyval_partial(flat_rows, cross_key, cross_value, head_cols, row_count):
    contract_first = (((0,), (1,)), ((), ()))
    block_count = row_count // (2 * head_cols)
    key_cols = lax.dot_general(
        cross_key, flat_rows, contract_first, preferred_element_type=jnp.float32
    )
    value_cols = lax.dot_general(
        cross_value, flat_rows, contract_first, preferred_element_type=jnp.float32
    )
    key_cols = key_cols.reshape(block_count, head_cols, flat_rows.shape[0])
    value_cols = value_cols.reshape(block_count, head_cols, flat_rows.shape[0])
    return jnp.concatenate([key_cols, value_cols], 1).reshape(row_count, flat_rows.shape[0])


def local(
    text_states,
    text_gain,
    gate_scale,
    live_counts,
    token_slot,
    wanted_images,
    patches,
    latent_init,
    context_gain,
    latent_gain,
    res_query,
    res_key,
    res_value,
    res_out,
    final_gain,
    cross_query,
    cross_key,
    cross_value,
    cross_out,
):
    my_feature = lax.axis_index("fsdp")
    my_shard = lax.axis_index("img")
    image_count = patches.shape[0]
    patch_count = patches.shape[1]
    feat_vis = patches.shape[2]
    latent_count = latent_init.shape[0]
    vis_width = latent_init.shape[1]
    res_cols = res_query.shape[1]
    res_heads = res_cols // RHD
    head_cols = cross_out.shape[0]
    token_count = text_states.shape[0]
    slot_count = wanted_images.shape[1]
    cross_heads = head_cols // HEAD
    contract_first = (((0,), (1,)), ((), ()))
    full_patches = lax.all_gather(patches, "fsdp", axis=2, tiled=True)
    context = layer_norm(full_patches, context_gain).astype(jnp.bfloat16)
    latent_normed = layer_norm(latent_init, latent_gain).astype(jnp.bfloat16)
    res_q_rows = jnp.dot(latent_normed, res_query, preferred_element_type=jnp.float32).astype(
        jnp.bfloat16
    )
    res_q_rows = res_q_rows.reshape(latent_count, res_heads, RHD)
    ctx_keys = jnp.einsum(
        "npv,vk->npk", context, res_key, preferred_element_type=jnp.float32
    ).astype(jnp.bfloat16)
    ctx_values = jnp.einsum(
        "npv,vk->npk", context, res_value, preferred_element_type=jnp.float32
    ).astype(jnp.bfloat16)
    lat_keys = jnp.dot(latent_normed, res_key, preferred_element_type=jnp.float32).astype(
        jnp.bfloat16
    )
    lat_values = jnp.dot(latent_normed, res_value, preferred_element_type=jnp.float32).astype(
        jnp.bfloat16
    )
    joined_shape = (image_count, latent_count, res_cols)
    key_rows = jnp.concatenate([ctx_keys, jnp.broadcast_to(lat_keys[None], joined_shape)], 1)
    value_rows = jnp.concatenate([ctx_values, jnp.broadcast_to(lat_values[None], joined_shape)], 1)
    key_rows = key_rows.reshape(image_count, patch_count + latent_count, res_heads, RHD)
    value_rows = value_rows.reshape(image_count, patch_count + latent_count, res_heads, RHD)
    res_scores = jnp.einsum(
        "rhe,nkhe->nhrk", res_q_rows, key_rows, preferred_element_type=jnp.float32
    ) * RHD ** (-0.5)
    res_weights = jnp.exp(res_scores)
    res_weights = (res_weights / jnp.sum(res_weights, -1, keepdims=True)).astype(jnp.bfloat16)
    res_mixed = jnp.einsum(
        "nhrk,nkhe->nrhe", res_weights, value_rows, preferred_element_type=jnp.float32
    )
    res_mixed = res_mixed.astype(jnp.bfloat16).reshape(image_count * latent_count, res_cols)
    columns = res_out
    mixed_sum = lax.psum_scatter(
        lax.dot_general(
            columns, res_mixed, contract_first, preferred_element_type=jnp.float32
        ).astype(jnp.bfloat16),
        "fsdp",
        scatter_dimension=0,
        tiled=True,
    ).astype(jnp.float32)
    init_cols = lax.dynamic_slice_in_dim(latent_init, my_feature * feat_vis, feat_vis, 1).astype(
        jnp.float32
    )
    latents = init_cols[None] + jnp.transpose(mixed_sum).reshape(
        image_count, latent_count, feat_vis
    )
    sum_first, sum_second = lax.psum((jnp.sum(latents, -1), jnp.sum(latents * latents, -1)), "fsdp")
    row_mean = sum_first / vis_width
    spread = sum_second / vis_width - row_mean * row_mean
    resampled = (
        (latents - row_mean[..., None]) * lax.rsqrt(spread + eps_norm)[..., None] * final_gain
    ).astype(jnp.bfloat16)
    text_f = text_states.astype(jnp.float32)
    squares = lax.psum(jnp.sum(text_f * text_f, -1), "fsdp")
    normed = (text_f * lax.rsqrt(squares / D + eps_rms)[:, None] * text_gain).astype(jnp.bfloat16)
    columns = cross_query
    query_cols = lax.psum_scatter(
        lax.dot_general(columns, normed, contract_first, preferred_element_type=jnp.float32).astype(
            jnp.bfloat16
        ),
        "fsdp",
        scatter_dimension=0,
        tiled=True,
    )
    per_image = resampled.reshape(image_count, latent_count * feat_vis)
    outgoing = pack_rows(per_image, wanted_images, my_shard, image_count, PAIR)
    incoming = lax.all_to_all(outgoing, "img", split_axis=0, concat_axis=0, tiled=True)
    slot_latents = unpack_rows(incoming, wanted_images, my_shard, image_count, PAIR).reshape(
        slot_count * latent_count, feat_vis
    )
    slot_kv = lax.psum_scatter(
        keyval_partial(
            slot_latents, cross_key, cross_value, head_cols, 2 * head_cols * lax.axis_size("fsdp")
        ).astype(jnp.bfloat16),
        "fsdp",
        scatter_dimension=0,
        tiled=True,
    )
    kv_slots = jnp.transpose(slot_kv.reshape(2 * head_cols, slot_count, latent_count), (1, 0, 2))
    query_heads = query_cols.reshape(cross_heads, HEAD, token_count)
    slot_keys = kv_slots[:, :head_cols].reshape(slot_count, cross_heads, HEAD, latent_count)
    slot_values = kv_slots[:, head_cols:].reshape(slot_count, cross_heads, HEAD, latent_count)
    scores = jnp.einsum(
        "het,cher->htcr", query_heads, slot_keys, preferred_element_type=jnp.float32
    ) * HEAD ** (-0.5)
    slot_hot = (token_slot[0][:, None] == jnp.arange(slot_count, dtype=jnp.int32)[None, :]).astype(
        jnp.float32
    )
    weights = jnp.exp(scores) * slot_hot[None, :, :, None]
    weights = (weights / jnp.sum(weights, axis=(2, 3), keepdims=True)).astype(jnp.bfloat16)
    attended = jnp.einsum(
        "htcr,cher->het", weights, slot_values, preferred_element_type=jnp.float32
    )
    attended = attended.astype(jnp.bfloat16).reshape(head_cols, token_count)
    columns = cross_out
    projected_cols = lax.psum_scatter(
        lax.dot_general(
            columns, attended, (((0,), (0,)), ((), ())), preferred_element_type=jnp.float32
        ).astype(jnp.bfloat16),
        "fsdp",
        scatter_dimension=0,
        tiled=True,
    ).astype(jnp.float32)
    projected = jnp.transpose(projected_cols)
    positions = jnp.arange(token_count, dtype=jnp.int32)
    live_mask = (positions < live_counts[0]).astype(jnp.float32)[:, None]
    return text_f + jnp.tanh(gate_scale) * projected * live_mask


def solution(mesh):
    placed = (
        P("img", "fsdp"),
        P("fsdp"),
        P("fsdp"),
        P("img"),
        P("img", None),
        P(),
        P("img", None, "fsdp"),
        P(),
        P(),
        P(),
        P(None, "fsdp"),
        P(None, "fsdp"),
        P(None, "fsdp"),
        P("fsdp", None),
        P("fsdp"),
        P("fsdp", None),
        P("fsdp", None),
        P("fsdp", None),
        P("fsdp", None),
    )
    return jax.shard_map(
        local, mesh=mesh, in_specs=placed, out_specs=P("img", "fsdp"), check_vma=False
    )
```

profile of v0, /device:TPU:0, one launch (start us, length us, event | category | flops | bytes accessed | tf_op | source)
XLA Modules:
  0.0 494.0 jit_solution(16812852713913608499)
XLA Ops:
  6.5 0.0 all-gather.2.cloned.1.call-start
  6.6 0.7 all-gather.2.cloned.1.call-update
  7.3 0.0 reduce-scatter.13.cloned.1.call-start
  7.3 1.1 convert_reduce_fusion.1
  8.4 1.3 convolution_convert_fusion.10
  9.7 0.1 copy.37
  9.8 1.3 convolution_convert_fusion.11
  11.2 0.1 copy.35
  11.3 46.9 %all-gather.2.cloned.1.call-done = bf16[4,256,1280]{1,2,0:T(8,128)(2,1)} async-done(((bf16[4,256,80]{1,2,0:T(8,128)(2,1)}), bf16[4,256,1280]{1,2,0:T(8,128)(2,1)}) %all-gather.2.cloned.1.call-update) | async-done | bytes 2621456 | tf_op jit(solution)/shard_map/all_gather | solution.py:114
  58.2 2.4 convert_reduce_fusion
  60.6 2.8 convolution_convert_fusion.6
  63.5 0.6 fusion.69
  64.2 2.8 convolution_convert_fusion.7
  67.0 0.3 convolution_convert_fusion.8
  67.3 0.3 fusion.8
  67.7 1.1 copy.49
  68.7 0.0 reduce-scatter.13.cloned.1.call-update
  68.8 0.0 reduce-scatter.9.cloned.1.call-start
  68.8 0.1 dynamic-slice_convert_fusion
  68.9 0.2 fusion.15
  69.1 72.8 %reduce-scatter.13.cloned.1.call-done = bf16[80,256]{1,0:T(8,128)(2,1)} async-done(((bf16[1280,256]{1,0:T(8,128)(2,1)}), bf16[80,256]{1,0:T(8,128)(2,1)}) %reduce-scatter.13.cloned.1.call-update) | async-done | bytes 40976
  141.9 0.9 copy.50
  142.7 0.2 fusion.42
  142.9 0.1 reduce_sum.105
  143.0 0.1 reduce_sum.107
  143.1 38.6 %all-reduce = (f32[512]{0:T(512)S(1)}, f32[4,64]{1,0:T(4,128)S(1)}, f32[4,64]{1,0:T(4,128)S(1)}) all-reduce(f32[512]{0:T(512)S(1)} %fusion.15, f32[4,64]{1,0:T(4,128)S(1)} %reduce_sum.107, f32[4,64]{1,0:T(4,128)S(1)} %reduce_sum.105), channel_id=1, replica_groups=mesh['img'=8,'fsdp'=16] {'fsdp'}, use_global_device_ids=true, to_apply=%region_13.14 | all-reduce | flops 1024 | bytes 8192 | tf_op jit(solution)/shard_map/psum | solution.py:169
  181.7 10.2 %fusion = bf16[8192,512]{0,1:T(8,128)(2,1)} fusion(bf16[512,8192]{1,0:T(8,128)(2,1)} %param.34, bf16[512,512]{1,0:T(8,128)(2,1)S(1)} %copy-done.2, f32[512]{0:T(512)S(1)} %copy-done.14, f32[512]{0:T(512)S(1)} %add_rsqrt_fusion.1), kind=kOutput, calls=%fused_computation.5 | convolution fusion | flops 4300210176 | bytes 17305600 | tf_op jit(solution)/shard_map/dot_general | solution.py:173
  191.9 0.1 add.87
  192.0 0.5 copy-done.9
  192.6 0.1 mul.200
  192.7 0.3 convert_reduce_fusion.2
  193.0 0.1 convolution_convert_fusion.12
  193.2 0.1 mul.196
  193.3 0.2 mul.197
  193.4 0.1 sub.61
  193.5 0.2 sub.62
  193.7 0.1 reshape.193
  193.9 0.2 convolution_convert_fusion.4
  194.0 0.8 copy.39
  194.9 4.3 all-to-all-start
  199.2 0.2 reduce-scatter.7.cloned.1.call-start
  199.4 0.1 fusion.56
  199.5 6.2 %all-to-all-done = bf16[8,2,5120]{2,1,0:T(2,128)(2,1)S(1)} async-done(((bf16[8,2,5120]{2,1,0:T(2,128)(2,1)}), bf16[8,2,5120]{2,1,0:T(2,128)(2,1)S(1)}, u32[]{:S(2)}, u32[]{:S(2)}) %all-to-all-start) | async-done | bytes 163872 | tf_op jit(solution)/shard_map/all_to_all | solution.py:182
  205.6 0.3 fusion.2
  205.9 0.2 reshape.194
  206.1 5.6 %convolution_convert_fusion.3 = bf16[512,8192]{1,0:T(8,128)(2,1)} fusion(bf16[512,80]{1,0:T(8,128)(2,1)S(1)} %reshape.194, bf16[80,8192]{1,0:T(8,128)(2,1)S(1)} %copy-done), kind=kOutput, calls=%fused_computation.4 | convolution fusion | flops 675282944 | bytes 9781248 | tf_op jit(solution)/shard_map/dot_general | solution.py:68
  211.7 11.6 %copy.53 = bf16[64,8,16,512]{3,2,1,0:T(8,128)(2,1)} copy(bf16[64,8,16,512]{3,1,2,0:T(8,128)(2,1)} %bitcast.115) | data formatting | bytes 16777216
  223.2 5.5 %convolution_convert_fusion.2 = bf16[512,8192]{1,0:T(8,128)(2,1)} fusion(bf16[512,80]{1,0:T(8,128)(2,1)S(1)} %reshape.194, bf16[80,8192]{1,0:T(8,128)(2,1)S(1)} %copy-done.3), kind=kOutput, calls=%fused_computation.3 | convolution fusion | flops 675282944 | bytes 9781248 | tf_op jit(solution)/shard_map/dot_general | solution.py:71
  228.8 11.4 %copy.54 = bf16[64,8,16,512]{3,2,1,0:T(8,128)(2,1)} copy(bf16[64,8,16,512]{3,1,2,0:T(8,128)(2,1)} %bitcast.114) | data formatting | bytes 16777216
  240.2 8.4 %pad_maximum_fusion = bf16[16,1024,512]{1,0,2:T(8,128)(2,1)S(1)} fusion(bf16[16,512,512]{1,0,2:T(8,128)(2,1)} %bitcast.117, bf16[16,512,512]{1,0,2:T(8,128)(2,1)} %bitcast.116), kind=kLoop, calls=%fused_computation | loop fusion | flops 33554432 | bytes 33554432 | tf_op jit(solution)/shard_map/concatenate | solution.py:76
  248.6 12.0 %copy.55 = bf16[64,8,16,1024]{3,1,2,0:T(8,128)(2,1)} copy(bf16[64,8,16,1024]{3,2,1,0:T(8,128)(2,1)S(1)} %bitcast.113) | data formatting | bytes 33554432
  260.6 0.0 reduce-scatter.11.cloned.1.call-start
  260.7 0.6 copy-done.7
  261.3 13.3 %reduce-scatter.9.cloned.1.call-done = bf16[512,512]{0,1:T(8,128)(2,1)} async-done(((bf16[8192,512]{0,1:T(8,128)(2,1)}), bf16[512,512]{0,1:T(8,128)(2,1)}) %reduce-scatter.9.cloned.1.call-update) | async-done | bytes 524304 | tf_op jit(solution)/shard_map/reduce_scatter | solution.py:172
  274.5 1.3 copy.48
  275.8 112.3 %reduce-scatter.7.cloned.1.call-done = bf16[1024,512]{0,1:T(8,128)(2,1)} async-done(((bf16[16384,512]{0,1:T(8,128)(2,1)}), bf16[1024,512]{0,1:T(8,128)(2,1)}) %reduce-scatter.7.cloned.1.call-update) | async-done | bytes 1048592 | tf_op jit(solution)/shard_map/reduce_scatter | solution.py:186
  388.1 1.3 slice_bitcast_fusion.1
  389.4 0.9 fusion.7
  390.3 1.0 fusion.11
  391.4 0.2 slice-done
  391.6 1.5 slice-done.1
  393.1 6.9 %fusion.1 = bf16[8192,512]{0,1:T(8,128)(2,1)} fusion(bf16[512,512]{1,0:T(8,128)(2,1)S(1)} %bitcast.122, bf16[512,8192]{1,0:T(8,128)(2,1)S(1)} %bitcast.119), kind=kOutput, calls=%fused_computation.6 | convolution fusion | flops 4299161600 | bytes 17301504 | tf_op jit(solution)/shard_map/dot_general | solution.py:212
  400.8 84.4 %reduce-scatter.11.cloned.1.call-done = bf16[512,512]{0,1:T(8,128)(2,1)} async-done(((bf16[8192,512]{0,1:T(8,128)(2,1)}), bf16[512,512]{0,1:T(8,128)(2,1)}) %reduce-scatter.11.cloned.1.call-update) | async-done | bytes 524304 | tf_op jit(solution)/shard_map/reduce_scatter | solution.py:211
  485.3 2.2 convert_add_fusion
  (51 shorter events, 0.3 us)
Async XLA Ops:
  6.5 199.6 %copy-start = (bf16[80,8192]{1,0:T(8,128)(2,1)S(1)}, bf16[80,8192]{1,0:T(8,128)(2,1)}, u32[]{:S(2)}) copy-start(bf16[80,8192]{1,0:T(8,128)(2,1)} %param.35) | copy-start | bytes 3932164
  6.5 56.9 %copy-start.5 = (bf16[64,1280]{1,0:T(8,128)(2,1)S(1)}, bf16[64,1280]{1,0:T(8,128)(2,1)}, u32[]{:S(2)}) copy-start(bf16[64,1280]{1,0:T(8,128)(2,1)} %param.26) | copy-start | bytes 491524
  6.5 56.9 %copy-start.12 = (f32[1280]{0:T(1024)S(1)}, f32[1280]{0:T(1024)}, u32[]{:S(2)}) copy-start(f32[1280]{0:T(1024)} %param.28) | copy-start | bytes 15364
  6.5 56.9 %copy-start.10 = (bf16[1280,96]{0,1:T(8,128)(2,1)S(1)}, bf16[1280,96]{0,1:T(8,128)(2,1)}, u32[]{:S(2)}) copy-start(bf16[1280,96]{0,1:T(8,128)(2,1)} %param.29) | copy-start | bytes 737284
  6.5 51.6 %all-gather.2.cloned.1.call-start = ((), (), s32[]{:S(2)}) async-start(), calls=%async_computation.5 | async-start | bytes 2785280 | tf_op jit(solution)/shard_map/all_gather | solution.py:114
  7.3 134.6 %reduce-scatter.13.cloned.1.call-start = ((), (), s32[]{:S(2)}) async-start(), calls=%async_computation.9 | async-start | bytes 696320
  9.8 54.3 %copy-start.11 = (bf16[1280,96]{0,1:T(8,128)(2,1)S(1)}, bf16[1280,96]{0,1:T(8,128)(2,1)}, u32[]{:S(2)}) copy-start(bf16[1280,96]{0,1:T(8,128)(2,1)} %param.31) | copy-start | bytes 737284
  9.8 54.3 %copy-start.13 = (f32[1280]{0:T(1024)S(1)}, f32[1280]{0:T(1024)}, u32[]{:S(2)}) copy-start(f32[1280]{0:T(1024)} %param.27) | copy-start | bytes 15364
  63.4 3.9 copy-start.4
  64.1 4.8 copy-start.2
  64.1 117.5 %copy-start.14 = (f32[512]{0:T(512)S(1)}, f32[512]{0:T(512)}, u32[]{:S(2)}) copy-start(f32[512]{0:T(512)} %param.20) | copy-start | bytes 6148
  68.8 205.8 %reduce-scatter.9.cloned.1.call-start = ((), (), s32[]{:S(2)}) async-start(), calls=%async_computation.7 | async-start | bytes 8912896 | tf_op jit(solution)/shard_map/reduce_scatter | solution.py:172
  191.9 0.7 copy-start.9
  191.9 0.7 copy-start.6
  194.9 10.7 %all-to-all-start = ((bf16[8,2,5120]{2,1,0:T(2,128)(2,1)}), bf16[8,2,5120]{2,1,0:T(2,128)(2,1)S(1)}, u32[]{:S(2)}, u32[]{:S(2)}) async-start(bf16[8,2,5120]{2,1,0:T(2,128)(2,1)} %copy.39), calls=%async_computation | async-start | bytes 327680 | tf_op jit(solution)/shard_map/all_to_all | solution.py:182
  199.2 188.9 %reduce-scatter.7.cloned.1.call-start = ((), (), s32[]{:S(2)}) async-start(), calls=%async_computation.6 | async-start | bytes 17825792 | tf_op jit(solution)/shard_map/reduce_scatter | solution.py:186
  211.7 11.6 %copy-start.3 = (bf16[80,8192]{1,0:T(8,128)(2,1)S(1)}, bf16[80,8192]{1,0:T(8,128)(2,1)}, u32[]{:S(2)}) copy-start(bf16[80,8192]{1,0:T(8,128)(2,1)} %param.36) | copy-start | bytes 3932164
  260.6 0.7 copy-start.7
  260.6 224.7 %reduce-scatter.11.cloned.1.call-start = ((), (), s32[]{:S(2)}) async-start(), calls=%async_computation.8 | async-start | bytes 8912896 | tf_op jit(solution)/shard_map/reduce_scatter | solution.py:211
  389.4 2.2 slice-start
  390.3 2.8 slice-start.1
  400.0 0.8 copy-start.8
  400.0 87.5 %copy-start.1 = (bf16[80,8192]{1,0:T(8,128)(2,1)S(1)}, bf16[80,8192]{1,0:T(8,128)(2,1)}, u32[]{:S(2)}) copy-start(bf16[80,8192]{1,0:T(8,128)(2,1)} %param.35) | copy-start | bytes 3932164
Sparse Core Ops, SparseCore 0:
  9.5 48.6 all-gather.1
  68.9 72.9 reduce-scatter.12
  192.1 82.4 reduce-scatter.8
  277.8 110.2 reduce-scatter.6
  400.2 85.0 reduce-scatter.10
where the time goes:
time: 495 us; the launch traced here: 494 us
  waiting for transfers between devices  337 us (68%)
  local copies, waits for them, and re-layouts  44.7 us (9%)
  matrix products  40.3 us (8%)
  blocking collectives  38.6 us (8%)
  other arithmetic  14.9 us (3%)
  between operations  14.3 us (3%)
    reduce_scatter x1, waiting for transfers between devices, local(): lax.psum_scatter(keyval_partial(slot_latents, cross_key, cross_value, hea...  112 us
    reduce_scatter x1, waiting for transfers between devices, local(): lax.psum_scatter(lax.dot_general(columns, attended, (((0,), (0,)), ((), (...  84.4 us
    unnamed x6, waiting for transfers between devices  73.5 us
    all_gather x1, waiting for transfers between devices, local(): full_patches = lax.all_gather(patches, 'fsdp', axis=2, tiled=True)  46.9 us
    unnamed x40, local copies, waits for them, and re-layouts  41.2 us
    psum x1, blocking collectives, local(): squares = lax.psum(jnp.sum(text_f * text_f, -1), 'fsdp')  38.6 us
    reduce_scatter x1, waiting for transfers between devices, local(): lax.psum_scatter(lax.dot_general(columns, normed, contract_first, preferr...  13.3 us
    dot_general x1, matrix products, local(): lax.dot_general(columns, normed, contract_first, preferred_element_type=j...  10.2 us
  transfers between devices with their start and end apart: 6, of which 6 were waited for; matrix products, arithmetic and copies ran while one was open for 13% of the time, Pallas kernels for 0%

commit v1 on v0

--- a/solution.py
+++ b/solution.py
@@ -62,18 +62,15 @@
     )
 
 
-def keyval_partial(flat_rows, cross_key, cross_value, head_cols, row_count):
-    contract_first = (((0,), (1,)), ((), ()))
-    block_count = row_count // (2 * head_cols)
-    key_cols = lax.dot_general(
-        cross_key, flat_rows, contract_first, preferred_element_type=jnp.float32
-    )
-    value_cols = lax.dot_general(
-        cross_value, flat_rows, contract_first, preferred_element_type=jnp.float32
-    )
-    key_cols = key_cols.reshape(block_count, head_cols, flat_rows.shape[0])
-    value_cols = value_cols.reshape(block_count, head_cols, flat_rows.shape[0])
-    return jnp.concatenate([key_cols, value_cols], 1).reshape(row_count, flat_rows.shape[0])
+def gather_blocks(block, axis_name, parts):
+    spread = jnp.broadcast_to(block[None], (parts,) + block.shape)
+    return lax.all_to_all(spread, axis_name, split_axis=0, concat_axis=0, tiled=True)
+
+
+def block_dot(rows, cols):
+    contracted = jnp.einsum("brk,bkc->brc", rows, cols, preferred_element_type=jnp.float32)
+    rounded = lax.reduce_precision(contracted, exponent_bits=8, mantissa_bits=7)
+    return jnp.sum(rounded, 0)
 
 
 def local(
@@ -99,6 +96,7 @@
 ):
     my_feature = lax.axis_index("fsdp")
     my_shard = lax.axis_index("img")
+    parts = lax.axis_size("fsdp")
     image_count = patches.shape[0]
     patch_count = patches.shape[1]
     feat_vis = patches.shape[2]
@@ -111,6 +109,21 @@
     slot_count = wanted_images.shape[1]
     cross_heads = head_cols // HEAD
     contract_first = (((0,), (1,)), ((), ()))
+    kv_weights = jnp.stack([cross_key, cross_value], 0).reshape(2, feat_vis, parts, head_cols)
+    kv_weights = lax.all_to_all(
+        jnp.transpose(kv_weights, (2, 0, 1, 3)), "fsdp", split_axis=0, concat_axis=0, tiled=True
+    )
+    text_f = text_states.astype(jnp.float32)
+    squares = jnp.sum(gather_blocks(jnp.sum(text_f * text_f, -1), "fsdp", parts), 0)
+    normed = (text_f * lax.rsqrt(squares / D + eps_rms)[:, None] * text_gain).astype(jnp.bfloat16)
+    query_cols = lax.psum_scatter(
+        lax.dot_general(
+            cross_query, normed, contract_first, preferred_element_type=jnp.float32
+        ).astype(jnp.bfloat16),
+        "fsdp",
+        scatter_dimension=0,
+        tiled=True,
+    )
     full_patches = lax.all_gather(patches, "fsdp", axis=2, tiled=True)
     context = layer_norm(full_patches, context_gain).astype(jnp.bfloat16)
     latent_normed = layer_norm(latent_init, latent_gain).astype(jnp.bfloat16)
@@ -144,37 +157,22 @@
         "nhrk,nkhe->nrhe", res_weights, value_rows, preferred_element_type=jnp.float32
     )
     res_mixed = res_mixed.astype(jnp.bfloat16).reshape(image_count * latent_count, res_cols)
-    columns = res_out
-    mixed_sum = lax.psum_scatter(
-        lax.dot_general(
-            columns, res_mixed, contract_first, preferred_element_type=jnp.float32
-        ).astype(jnp.bfloat16),
+    row_total = image_count * latent_count
+    row_part = row_total // parts
+    head_part = jnp.dot(res_mixed, res_out, preferred_element_type=jnp.float32).astype(jnp.bfloat16)
+    head_part = lax.all_to_all(
+        head_part.reshape(parts, row_part, vis_width), "fsdp", split_axis=0, concat_axis=0, tiled=True
+    )
+    my_rows = my_feature * row_part
+    init_rows = lax.dynamic_slice_in_dim(latent_init, my_rows % latent_count, row_part, 0)
+    latents = init_rows.astype(jnp.float32) + jnp.sum(head_part.astype(jnp.float32), 0)
+    full_gain = gather_blocks(final_gain, "fsdp", parts).reshape(vis_width)
+    resampled_rows = layer_norm(latents, full_gain).astype(jnp.bfloat16)
+    resampled = lax.all_to_all(
+        jnp.transpose(resampled_rows.reshape(row_part, parts, feat_vis), (1, 0, 2)),
         "fsdp",
-        scatter_dimension=0,
-        tiled=True,
-    ).astype(jnp.float32)
-    init_cols = lax.dynamic_slice_in_dim(latent_init, my_feature * feat_vis, feat_vis, 1).astype(
-        jnp.float32
-    )
-    latents = init_cols[None] + jnp.transpose(mixed_sum).reshape(
-        image_count, latent_count, feat_vis
-    )
-    sum_first, sum_second = lax.psum((jnp.sum(latents, -1), jnp.sum(latents * latents, -1)), "fsdp")
-    row_mean = sum_first / vis_width
-    spread = sum_second / vis_width - row_mean * row_mean
-    resampled = (
-        (latents - row_mean[..., None]) * lax.rsqrt(spread + eps_norm)[..., None] * final_gain
-    ).astype(jnp.bfloat16)
-    text_f = text_states.astype(jnp.float32)
-    squares = lax.psum(jnp.sum(text_f * text_f, -1), "fsdp")
-    normed = (text_f * lax.rsqrt(squares / D + eps_rms)[:, None] * text_gain).astype(jnp.bfloat16)
-    columns = cross_query
-    query_cols = lax.psum_scatter(
-        lax.dot_general(columns, normed, contract_first, preferred_element_type=jnp.float32).astype(
-            jnp.bfloat16
-        ),
-        "fsdp",
-        scatter_dimension=0,
+        split_axis=0,
+        concat_axis=0,
         tiled=True,
     )
     per_image = resampled.reshape(image_count, latent_count * feat_vis)
@@ -183,20 +181,14 @@
     slot_latents = unpack_rows(incoming, wanted_images, my_shard, image_count, PAIR).reshape(
         slot_count * latent_count, feat_vis
     )
-    slot_kv = lax.psum_scatter(
-        keyval_partial(
-            slot_latents, cross_key, cross_value, head_cols, 2 * head_cols * lax.axis_size("fsdp")
-        ).astype(jnp.bfloat16),
-        "fsdp",
-        scatter_dimension=0,
-        tiled=True,
-    )
-    kv_slots = jnp.transpose(slot_kv.reshape(2 * head_cols, slot_count, latent_count), (1, 0, 2))
+    slot_blocks = gather_blocks(slot_latents, "fsdp", parts)
+    slot_keys = block_dot(slot_blocks, kv_weights[:, 0]).astype(jnp.bfloat16)
+    slot_values = block_dot(slot_blocks, kv_weights[:, 1]).astype(jnp.bfloat16)
+    slot_keys = slot_keys.reshape(slot_count, latent_count, cross_heads, HEAD)
+    slot_values = slot_values.reshape(slot_count, latent_count, cross_heads, HEAD)
     query_heads = query_cols.reshape(cross_heads, HEAD, token_count)
-    slot_keys = kv_slots[:, :head_cols].reshape(slot_count, cross_heads, HEAD, latent_count)
-    slot_values = kv_slots[:, head_cols:].reshape(slot_count, cross_heads, HEAD, latent_count)
     scores = jnp.einsum(
-        "het,cher->htcr", query_heads, slot_keys, preferred_element_type=jnp.float32
+        "het,crhe->htcr", query_heads, slot_keys, preferred_element_type=jnp.float32
     ) * HEAD ** (-0.5)
     slot_hot = (token_slot[0][:, None] == jnp.arange(slot_count, dtype=jnp.int32)[None, :]).astype(
         jnp.float32
@@ -204,13 +196,12 @@
     weights = jnp.exp(scores) * slot_hot[None, :, :, None]
     weights = (weights / jnp.sum(weights, axis=(2, 3), keepdims=True)).astype(jnp.bfloat16)
     attended = jnp.einsum(
-        "htcr,cher->het", weights, slot_values, preferred_element_type=jnp.float32
+        "htcr,crhe->het", weights, slot_values, preferred_element_type=jnp.float32
     )
     attended = attended.astype(jnp.bfloat16).reshape(head_cols, token_count)
-    columns = cross_out
     projected_cols = lax.psum_scatter(
         lax.dot_general(
-            columns, attended, (((0,), (0,)), ((), ())), preferred_element_type=jnp.float32
+            cross_out, attended, (((0,), (0,)), ((), ())), preferred_element_type=jnp.float32
         ).astype(jnp.bfloat16),
         "fsdp",
         scatter_dimension=0,

time: 495 us -> 313 us (0.63)
  waiting for transfers between devices: 337 us -> 189 us
  local copies, waits for them, and re-layouts: 44.7 us -> 16.9 us
  starting transfers between devices: 4.66 us -> 28.9 us
  blocking collectives: 38.6 us -> 15.4 us
  other arithmetic: 14.9 us -> 7.65 us
    reduce_scatter x3 -> x2, waiting for transfers between devices: 210 us -> 84.2 us  [the longest x1 84.2 us: local(): lax.psum_scatter(lax.dot_general(cross_out, attended, (((0,), (0,)), ((),...]
    all_to_all x0 -> x5, waiting for transfers between devices: none -> 83.8 us  [the longest x1 36.3 us: local(): lax.all_to_all(jnp.transpose(kv_weights, (2, 0, 1, 3)), 'fsdp', split_axi...]
    unnamed x6 -> x3, waiting for transfers between devices: 73.5 us -> 0.74 us
    psum x1 -> x0, blocking collectives: 38.6 us -> none  [local(): squares = lax.psum(jnp.sum(text_f * text_f, -1), 'fsdp')]
    unnamed x40 -> x36, local copies, waits for them, and re-layouts: 41.2 us -> 4.66 us
    all_gather x1, waiting for transfers between devices: 46.9 us -> 17.2 us  [local(): full_patches = lax.all_gather(patches, 'fsdp', axis=2, tiled=True)]
    all_to_all x0 -> x5, starting transfers between devices: none -> 24.4 us  [the longest x2 11.3 us: gather_blocks(): lax.all_to_all(spread, axis_name, split_axis=0, concat_axis=0, tiled=True)]
    all_to_all x0 -> x1, blocking collectives: none -> 15.4 us  [gather_blocks(): lax.all_to_all(spread, axis_name, split_axis=0, concat_axis=0, tiled=True)]
  transfers between devices with their start and end apart: 6 -> 9, of which waited for: 6 -> 7; matrix products, arithmetic and copies ran while one was open for 13% -> 16% of each run, Pallas kernels for 0% -> 0%
where the time goes in v1:
time: 313 us; the launch traced here: 312 us
  waiting for transfers between devices  189 us (60%)
  matrix products  39.2 us (13%)
  starting transfers between devices  28.9 us (9%)
  local copies, waits for them, and re-layouts  16.9 us (5%)
  blocking collectives  15.4 us (5%)
  between operations  14.3 us (5%)
  other arithmetic  7.65 us (2%)
    reduce_scatter x1, waiting for transfers between devices, local(): lax.psum_scatter(lax.dot_general(cross_out, attended, (((0,), (0,)), ((),...  84.2 us
    all_to_all x1, waiting for transfers between devices, local(): lax.all_to_all(jnp.transpose(kv_weights, (2, 0, 1, 3)), 'fsdp', split_axi...  36.3 us
    all_to_all x2, waiting for transfers between devices, gather_blocks(): lax.all_to_all(spread, axis_name, split_axis=0, concat_axis=0, tiled=True)  27.2 us
    all_gather x1, waiting for transfers between devices, local(): full_patches = lax.all_gather(patches, 'fsdp', axis=2, tiled=True)  17.2 us
    all_to_all x1, blocking collectives, gather_blocks(): lax.all_to_all(spread, axis_name, split_axis=0, concat_axis=0, tiled=True)  15.4 us
    all_to_all x1, waiting for transfers between devices, local(): lax.all_to_all(head_part.reshape(parts, row_part, vis_width), 'fsdp', spl...  14.7 us
    dot_general x1, matrix products, local(): lax.dot_general(cross_query, normed, contract_first, preferred_element_ty...  11.4 us
    all_to_all x2, starting transfers between devices, gather_blocks(): lax.all_to_all(spread, axis_name, split_axis=0, concat_axis=0, tiled=True)  11.3 us
  transfers between devices with their start and end apart: 9, of which 7 were waited for; matrix products, arithmetic and copies ran while one was open for 16% of the time, Pallas kernels for 0%

profile of v1, /device:TPU:0, one launch (start us, length us, event | category | flops | bytes accessed | tf_op | source)
XLA Modules:
  0.0 311.5 jit_solution(16426772902584845038)
XLA Ops:
  6.5 0.7 all-gather.2.cloned.1.call-update
  7.3 1.2 fusion.14
  8.6 15.4 %all_to_all.37 = f32[16,1,512]{2,1,0:T(1,128)S(1)} all-to-all(f32[16,1,512]{2,1,0:T(1,128)S(1)} %broadcast_in_dim.17), channel_id=1, replica_groups=mesh['img'=8,'fsdp'=16] {'fsdp'}, dimensions={0} | all-to-all | bytes 65536 | tf_op jit(solution)/shard_map/all_to_all | solution.py:67
  24.0 11.4 %fusion = bf16[8192,512]{0,1:T(8,128)(2,1)} fusion(bf16[512,8192]{1,0:T(8,128)(2,1)} %param.34, bf16[512,512]{1,0:T(8,128)(2,1)} %param.19, f32[512]{0:T(512)} %param.20, f32[512]{0:T(512)S(1)} %add_rsqrt_fusion.1), kind=kOutput, calls=%fused_computation.4 | convolution fusion | flops 4300210176 | bytes 17305600 | tf_op jit(solution)/shard_map/dot_general | solution.py:120
  35.5 0.6 copy-done.9
  36.1 0.6 broadcast_in_dim.14
  36.7 3.5 %all-to-all-start.1 = ((f32[16,1,80]{2,1,0:T(1,128)}), f32[16,1,80]{2,1,0:T(1,128)S(1)}, u32[]{:S(2)}, u32[]{:S(2)}) async-start(f32[16,1,80]{2,1,0:T(1,128)} %broadcast_in_dim.14), calls=%async_computation.1 | async-start | bytes 16384 | tf_op jit(solution)/shard_map/all_to_all | solution.py:67
  40.2 0.1 convert_reduce_fusion.2
  40.4 0.3 convolution_convert_fusion.8
  40.6 0.1 copy.62
  40.8 0.3 convolution_convert_fusion.9
  41.0 0.1 copy.60
  41.1 17.2 %all-gather.2.cloned.1.call-done = bf16[4,256,1280]{1,2,0:T(8,128)(2,1)} async-done(((bf16[4,256,80]{1,2,0:T(8,128)(2,1)}), bf16[4,256,1280]{1,2,0:T(8,128)(2,1)}) %all-gather.2.cloned.1.call-update) | async-done | bytes 2621456 | tf_op jit(solution)/shard_map/all_gather | solution.py:127
  58.3 2.4 convert_reduce_fusion
  60.8 3.6 %convolution_convert_fusion.4 = bf16[4,256,96]{1,2,0:T(8,128)(2,1)} fusion(bf16[4,256,1280]{1,2,0:T(8,128)(2,1)} %all-gather.2.cloned.1.call-done, f32[1280]{0:T(1024)S(1)} %copy-done.13, f32[4,256]{1,0:T(4,128)S(1)} %get-tuple-element.14, f32[4,256]{1,0:T(4,128)S(1)} %get-tuple-element.13, bf16[1280,96]{0,1:T(8,128)(2,1)S(1)} %copy-done.10), kind=kOutput, calls=%fused_computation.33 | convolution fusion | flops 258310144 | bytes 3077120 | tf_op jit(solution)/shard_map/npv,vk->npk/dot_general | solution.py:134
  64.4 2.3 fusion.60
  66.8 2.0 convolution_convert_fusion.5
  68.9 0.3 convolution_convert_fusion.6
  69.2 1.2 convolution_convert_fusion.3
  70.3 4.8 %all-to-all-start = ((bf16[16,16,1280]{2,1,0:T(8,128)(2,1)}), bf16[16,16,1280]{2,1,0:T(8,128)(2,1)S(1)}, u32[]{:S(2)}, u32[]{:S(2)}) async-start(bf16[16,16,1280]{2,1,0:T(8,128)(2,1)} %bitcast.12), calls=%async_computation | async-start | bytes 1310720 | tf_op jit(solution)/shard_map/all_to_all | solution.py:163
  75.2 0.3 convert_reduce_fusion.3
  75.5 0.5 broadcast.192
  76.0 0.6 reduce.5
  76.6 0.1 mul.196
  76.6 14.7 %all-to-all-done = bf16[16,16,1280]{2,1,0:T(8,128)(2,1)S(1)} async-done(((bf16[16,16,1280]{2,1,0:T(8,128)(2,1)}), bf16[16,16,1280]{2,1,0:T(8,128)(2,1)S(1)}, u32[]{:S(2)}, u32[]{:S(2)}) %all-to-all-start) | async-done | bytes 655392 | tf_op jit(solution)/shard_map/all_to_all | solution.py:163
  91.4 0.1 convert_reduce_fusion.1
  91.5 0.1 fusion.37
  91.6 0.1 multiply_convert_fusion
  91.7 0.1 reshape.211
  91.8 0.6 copy.91
  92.5 4.6 %all-to-all-start.2 = ((bf16[16,16,80]{2,1,0:T(8,128)(2,1)}), bf16[16,16,80]{2,1,0:T(8,128)(2,1)S(1)}, u32[]{:S(2)}, u32[]{:S(2)}) async-start(bf16[16,16,80]{2,1,0:T(8,128)(2,1)} %bitcast.92), calls=%async_computation.2 | async-start | bytes 131072 | tf_op jit(solution)/shard_map/all_to_all | solution.py:171
  97.1 0.1 convolution_convert_fusion.10
  97.2 0.5 copy.82
  97.7 1.8 copy.83
  99.5 5.6 %all-to-all-done.2 = bf16[16,16,80]{2,1,0:T(8,128)(2,1)S(1)} async-done(((bf16[16,16,80]{2,1,0:T(8,128)(2,1)}), bf16[16,16,80]{2,1,0:T(8,128)(2,1)S(1)}, u32[]{:S(2)}, u32[]{:S(2)}) %all-to-all-start.2) | async-done | bytes 40992 | tf_op jit(solution)/shard_map/all_to_all | solution.py:171
  105.1 0.2 reshape.218
  105.3 0.2 convolution_convert_fusion.2
  105.4 0.8 copy.65
  106.3 4.4 %all-to-all-start.3 = ((bf16[8,2,5120]{2,1,0:T(2,128)(2,1)}), bf16[8,2,5120]{2,1,0:T(2,128)(2,1)S(1)}, u32[]{:S(2)}, u32[]{:S(2)}) async-start(bf16[8,2,5120]{2,1,0:T(2,128)(2,1)} %copy.65), calls=%async_computation.3 | async-start | bytes 327680 | tf_op jit(solution)/shard_map/all_to_all | solution.py:180
  110.7 0.2 maximum_bitcast_fusion
  110.9 3.0 copy.68
  113.9 3.2 %all-to-all-done.3 = bf16[8,2,5120]{2,1,0:T(2,128)(2,1)S(1)} async-done(((bf16[8,2,5120]{2,1,0:T(2,128)(2,1)}), bf16[8,2,5120]{2,1,0:T(2,128)(2,1)S(1)}, u32[]{:S(2)}, u32[]{:S(2)}) %all-to-all-start.3) | async-done | bytes 163872 | tf_op jit(solution)/shard_map/all_to_all | solution.py:180
  117.1 3.8 %all-to-all-start.5 = ((bf16[16,2,80,512]{3,2,1,0:T(8,128)(2,1)}), bf16[16,2,80,512]{3,2,1,0:T(8,128)(2,1)S(1)}, u32[]{:S(2)}, u32[]{:S(2)}) async-start(bf16[16,2,80,512]{3,2,1,0:T(8,128)(2,1)} %copy.68), calls=%async_computation.5 | async-start | bytes 5242880 | tf_op jit(solution)/shard_map/all_to_all | solution.py:113
  121.0 0.1 fusion.47
  121.0 0.3 fusion.2
  121.3 0.2 broadcast_in_dim.15
  121.5 0.1 copy.67
  121.6 36.3 %all-to-all-done.5 = bf16[16,2,80,512]{3,2,1,0:T(8,128)(2,1)S(1)} async-done(((bf16[16,2,80,512]{3,2,1,0:T(8,128)(2,1)}), bf16[16,2,80,512]{3,2,1,0:T(8,128)(2,1)S(1)}, u32[]{:S(2)}, u32[]{:S(2)}) %all-to-all-start.5) | async-done | bytes 2621472 | tf_op jit(solution)/shard_map/all_to_all | solution.py:113
  157.9 1.2 broadcast_in_dim.16
  159.1 7.8 %all-to-all-start.4 = ((bf16[16,512,80]{1,2,0:T(8,128)(2,1)}), bf16[16,512,80]{1,2,0:T(8,128)(2,1)}, u32[]{:S(2)}, u32[]{:S(2)}) async-start(bf16[16,512,80]{1,2,0:T(8,128)(2,1)} %broadcast_in_dim.16), calls=%async_computation.4 | async-start | bytes 2621440 | tf_op jit(solution)/shard_map/all_to_all | solution.py:67
  167.0 27.2 %all-to-all-done.4 = bf16[16,512,80]{1,2,0:T(8,128)(2,1)} async-done(((bf16[16,512,80]{1,2,0:T(8,128)(2,1)}), bf16[16,512,80]{1,2,0:T(8,128)(2,1)}, u32[]{:S(2)}, u32[]{:S(2)}) %all-to-all-start.4) | async-done | bytes 1310752 | tf_op jit(solution)/shard_map/all_to_all | solution.py:67
  194.2 3.7 %reduce-precision_reduce_fusion = bf16[512,512]{1,0:T(8,128)(2,1)S(1)} fusion(bf16[16,512,80]{1,2,0:T(8,128)(2,1)} %all-to-all-done.4, bf16[16,2,80,512]{3,2,1,0:T(8,128)(2,1)S(1)} %all-to-all-done.5), kind=kOutput, calls=%fused_computation | convolution fusion | flops 679215104 | bytes 3145728 | tf_op jit(solution)/shard_map/brk,bkc->brc/dot_general | solution.py:71
  198.0 0.9 convert_element_type.169
  198.9 1.2 copy.73
  200.0 4.6 %reduce-precision_reduce_fusion.1 = bf16[512,512]{1,0:T(8,128)(2,1)} fusion(bf16[16,512,80]{1,2,0:T(8,128)(2,1)} %all-to-all-done.4, bf16[16,2,80,512]{3,2,1,0:T(8,128)(2,1)S(1)} %all-to-all-done.5), kind=kOutput, calls=%fused_computation.1 | convolution fusion | flops 679215104 | bytes 3145728 | tf_op jit(solution)/shard_map/brk,bkc->brc/dot_general | solution.py:71
  204.7 1.2 convert_element_type.164
  205.9 1.3 copy.78
  207.1 0.9 fusion.7
  208.0 1.0 fusion.10
  209.1 0.2 slice-done
  209.3 1.5 slice-done.1
  210.8 7.0 %fusion.1 = bf16[8192,512]{0,1:T(8,128)(2,1)} fusion(bf16[512,512]{1,0:T(8,128)(2,1)S(1)} %bitcast.102, bf16[512,8192]{1,0:T(8,128)(2,1)S(1)} %bitcast.95), kind=kOutput, calls=%fused_computation.5 | convolution fusion | flops 4299161600 | bytes 17301504 | tf_op jit(solution)/shard_map/dot_general | solution.py:203
  218.6 84.2 %reduce-scatter.5.cloned.1.call-done = bf16[512,512]{0,1:T(8,128)(2,1)} async-done(((bf16[8192,512]{0,1:T(8,128)(2,1)}), bf16[512,512]{0,1:T(8,128)(2,1)}) %reduce-scatter.5.cloned.1.call-update) | async-done | bytes 524304 | tf_op jit(solution)/shard_map/reduce_scatter | solution.py:202
  302.8 2.2 convert_add_fusion
  (56 shorter events, 0.4 us)
Async XLA Ops:
  6.5 62.6 %copy-start = (bf16[96,1280]{1,0:T(8,128)(2,1)S(1)}, bf16[96,1280]{1,0:T(8,128)(2,1)}, u32[]{:S(2)}) copy-start(bf16[96,1280]{1,0:T(8,128)(2,1)} %param.32) | copy-start | bytes 737284
  6.5 51.8 %all-gather.2.cloned.1.call-start = ((), (), s32[]{:S(2)}) async-start(), calls=%async_computation.9 | async-start | bytes 2785280 | tf_op jit(solution)/shard_map/all_gather | solution.py:127
  7.3 198.6 %reduce-scatter.3.cloned.1.call-start = ((), (), s32[]{:S(2)}) async-start(), calls=%async_computation.10 | async-start | bytes 8912896 | tf_op jit(solution)/shard_map/reduce_scatter | solution.py:119
  35.4 0.7 copy-start.9
  35.4 4.8 %copy-start.5 = (bf16[64,1280]{1,0:T(8,128)(2,1)S(1)}, bf16[64,1280]{1,0:T(8,128)(2,1)}, u32[]{:S(2)}) copy-start(bf16[64,1280]{1,0:T(8,128)(2,1)} %param.26) | copy-start | bytes 491524
  35.4 4.9 %copy-start.10 = (bf16[1280,96]{0,1:T(8,128)(2,1)S(1)}, bf16[1280,96]{0,1:T(8,128)(2,1)}, u32[]{:S(2)}) copy-start(bf16[1280,96]{0,1:T(8,128)(2,1)} %param.30) | copy-start | bytes 737284
  35.4 4.9 %copy-start.12 = (f32[1280]{0:T(1024)S(1)}, f32[1280]{0:T(1024)}, u32[]{:S(2)}) copy-start(f32[1280]{0:T(1024)} %param.28) | copy-start | bytes 15364
  35.4 5.3 %copy-start.11 = (bf16[1280,96]{0,1:T(8,128)(2,1)S(1)}, bf16[1280,96]{0,1:T(8,128)(2,1)}, u32[]{:S(2)}) copy-start(bf16[1280,96]{0,1:T(8,128)(2,1)} %param.31) | copy-start | bytes 737284
  35.4 25.3 %copy-start.13 = (f32[1280]{0:T(1024)S(1)}, f32[1280]{0:T(1024)}, u32[]{:S(2)}) copy-start(f32[1280]{0:T(1024)} %param.27) | copy-start | bytes 15364
  36.7 33.7 %all-to-all-start.1 = ((f32[16,1,80]{2,1,0:T(1,128)}), f32[16,1,80]{2,1,0:T(1,128)S(1)}, u32[]{:S(2)}, u32[]{:S(2)}) async-start(f32[16,1,80]{2,1,0:T(1,128)} %broadcast_in_dim.14), calls=%async_computation.1 | async-start | bytes 16384 | tf_op jit(solution)/shard_map/all_to_all | solution.py:67
  60.7 6.0 %copy-start.2 = (bf16[4,256,1280]{1,2,0:T(8,128)(2,1)S(1)}, bf16[4,256,1280]{1,2,0:T(8,128)(2,1)}, u32[]{:S(2)}) copy-start(bf16[4,256,1280]{1,2,0:T(8,128)(2,1)} %all-gather.2.cloned.1.call-done) | copy-start | bytes 7864324
  66.8 2.1 copy-start.14
  66.8 8.4 %copy-start.6 = (s32[8,8]{1,0:T(8,128)S(1)}, s32[8,8]{1,0:T(8,128)}, u32[]{:S(2)}) copy-start(s32[8,8]{1,0:T(8,128)} %param.24) | copy-start | bytes 772
  68.8 28.4 %copy-start.4 = (bf16[80,8192]{1,0:T(8,128)(2,1)S(1)}, bf16[80,8192]{1,0:T(8,128)(2,1)}, u32[]{:S(2)}) copy-start(bf16[80,8192]{1,0:T(8,128)(2,1)} %param.35) | copy-start | bytes 3932164
  70.3 21.0 %all-to-all-start = ((bf16[16,16,1280]{2,1,0:T(8,128)(2,1)}), bf16[16,16,1280]{2,1,0:T(8,128)(2,1)S(1)}, u32[]{:S(2)}, u32[]{:S(2)}) async-start(bf16[16,16,1280]{2,1,0:T(8,128)(2,1)} %bitcast.12), calls=%async_computation | async-start | bytes 1310720 | tf_op jit(solution)/shard_map/all_to_all | solution.py:163
  92.5 12.6 %all-to-all-start.2 = ((bf16[16,16,80]{2,1,0:T(8,128)(2,1)}), bf16[16,16,80]{2,1,0:T(8,128)(2,1)S(1)}, u32[]{:S(2)}, u32[]{:S(2)}) async-start(bf16[16,16,80]{2,1,0:T(8,128)(2,1)} %bitcast.92), calls=%async_computation.2 | async-start | bytes 131072 | tf_op jit(solution)/shard_map/all_to_all | solution.py:171
  106.3 10.8 %all-to-all-start.3 = ((bf16[8,2,5120]{2,1,0:T(2,128)(2,1)}), bf16[8,2,5120]{2,1,0:T(2,128)(2,1)S(1)}, u32[]{:S(2)}, u32[]{:S(2)}) async-start(bf16[8,2,5120]{2,1,0:T(2,128)(2,1)} %copy.65), calls=%async_computation.3 | async-start | bytes 327680 | tf_op jit(solution)/shard_map/all_to_all | solution.py:180
  113.9 53.1 %copy-start.7 = (s32[1,512]{1,0:T(1,128)S(1)}, s32[1,512]{1,0:T(1,128)}, u32[]{:S(2)}) copy-start(s32[1,512]{1,0:T(1,128)} %param.23) | copy-start | bytes 6148
  117.1 40.8 %all-to-all-start.5 = ((bf16[16,2,80,512]{3,2,1,0:T(8,128)(2,1)}), bf16[16,2,80,512]{3,2,1,0:T(8,128)(2,1)S(1)}, u32[]{:S(2)}, u32[]{:S(2)}) async-start(bf16[16,2,80,512]{3,2,1,0:T(8,128)(2,1)} %copy.68), calls=%async_computation.5 | async-start | bytes 5242880 | tf_op jit(solution)/shard_map/all_to_all | solution.py:113
  159.1 35.1 %all-to-all-start.4 = ((bf16[16,512,80]{1,2,0:T(8,128)(2,1)}), bf16[16,512,80]{1,2,0:T(8,128)(2,1)}, u32[]{:S(2)}, u32[]{:S(2)}) async-start(bf16[16,512,80]{1,2,0:T(8,128)(2,1)} %broadcast_in_dim.16), calls=%async_computation.4 | async-start | bytes 2621440 | tf_op jit(solution)/shard_map/all_to_all | solution.py:67
  167.0 135.8 %reduce-scatter.5.cloned.1.call-start = ((), (), s32[]{:S(2)}) async-start(), calls=%async_computation.11 | async-start | bytes 8912896 | tf_op jit(solution)/shard_map/reduce_scatter | solution.py:202
  207.1 2.2 slice-start
  208.0 2.8 slice-start.1
  217.8 87.2 %copy-start.1 = (bf16[96,1280]{1,0:T(8,128)(2,1)S(1)}, bf16[96,1280]{1,0:T(8,128)(2,1)}, u32[]{:S(2)}) copy-start(bf16[96,1280]{1,0:T(8,128)(2,1)} %param.32) | copy-start | bytes 737284
  217.8 0.7 copy-start.8
  217.8 85.0 %copy-start.3 = (bf16[512,512]{1,0:T(8,128)(2,1)S(1)}, bf16[512,512]{1,0:T(8,128)(2,1)}, u32[]{:S(2)}) copy-start(bf16[512,512]{1,0:T(8,128)(2,1)} %param.19) | copy-start | bytes 1572868
Sparse Core Ops, SparseCore 0:
  9.5 48.7 all-gather.1
  61.7 131.9 reduce-scatter.2
  217.9 84.7 reduce-scatter.4

commit v2 on v1

--- a/solution.py
+++ b/solution.py
@@ -109,10 +109,17 @@
     slot_count = wanted_images.shape[1]
     cross_heads = head_cols // HEAD
     contract_first = (((0,), (1,)), ((), ()))
-    kv_weights = jnp.stack([cross_key, cross_value], 0).reshape(2, feat_vis, parts, head_cols)
-    kv_weights = lax.all_to_all(
-        jnp.transpose(kv_weights, (2, 0, 1, 3)), "fsdp", split_axis=0, concat_axis=0, tiled=True
-    )
+    kv_stack = jnp.stack([cross_key, cross_value], 0)
+    kv_blocks = []
+    for shift in range(parts):
+        dest_cols = ((my_feature + shift) % parts) * head_cols
+        block = lax.dynamic_slice_in_dim(kv_stack, dest_cols, head_cols, 2)
+        if shift:
+            ring = [(j, (j + shift) % parts) for j in range(parts)]
+            block = lax.ppermute(block, "fsdp", ring)
+        kv_blocks.append(block)
+    kv_weights = jnp.stack(kv_blocks, 0)
+    block_source = (my_feature - jnp.arange(parts, dtype=jnp.int32)) % parts
     text_f = text_states.astype(jnp.float32)
     squares = jnp.sum(gather_blocks(jnp.sum(text_f * text_f, -1), "fsdp", parts), 0)
     normed = (text_f * lax.rsqrt(squares / D + eps_rms)[:, None] * text_gain).astype(jnp.bfloat16)
@@ -181,7 +188,7 @@
     slot_latents = unpack_rows(incoming, wanted_images, my_shard, image_count, PAIR).reshape(
         slot_count * latent_count, feat_vis
     )
-    slot_blocks = gather_blocks(slot_latents, "fsdp", parts)
+    slot_blocks = jnp.take(gather_blocks(slot_latents, "fsdp", parts), block_source, axis=0)
     slot_keys = block_dot(slot_blocks, kv_weights[:, 0]).astype(jnp.bfloat16)
     slot_values = block_dot(slot_blocks, kv_weights[:, 1]).astype(jnp.bfloat16)
     slot_keys = slot_keys.reshape(slot_count, latent_count, cross_heads, HEAD)

time: 313 us -> 315 us (level)
  waiting for transfers between devices: 189 us -> 136 us
  starting transfers between devices: 28.9 us -> 67.3 us
  local copies, waits for them, and re-layouts: 16.9 us -> 26.6 us
  other arithmetic: 7.65 us -> 13.7 us
    ppermute x0 -> x15, waiting for transfers between devices: none -> 44.3 us  [local(): block = lax.ppermute(block, 'fsdp', ring)]
    ppermute x0 -> x15, starting transfers between devices: none -> 40.4 us  [local(): block = lax.ppermute(block, 'fsdp', ring)]
    all_to_all x1 -> x0, waiting for transfers between devices: 36.3 us -> none  [local(): lax.all_to_all(jnp.transpose(kv_weights, (2, 0, 1, 3)), 'fsdp', split_axi...]
    all_to_all x2, waiting for transfers between devices: 27.2 us -> 0.4 us  [gather_blocks(): lax.all_to_all(spread, axis_name, split_axis=0, concat_axis=0, tiled=True)]
    all_gather x1, waiting for transfers between devices: 17.2 us -> 0.01 us  [local(): full_patches = lax.all_gather(patches, 'fsdp', axis=2, tiled=True)]
    all_to_all x1, waiting for transfers between devices: 14.7 us -> 0.01 us  [local(): lax.all_to_all(head_part.reshape(parts, row_part, vis_width), 'fsdp', spl...]
    unnamed x36 -> x76, local copies, waits for them, and re-layouts: 4.66 us -> 17.5 us
    all_to_all x2, starting transfers between devices: 11.3 us -> 7.17 us  [gather_blocks(): lax.all_to_all(spread, axis_name, split_axis=0, concat_axis=0, tiled=True)]
  transfers between devices with their start and end apart: 9 -> 23, of which waited for: 7 -> 10; matrix products, arithmetic and copies ran while one was open for 16% -> 21% of each run, Pallas kernels for 0% -> 0%
where the time goes in v2:
time: 315 us; the launch traced here: 314 us
  waiting for transfers between devices  136 us (43%)
  starting transfers between devices  67.3 us (21%)
  matrix products  40.4 us (13%)
  local copies, waits for them, and re-layouts  26.6 us (8%)
  blocking collectives  15.4 us (5%)
  between operations  14.4 us (5%)
  other arithmetic  13.7 us (4%)
    reduce_scatter x1, waiting for transfers between devices, local(): lax.psum_scatter(lax.dot_general(cross_out, attended, (((0,), (0,)), ((),...  84.7 us
    ppermute x15, waiting for transfers between devices, local(): block = lax.ppermute(block, 'fsdp', ring)  44.3 us
    ppermute x15, starting transfers between devices, local(): block = lax.ppermute(block, 'fsdp', ring)  40.4 us
    unnamed x76, local copies, waits for them, and re-layouts  17.5 us
    all_to_all x1, blocking collectives, gather_blocks(): lax.all_to_all(spread, axis_name, split_axis=0, concat_axis=0, tiled=True)  15.4 us
    dot_general x1, matrix products, local(): lax.dot_general(cross_query, normed, contract_first, preferred_element_ty...  11.5 us
    all_to_all x1, starting transfers between devices, local(): lax.all_to_all(head_part.reshape(parts, row_part, vis_width), 'fsdp', spl...  8.28 us
    dot_general x2, matrix products, block_dot(): jnp.einsum('brk,bkc->brc', rows, cols, preferred_element_type=jnp.float32)  7.71 us
  transfers between devices with their start and end apart: 23, of which 10 were waited for; matrix products, arithmetic and copies ran while one was open for 21% of the time, Pallas kernels for 0%

profile of v2, /device:TPU:0, one launch (start us, length us, event | category | flops | bytes accessed | tf_op | source)
XLA Modules:
  0.0 314.3 jit_solution(11577665753230252336)
XLA Ops:
  6.5 0.7 all-gather.2.cloned.1.call-update
  7.3 1.2 fusion.14
  8.6 15.4 %all_to_all.32 = f32[16,1,512]{2,1,0:T(1,128)S(1)} all-to-all(f32[16,1,512]{2,1,0:T(1,128)S(1)} %broadcast_in_dim.26), channel_id=1, replica_groups=mesh['img'=8,'fsdp'=16] {'fsdp'}, dimensions={0} | all-to-all | bytes 65536 | tf_op jit(solution)/shard_map/all_to_all | solution.py:67
  24.0 11.5 %fusion = bf16[8192,512]{0,1:T(8,128)(2,1)} fusion(bf16[512,8192]{1,0:T(8,128)(2,1)} %param.34, bf16[512,512]{1,0:T(8,128)(2,1)} %param.19, f32[512]{0:T(512)} %param.20, f32[512]{0:T(512)S(1)} %add_rsqrt_fusion.1), kind=kOutput, calls=%fused_computation.5 | convolution fusion | flops 4300210176 | bytes 17305600 | tf_op jit(solution)/shard_map/dot_general | solution.py:127
  36.7 3.5 %all-to-all-start.1 = ((f32[16,1,80]{2,1,0:T(1,128)}), f32[16,1,80]{2,1,0:T(1,128)S(1)}, u32[]{:S(2)}, u32[]{:S(2)}) async-start(f32[16,1,80]{2,1,0:T(1,128)} %broadcast_in_dim.22), calls=%async_computation.1 | async-start | bytes 16384 | tf_op jit(solution)/shard_map/all_to_all | solution.py:67
  40.3 4.1 %collective-permute-start.12 = (bf16[2,80,512]{2,1,0:T(8,128)(2,1)S(1)}, bf16[2,80,512]{2,1,0:T(8,128)(2,1)}, u32[]{:S(2)}, u32[]{:S(2)}) collective-permute-start(bf16[2,80,512]{2,1,0:T(8,128)(2,1)S(1)} %get-tuple-element.23), channel_id=1, source_target_pairs={{0,13},{1,14},{2,15},{3,0},{4,1},{5,2},{6,3},{7,4},{8,5},{9,6},{10... | collective-permute-start | bytes 491528 | tf_op jit(solution)/shard_map/ppermute | solution.py:119
  44.4 2.1 collective-permute-start.10
  46.4 1.2 collective-permute-start.11
  47.6 1.0 fusion.51
  48.6 1.1 collective-permute-start.13
  49.7 0.9 fusion.36
  53.7 0.7 convolution_convert_fusion.10
  54.5 1.3 fusion.54
  55.7 1.0 convolution_convert_fusion.8
  56.7 1.0 convolution_convert_fusion.9
  58.8 0.7 copy.109
  60.8 4.4 %collective-permute-start.1 = (bf16[2,80,512]{2,1,0:T(8,128)(2,1)}, bf16[2,80,512]{2,1,0:T(8,128)(2,1)S(1)}, u32[]{:S(2)}, u32[]{:S(2)}) collective-permute-start(bf16[2,80,512]{2,1,0:T(8,128)(2,1)} %get-tuple-element.13), channel_id=1, source_target_pairs={{0,2},{1,3},{2,4},{3,5},{4,6},{5,7},{6,8},{7,9},{8,10},{9,11},{10,... | collective-permute-start | bytes 491528 | tf_op jit(solution)/shard_map/ppermute | solution.py:119
  65.2 1.6 bitcast_dynamic-update-slice_fusion.13
  66.8 6.0 %collective-permute-done.1 = bf16[2,80,512]{2,1,0:T(8,128)(2,1)S(1)} collective-permute-done((bf16[2,80,512]{2,1,0:T(8,128)(2,1)}, bf16[2,80,512]{2,1,0:T(8,128)(2,1)S(1)}, u32[]{:S(2)}, u32[]{:S(2)}) %collective-permute-start.1) | collective-permute-done | bytes 163872 | tf_op jit(solution)/shard_map/ppermute | solution.py:119
  72.9 1.2 collective-permute-start.2
  74.7 5.8 %collective-permute-done.2 = bf16[2,80,512]{2,1,0:T(8,128)(2,1)S(1)} collective-permute-done((bf16[2,80,512]{2,1,0:T(8,128)(2,1)}, bf16[2,80,512]{2,1,0:T(8,128)(2,1)S(1)}, u32[]{:S(2)}, u32[]{:S(2)}) %collective-permute-start.2) | collective-permute-done | bytes 163872 | tf_op jit(solution)/shard_map/ppermute | solution.py:119
  80.6 3.8 %collective-permute-start.3 = (bf16[2,80,512]{2,1,0:T(8,128)(2,1)}, bf16[2,80,512]{2,1,0:T(8,128)(2,1)S(1)}, u32[]{:S(2)}, u32[]{:S(2)}) collective-permute-start(bf16[2,80,512]{2,1,0:T(8,128)(2,1)} %get-tuple-element.15), channel_id=1, source_target_pairs={{0,4},{1,5},{2,6},{3,7},{4,8},{5,9},{6,10},{7,11},{8,12},{9,13},{1... | collective-permute-start | bytes 491528 | tf_op jit(solution)/shard_map/ppermute | solution.py:119
  85.0 5.0 %collective-permute-done.3 = bf16[2,80,512]{2,1,0:T(8,128)(2,1)S(1)} collective-permute-done((bf16[2,80,512]{2,1,0:T(8,128)(2,1)}, bf16[2,80,512]{2,1,0:T(8,128)(2,1)S(1)}, u32[]{:S(2)}, u32[]{:S(2)}) %collective-permute-start.3) | collective-permute-done | bytes 163872 | tf_op jit(solution)/shard_map/ppermute | solution.py:119
  90.0 2.4 collective-permute-start.4
  92.4 0.7 bitcast_dynamic-update-slice_fusion.10
  93.1 2.6 convert_reduce_fusion
  95.8 2.7 convolution_convert_fusion.4
  99.2 3.0 fusion.82
  102.2 2.0 convolution_convert_fusion.5
  104.7 1.2 convolution_convert_fusion.3
  105.8 8.3 %all-to-all-start = ((bf16[16,16,1280]{2,1,0:T(8,128)(2,1)}), bf16[16,16,1280]{2,1,0:T(8,128)(2,1)S(1)}, u32[]{:S(2)}, u32[]{:S(2)}) async-start(bf16[16,16,1280]{2,1,0:T(8,128)(2,1)} %bitcast.12), calls=%async_computation | async-start | bytes 1310720 | tf_op jit(solution)/shard_map/all_to_all | solution.py:170
  114.1 4.4 %collective-permute-start.5 = (bf16[2,80,512]{2,1,0:T(8,128)(2,1)S(1)}, bf16[2,80,512]{2,1,0:T(8,128)(2,1)S(1)}, u32[]{:S(2)}, u32[]{:S(2)}) collective-permute-start(bf16[2,80,512]{2,1,0:T(8,128)(2,1)S(1)} %copy-done.10), channel_id=1, source_target_pairs={{0,6},{1,7},{2,8},{3,9},{4,10},{5,11},{6,12},{7,13},{8,14},{9,15},... | collective-permute-start | bytes 491528 | tf_op jit(solution)/shard_map/ppermute | solution.py:119
  118.5 1.6 bitcast_dynamic-update-slice_fusion.9
  120.1 13.9 %collective-permute-done.5 = bf16[2,80,512]{2,1,0:T(8,128)(2,1)S(1)} collective-permute-done((bf16[2,80,512]{2,1,0:T(8,128)(2,1)S(1)}, bf16[2,80,512]{2,1,0:T(8,128)(2,1)S(1)}, u32[]{:S(2)}, u32[]{:S(2)}) %collective-permute-start.5) | collective-permute-done | bytes 163872 | tf_op jit(solution)/shard_map/ppermute | solution.py:119
  134.0 1.7 collective-permute-start.6
  136.4 6.2 %collective-permute-done.6 = bf16[2,80,512]{2,1,0:T(8,128)(2,1)S(1)} collective-permute-done((bf16[2,80,512]{2,1,0:T(8,128)(2,1)S(1)}, bf16[2,80,512]{2,1,0:T(8,128)(2,1)S(1)}, u32[]{:S(2)}, u32[]{:S(2)}) %collective-permute-start.6) | collective-permute-done | bytes 163872 | tf_op jit(solution)/shard_map/ppermute | solution.py:119
  142.7 1.1 collective-permute-start.7
  145.5 6.0 %all-to-all-start.2 = ((bf16[16,16,80]{2,1,0:T(8,128)(2,1)}), bf16[16,16,80]{2,1,0:T(8,128)(2,1)S(1)}, u32[]{:S(2)}, u32[]{:S(2)}) async-start(bf16[16,16,80]{2,1,0:T(8,128)(2,1)} %bitcast.142), calls=%async_computation.2 | async-start | bytes 131072 | tf_op jit(solution)/shard_map/all_to_all | solution.py:178
  151.6 4.4 %collective-permute-start.8 = (bf16[2,80,512]{2,1,0:T(8,128)(2,1)S(1)}, bf16[2,80,512]{2,1,0:T(8,128)(2,1)S(1)}, u32[]{:S(2)}, u32[]{:S(2)}) collective-permute-start(bf16[2,80,512]{2,1,0:T(8,128)(2,1)S(1)} %copy-done.7), channel_id=1, source_target_pairs={{0,9},{1,10},{2,11},{3,12},{4,13},{5,14},{6,15},{7,0},{8,1},{9,2},... | collective-permute-start | bytes 491528 | tf_op jit(solution)/shard_map/ppermute | solution.py:119
  156.0 0.7 bitcast_dynamic-update-slice_fusion.6
  156.7 2.9 all-to-all-done.2
  159.9 0.8 copy.112
  160.7 5.4 %all-to-all-start.3 = ((bf16[8,2,5120]{2,1,0:T(2,128)(2,1)}), bf16[8,2,5120]{2,1,0:T(2,128)(2,1)S(1)}, u32[]{:S(2)}, u32[]{:S(2)}) async-start(bf16[8,2,5120]{2,1,0:T(2,128)(2,1)} %copy.112), calls=%async_computation.3 | async-start | bytes 327680 | tf_op jit(solution)/shard_map/all_to_all | solution.py:187
  166.1 2.4 collective-permute-start.9
  168.5 0.7 bitcast_dynamic-update-slice_fusion.5
  169.2 3.3 %all-to-all-done.3 = bf16[8,2,5120]{2,1,0:T(2,128)(2,1)S(1)} async-done(((bf16[8,2,5120]{2,1,0:T(2,128)(2,1)}), bf16[8,2,5120]{2,1,0:T(2,128)(2,1)S(1)}, u32[]{:S(2)}, u32[]{:S(2)}) %all-to-all-start.3) | async-done | bytes 163872 | tf_op jit(solution)/shard_map/all_to_all | solution.py:187
  173.1 1.2 broadcast_in_dim.24
  174.4 3.7 %all-to-all-start.4 = ((bf16[16,512,80]{1,2,0:T(8,128)(2,1)}), bf16[16,512,80]{1,2,0:T(8,128)(2,1)S(1)}, u32[]{:S(2)}, u32[]{:S(2)}) async-start(bf16[16,512,80]{1,2,0:T(8,128)(2,1)} %broadcast_in_dim.24), calls=%async_computation.4 | async-start | bytes 2621440 | tf_op jit(solution)/shard_map/all_to_all | solution.py:67
  178.2 5.5 %collective-permute-start.14 = (bf16[2,80,512]{2,1,0:T(8,128)(2,1)S(1)}, bf16[2,80,512]{2,1,0:T(8,128)(2,1)S(1)}, u32[]{:S(2)}, u32[]{:S(2)}) collective-permute-start(bf16[2,80,512]{2,1,0:T(8,128)(2,1)S(1)} %copy-done.11), channel_id=1, source_target_pairs={{0,15},{1,0},{2,1},{3,2},{4,3},{5,4},{6,5},{7,6},{8,7},{9,8},{10,9... | collective-permute-start | bytes 491528 | tf_op jit(solution)/shard_map/ppermute | solution.py:119
  184.4 1.6 bitcast_dynamic-update-slice_fusion.3
  186.0 1.6 bitcast_dynamic-update-slice_fusion.2
  187.6 1.6 bitcast_dynamic-update-slice_fusion.1
  189.2 1.6 bitcast_dynamic-update-slice_fusion
  190.8 7.3 %collective-permute-done.14 = bf16[2,80,512]{2,1,0:T(8,128)(2,1)S(1)} collective-permute-done((bf16[2,80,512]{2,1,0:T(8,128)(2,1)S(1)}, bf16[2,80,512]{2,1,0:T(8,128)(2,1)S(1)}, u32[]{:S(2)}, u32[]{:S(2)}) %collective-permute-start.14) | collective-permute-done | bytes 163872 | tf_op jit(solution)/shard_map/ppermute | solution.py:119
  199.2 0.8 gather_fusion
  199.9 3.9 %reduce-precision_reduce_fusion.1 = bf16[512,512]{1,0:T(8,128)(2,1)S(1)} fusion(bf16[16,2,80,512]{3,2,0,1:T(8,128)(2,1)} %bitcast_dynamic-update-slice_fusion.14, bf16[16,512,80]{1,2,0:T(8,128)(2,1)S(1)} %gather_fusion, pred[16]{0:T(512)(128)(4,1)S(1)} %copy-done.26), kind=kOutput, calls=%fused_computation.2 | convolution fusion | flops 679870464 | bytes 3145744 | tf_op jit(solution)/shard_map/brk,bkc->brc/dot_general | solution.py:71
  203.9 3.9 %reduce-precision_reduce_fusion = bf16[512,512]{1,0:T(8,128)(2,1)S(1)} fusion(bf16[16,2,80,512]{3,2,0,1:T(8,128)(2,1)} %bitcast_dynamic-update-slice_fusion.14, bf16[16,512,80]{1,2,0:T(8,128)(2,1)S(1)} %gather_fusion, pred[16]{0:T(512)(128)(4,1)S(1)} %copy-done.26), kind=kOutput, calls=%fused_computation.1 | convolution fusion | flops 679870464 | bytes 3145744 | tf_op jit(solution)/shard_map/brk,bkc->brc/dot_general | solution.py:71
  208.1 1.3 copy.136
  209.4 0.9 fusion.7
  210.3 1.0 fusion.10
  211.6 1.5 slice-done.1
  213.1 7.0 %fusion.1 = bf16[8192,512]{0,1:T(8,128)(2,1)} fusion(bf16[512,512]{1,0:T(8,128)(2,1)S(1)} %bitcast.156, bf16[512,8192]{1,0:T(8,128)(2,1)S(1)} %bitcast.153), kind=kOutput, calls=%fused_computation.6 | convolution fusion | flops 4299161600 | bytes 17301504 | tf_op jit(solution)/shard_map/dot_general | solution.py:210
  220.8 84.7 %reduce-scatter.5.cloned.1.call-done = bf16[512,512]{0,1:T(8,128)(2,1)} async-done(((bf16[8192,512]{0,1:T(8,128)(2,1)}), bf16[512,512]{0,1:T(8,128)(2,1)}) %reduce-scatter.5.cloned.1.call-update) | async-done | bytes 524304 | tf_op jit(solution)/shard_map/reduce_scatter | solution.py:209
  305.5 2.2 convert_add_fusion
  (131 shorter events, 15.1 us)
Async XLA Ops:
  6.5 98.1 %copy-start = (bf16[96,1280]{1,0:T(8,128)(2,1)S(1)}, bf16[96,1280]{1,0:T(8,128)(2,1)}, u32[]{:S(2)}) copy-start(bf16[96,1280]{1,0:T(8,128)(2,1)} %param.32) | copy-start | bytes 737284
  6.5 86.6 %all-gather.2.cloned.1.call-start = ((), (), s32[]{:S(2)}) async-start(), calls=%async_computation.8 | async-start | bytes 2785280 | tf_op jit(solution)/shard_map/all_gather | solution.py:134
  7.3 200.8 %reduce-scatter.3.cloned.1.call-start = ((), (), s32[]{:S(2)}) async-start(), calls=%async_computation.9 | async-start | bytes 8912896 | tf_op jit(solution)/shard_map/reduce_scatter | solution.py:126
  35.5 0.7 copy-start.21
  35.5 4.8 %copy-start.1 = (bf16[80,8192]{1,0:T(8,128)(2,1)S(1)}, bf16[80,8192]{1,0:T(8,128)(2,1)}, u32[]{:S(2)}) copy-start(bf16[80,8192]{1,0:T(8,128)(2,1)} %param.36) | copy-start | bytes 3932164
  35.5 4.8 %copy-start.2 = (bf16[80,8192]{1,0:T(8,128)(2,1)S(1)}, bf16[80,8192]{1,0:T(8,128)(2,1)}, u32[]{:S(2)}) copy-start(bf16[80,8192]{1,0:T(8,128)(2,1)} %param.35) | copy-start | bytes 3932164
  36.7 22.9 %all-to-all-start.1 = ((f32[16,1,80]{2,1,0:T(1,128)}), f32[16,1,80]{2,1,0:T(1,128)S(1)}, u32[]{:S(2)}, u32[]{:S(2)}) async-start(f32[16,1,80]{2,1,0:T(1,128)} %broadcast_in_dim.22), calls=%async_computation.1 | async-start | bytes 16384 | tf_op jit(solution)/shard_map/all_to_all | solution.py:67
  40.3 147.3 %collective-permute-start.12 = (bf16[2,80,512]{2,1,0:T(8,128)(2,1)S(1)}, bf16[2,80,512]{2,1,0:T(8,128)(2,1)}, u32[]{:S(2)}, u32[]{:S(2)}) collective-permute-start(bf16[2,80,512]{2,1,0:T(8,128)(2,1)S(1)} %get-tuple-element.23), channel_id=1, source_target_pairs={{0,13},{1,14},{2,15},{3,0},{4,1},{5,2},{6,3},{7,4},{8,5},{9,6},{10... | collective-permute-start | bytes 491528 | tf_op jit(solution)/shard_map/ppermute | solution.py:119
  44.4 140.0 %collective-permute-start.10 = (bf16[2,80,512]{2,1,0:T(8,128)(2,1)S(1)}, bf16[2,80,512]{2,1,0:T(8,128)(2,1)}, u32[]{:S(2)}, u32[]{:S(2)}) collective-permute-start(bf16[2,80,512]{2,1,0:T(8,128)(2,1)S(1)} %get-tuple-element.24), channel_id=1, source_target_pairs={{0,11},{1,12},{2,13},{3,14},{4,15},{5,0},{6,1},{7,2},{8,3},{9,4},{... | collective-permute-start | bytes 491528 | tf_op jit(solution)/shard_map/ppermute | solution.py:119
  46.4 139.5 %collective-permute-start.11 = (bf16[2,80,512]{2,1,0:T(8,128)(2,1)S(1)}, bf16[2,80,512]{2,1,0:T(8,128)(2,1)}, u32[]{:S(2)}, u32[]{:S(2)}) collective-permute-start(bf16[2,80,512]{2,1,0:T(8,128)(2,1)S(1)} %get-tuple-element.25), channel_id=1, source_target_pairs={{0,12},{1,13},{2,14},{3,15},{4,0},{5,1},{6,2},{7,3},{8,4},{9,5},{1... | collective-permute-start | bytes 491528 | tf_op jit(solution)/shard_map/ppermute | solution.py:119
  48.6 2.7 copy-start.15
  48.6 140.6 %collective-permute-start.13 = (bf16[2,80,512]{2,1,0:T(8,128)(2,1)}, bf16[2,80,512]{2,1,0:T(8,128)(2,1)}, u32[]{:S(2)}, u32[]{:S(2)}) collective-permute-start(bf16[2,80,512]{2,1,0:T(8,128)(2,1)} %get-tuple-element.17), channel_id=1, source_target_pairs={{0,14},{1,15},{2,0},{3,1},{4,2},{5,3},{6,4},{7,5},{8,6},{9,7},{10,... | collective-permute-start | bytes 491528 | tf_op jit(solution)/shard_map/ppermute | solution.py:119
  49.7 3.1 copy-start.5
  50.7 10.1 %collective-permute-start = (bf16[2,80,512]{2,1,0:T(8,128)(2,1)}, bf16[2,80,512]{2,1,0:T(8,128)(2,1)}, u32[]{:S(2)}, u32[]{:S(2)}) collective-permute-start(bf16[2,80,512]{2,1,0:T(8,128)(2,1)} %get-tuple-element.12), channel_id=1, source_target_pairs={{0,1},{1,2},{2,3},{3,4},{4,5},{5,6},{6,7},{7,8},{8,9},{9,10},{10,1... | collective-permute-start | bytes 491528 | tf_op jit(solution)/shard_map/ppermute | solution.py:119
  51.2 4.5 %copy-start.24 = (bf16[1280,96]{0,1:T(8,128)(2,1)S(1)}, bf16[1280,96]{0,1:T(8,128)(2,1)}, u32[]{:S(2)}) copy-start(bf16[1280,96]{0,1:T(8,128)(2,1)} %param.30) | copy-start | bytes 737284
  51.2 5.5 %copy-start.25 = (bf16[1280,96]{0,1:T(8,128)(2,1)S(1)}, bf16[1280,96]{0,1:T(8,128)(2,1)}, u32[]{:S(2)}) copy-start(bf16[1280,96]{0,1:T(8,128)(2,1)} %param.31) | copy-start | bytes 737284
  53.0 7.8 %copy-start.22 = (f32[64]{0:T(128)}, f32[64]{0:T(128)S(1)}, u32[]{:S(2)}) copy-start(f32[64]{0:T(128)S(1)} %get-tuple-element.32) | copy-start | bytes 772
  53.0 7.8 %copy-start.23 = (f32[64]{0:T(128)}, f32[64]{0:T(128)S(1)}, u32[]{:S(2)}) copy-start(f32[64]{0:T(128)S(1)} %get-tuple-element.33) | copy-start | bytes 772
  60.8 12.0 %collective-permute-start.1 = (bf16[2,80,512]{2,1,0:T(8,128)(2,1)}, bf16[2,80,512]{2,1,0:T(8,128)(2,1)S(1)}, u32[]{:S(2)}, u32[]{:S(2)}) collective-permute-start(bf16[2,80,512]{2,1,0:T(8,128)(2,1)} %get-tuple-element.13), channel_id=1, source_target_pairs={{0,2},{1,3},{2,4},{3,5},{4,6},{5,7},{6,8},{7,9},{8,10},{9,11},{10,... | collective-permute-start | bytes 491528 | tf_op jit(solution)/shard_map/ppermute | solution.py:119
  72.9 7.7 %collective-permute-start.2 = (bf16[2,80,512]{2,1,0:T(8,128)(2,1)}, bf16[2,80,512]{2,1,0:T(8,128)(2,1)S(1)}, u32[]{:S(2)}, u32[]{:S(2)}) collective-permute-start(bf16[2,80,512]{2,1,0:T(8,128)(2,1)} %get-tuple-element.14), channel_id=1, source_target_pairs={{0,3},{1,4},{2,5},{3,6},{4,7},{5,8},{6,9},{7,10},{8,11},{9,12},{10... | collective-permute-start | bytes 491528 | tf_op jit(solution)/shard_map/ppermute | solution.py:119
  80.6 9.5 %collective-permute-start.3 = (bf16[2,80,512]{2,1,0:T(8,128)(2,1)}, bf16[2,80,512]{2,1,0:T(8,128)(2,1)S(1)}, u32[]{:S(2)}, u32[]{:S(2)}) collective-permute-start(bf16[2,80,512]{2,1,0:T(8,128)(2,1)} %get-tuple-element.15), channel_id=1, source_target_pairs={{0,4},{1,5},{2,6},{3,7},{4,8},{5,9},{6,10},{7,11},{8,12},{9,13},{1... | collective-permute-start | bytes 491528 | tf_op jit(solution)/shard_map/ppermute | solution.py:119
  90.0 24.1 %collective-permute-start.4 = (bf16[2,80,512]{2,1,0:T(8,128)(2,1)}, bf16[2,80,512]{2,1,0:T(8,128)(2,1)}, u32[]{:S(2)}, u32[]{:S(2)}) collective-permute-start(bf16[2,80,512]{2,1,0:T(8,128)(2,1)} %get-tuple-element.16), channel_id=1, source_target_pairs={{0,5},{1,6},{2,7},{3,8},{4,9},{5,10},{6,11},{7,12},{8,13},{9,14},{... | collective-permute-start | bytes 491528 | tf_op jit(solution)/shard_map/ppermute | solution.py:119
  93.1 2.7 copy-start.3
  95.7 2.8 copy-start.18
  95.8 2.8 copy-start.19
  95.8 2.7 copy-start.12
  102.2 2.1 copy-start.27
  102.2 2.1 copy-start.28
  104.3 9.9 %copy-start.10 = (bf16[2,80,512]{2,1,0:T(8,128)(2,1)S(1)}, bf16[2,80,512]{2,1,0:T(8,128)(2,1)}, u32[]{:S(2)}) copy-start(bf16[2,80,512]{2,1,0:T(8,128)(2,1)} %get-tuple-element.18) | copy-start | bytes 491524
  104.3 29.8 %copy-start.9 = (bf16[2,80,512]{2,1,0:T(8,128)(2,1)S(1)}, bf16[2,80,512]{2,1,0:T(8,128)(2,1)}, u32[]{:S(2)}) copy-start(bf16[2,80,512]{2,1,0:T(8,128)(2,1)} %get-tuple-element.19) | copy-start | bytes 491524
  104.3 38.4 %copy-start.8 = (bf16[2,80,512]{2,1,0:T(8,128)(2,1)S(1)}, bf16[2,80,512]{2,1,0:T(8,128)(2,1)}, u32[]{:S(2)}) copy-start(bf16[2,80,512]{2,1,0:T(8,128)(2,1)} %get-tuple-element.20) | copy-start | bytes 491524
  104.6 47.0 %copy-start.7 = (bf16[2,80,512]{2,1,0:T(8,128)(2,1)S(1)}, bf16[2,80,512]{2,1,0:T(8,128)(2,1)}, u32[]{:S(2)}) copy-start(bf16[2,80,512]{2,1,0:T(8,128)(2,1)} %get-tuple-element.21) | copy-start | bytes 491524
  104.7 55.1 %copy-start.17 = (bf16[8,2,4]{2,1,0:T(2,128)(2,1)S(1)}, bf16[8,2,4]{2,1,0:T(2,128)(2,1)}, u32[]{:S(2)}) copy-start(bf16[8,2,4]{2,1,0:T(2,128)(2,1)} %convolution_convert_fusion.10) | copy-start | bytes 388
  105.8 60.3 %copy-start.6 = (bf16[2,80,512]{2,1,0:T(8,128)(2,1)S(1)}, bf16[2,80,512]{2,1,0:T(8,128)(2,1)}, u32[]{:S(2)}) copy-start(bf16[2,80,512]{2,1,0:T(8,128)(2,1)} %get-tuple-element.22) | copy-start | bytes 491524
  105.8 66.7 %copy-start.14 = (f32[8,8]{1,0:T(8,128)S(1)}, f32[8,8]{1,0:T(8,128)}, u32[]{:S(2)}) copy-start(f32[8,8]{1,0:T(8,128)} %fusion.63) | copy-start | bytes 772
  105.8 66.7 %copy-start.16 = (f32[8,2]{0,1:T(2,128)S(1)}, f32[8,2]{0,1:T(2,128)}, u32[]{:S(2)}) copy-start(f32[8,2]{0,1:T(2,128)} %fusion.67) | copy-start | bytes 196
  105.8 38.6 %all-to-all-start = ((bf16[16,16,1280]{2,1,0:T(8,128)(2,1)}), bf16[16,16,1280]{2,1,0:T(8,128)(2,1)S(1)}, u32[]{:S(2)}, u32[]{:S(2)}) async-start(bf16[16,16,1280]{2,1,0:T(8,128)(2,1)} %bitcast.12), calls=%async_computation | async-start | bytes 1310720 | tf_op jit(solution)/shard_map/all_to_all | solution.py:170
  114.1 19.9 %collective-permute-start.5 = (bf16[2,80,512]{2,1,0:T(8,128)(2,1)S(1)}, bf16[2,80,512]{2,1,0:T(8,128)(2,1)S(1)}, u32[]{:S(2)}, u32[]{:S(2)}) collective-permute-start(bf16[2,80,512]{2,1,0:T(8,128)(2,1)S(1)} %copy-done.10), channel_id=1, source_target_pairs={{0,6},{1,7},{2,8},{3,9},{4,10},{5,11},{6,12},{7,13},{8,14},{9,15},... | collective-permute-start | bytes 491528 | tf_op jit(solution)/shard_map/ppermute | solution.py:119
  134.0 8.6 %collective-permute-start.6 = (bf16[2,80,512]{2,1,0:T(8,128)(2,1)S(1)}, bf16[2,80,512]{2,1,0:T(8,128)(2,1)S(1)}, u32[]{:S(2)}, u32[]{:S(2)}) collective-permute-start(bf16[2,80,512]{2,1,0:T(8,128)(2,1)S(1)} %copy-done.9), channel_id=1, source_target_pairs={{0,7},{1,8},{2,9},{3,10},{4,11},{5,12},{6,13},{7,14},{8,15},{9,0},... | collective-permute-start | bytes 491528 | tf_op jit(solution)/shard_map/ppermute | solution.py:119
  142.7 8.9 %collective-permute-start.7 = (bf16[2,80,512]{2,1,0:T(8,128)(2,1)S(1)}, bf16[2,80,512]{2,1,0:T(8,128)(2,1)S(1)}, u32[]{:S(2)}, u32[]{:S(2)}) collective-permute-start(bf16[2,80,512]{2,1,0:T(8,128)(2,1)S(1)} %copy-done.8), channel_id=1, source_target_pairs={{0,8},{1,9},{2,10},{3,11},{4,12},{5,13},{6,14},{7,15},{8,0},{9,1},... | collective-permute-start | bytes 491528 | tf_op jit(solution)/shard_map/ppermute | solution.py:119
  145.5 14.0 %all-to-all-start.2 = ((bf16[16,16,80]{2,1,0:T(8,128)(2,1)}), bf16[16,16,80]{2,1,0:T(8,128)(2,1)S(1)}, u32[]{:S(2)}, u32[]{:S(2)}) async-start(bf16[16,16,80]{2,1,0:T(8,128)(2,1)} %bitcast.142), calls=%async_computation.2 | async-start | bytes 131072 | tf_op jit(solution)/shard_map/all_to_all | solution.py:178
  151.6 14.5 %collective-permute-start.8 = (bf16[2,80,512]{2,1,0:T(8,128)(2,1)S(1)}, bf16[2,80,512]{2,1,0:T(8,128)(2,1)S(1)}, u32[]{:S(2)}, u32[]{:S(2)}) collective-permute-start(bf16[2,80,512]{2,1,0:T(8,128)(2,1)S(1)} %copy-done.7), channel_id=1, source_target_pairs={{0,9},{1,10},{2,11},{3,12},{4,13},{5,14},{6,15},{7,0},{8,1},{9,2},... | collective-permute-start | bytes 491528 | tf_op jit(solution)/shard_map/ppermute | solution.py:119
  160.7 17.4 %copy-start.11 = (bf16[2,80,512]{2,1,0:T(8,128)(2,1)S(1)}, bf16[2,80,512]{2,1,0:T(8,128)(2,1)}, u32[]{:S(2)}) copy-start(bf16[2,80,512]{2,1,0:T(8,128)(2,1)} %get-tuple-element.11) | copy-start | bytes 491524
  160.7 11.8 %all-to-all-start.3 = ((bf16[8,2,5120]{2,1,0:T(2,128)(2,1)}), bf16[8,2,5120]{2,1,0:T(2,128)(2,1)S(1)}, u32[]{:S(2)}, u32[]{:S(2)}) async-start(bf16[8,2,5120]{2,1,0:T(2,128)(2,1)} %copy.112), calls=%async_computation.3 | async-start | bytes 327680 | tf_op jit(solution)/shard_map/all_to_all | solution.py:187
  166.1 12.0 %collective-permute-start.9 = (bf16[2,80,512]{2,1,0:T(8,128)(2,1)S(1)}, bf16[2,80,512]{2,1,0:T(8,128)(2,1)S(1)}, u32[]{:S(2)}, u32[]{:S(2)}) collective-permute-start(bf16[2,80,512]{2,1,0:T(8,128)(2,1)S(1)} %copy-done.6), channel_id=1, source_target_pairs={{0,10},{1,11},{2,12},{3,13},{4,14},{5,15},{6,0},{7,1},{8,2},{9,3},... | collective-permute-start | bytes 491528 | tf_op jit(solution)/shard_map/ppermute | solution.py:119
  174.4 24.8 %all-to-all-start.4 = ((bf16[16,512,80]{1,2,0:T(8,128)(2,1)}), bf16[16,512,80]{1,2,0:T(8,128)(2,1)S(1)}, u32[]{:S(2)}, u32[]{:S(2)}) async-start(bf16[16,512,80]{1,2,0:T(8,128)(2,1)} %broadcast_in_dim.24), calls=%async_computation.4 | async-start | bytes 2621440 | tf_op jit(solution)/shard_map/all_to_all | solution.py:67
  178.1 127.4 %reduce-scatter.5.cloned.1.call-start = ((), (), s32[]{:S(2)}) async-start(), calls=%async_computation.10 | async-start | bytes 8912896 | tf_op jit(solution)/shard_map/reduce_scatter | solution.py:209
  178.2 19.9 %collective-permute-start.14 = (bf16[2,80,512]{2,1,0:T(8,128)(2,1)S(1)}, bf16[2,80,512]{2,1,0:T(8,128)(2,1)S(1)}, u32[]{:S(2)}, u32[]{:S(2)}) collective-permute-start(bf16[2,80,512]{2,1,0:T(8,128)(2,1)S(1)} %copy-done.11), channel_id=1, source_target_pairs={{0,15},{1,0},{2,1},{3,2},{4,3},{5,4},{6,5},{7,6},{8,7},{9,8},{10,9... | collective-permute-start | bytes 491528 | tf_op jit(solution)/shard_map/ppermute | solution.py:119
  187.6 12.4 %copy-start.26 = (pred[16]{0:T(512)(128)(4,1)S(1)}, pred[16]{0:T(512)(128)(4,1)}, u32[]{:S(2)}) copy-start(pred[16]{0:T(512)(128)(4,1)} %compare_and_fusion) | copy-start | bytes 52
  207.8 1.5 copy-start.13
  209.4 2.2 slice-start
  210.3 2.8 slice-start.1
  220.0 0.7 copy-start.20
  220.0 85.5 %copy-start.4 = (bf16[512,512]{1,0:T(8,128)(2,1)S(1)}, bf16[512,512]{1,0:T(8,128)(2,1)}, u32[]{:S(2)}) copy-start(bf16[512,512]{1,0:T(8,128)(2,1)} %param.19) | copy-start | bytes 1572868
Sparse Core Ops, SparseCore 0:
  9.5 57.2 all-gather.1
  70.2 99.9 reduce-scatter.2
  220.2 85.3 reduce-scatter.4

commit v3 on v1

--- a/solution.py
+++ b/solution.py
@@ -114,11 +114,15 @@
         jnp.transpose(kv_weights, (2, 0, 1, 3)), "fsdp", split_axis=0, concat_axis=0, tiled=True
     )
     text_f = text_states.astype(jnp.float32)
-    squares = jnp.sum(gather_blocks(jnp.sum(text_f * text_f, -1), "fsdp", parts), 0)
-    normed = (text_f * lax.rsqrt(squares / D + eps_rms)[:, None] * text_gain).astype(jnp.bfloat16)
+    gained = (text_f * text_gain).astype(jnp.bfloat16)
+    after_weights = kv_weights[0, 0, 0, 0].astype(jnp.float32) * 0.0
+    stats = jnp.concatenate([jnp.sum(text_f * text_f, -1), final_gain], 0) + after_weights
+    stats = gather_blocks(stats, "fsdp", parts)
+    squares = jnp.sum(stats[:, :token_count], 0)
+    full_gain = stats[:, token_count:].reshape(vis_width)
     query_cols = lax.psum_scatter(
         lax.dot_general(
-            cross_query, normed, contract_first, preferred_element_type=jnp.float32
+            cross_query, gained, contract_first, preferred_element_type=jnp.float32
         ).astype(jnp.bfloat16),
         "fsdp",
         scatter_dimension=0,
@@ -166,7 +170,6 @@
     my_rows = my_feature * row_part
     init_rows = lax.dynamic_slice_in_dim(latent_init, my_rows % latent_count, row_part, 0)
     latents = init_rows.astype(jnp.float32) + jnp.sum(head_part.astype(jnp.float32), 0)
-    full_gain = gather_blocks(final_gain, "fsdp", parts).reshape(vis_width)
     resampled_rows = layer_norm(latents, full_gain).astype(jnp.bfloat16)
     resampled = lax.all_to_all(
         jnp.transpose(resampled_rows.reshape(row_part, parts, feat_vis), (1, 0, 2)),
@@ -186,6 +189,8 @@
     slot_values = block_dot(slot_blocks, kv_weights[:, 1]).astype(jnp.bfloat16)
     slot_keys = slot_keys.reshape(slot_count, latent_count, cross_heads, HEAD)
     slot_values = slot_values.reshape(slot_count, latent_count, cross_heads, HEAD)
+    token_scale = lax.rsqrt(squares / D + eps_rms)
+    query_cols = (query_cols.astype(jnp.float32) * token_scale[None, :]).astype(jnp.bfloat16)
     query_heads = query_cols.reshape(cross_heads, HEAD, token_count)
     scores = jnp.einsum(
         "het,crhe->htcr", query_heads, slot_keys, preferred_element_type=jnp.float32

time: 313 us -> 298 us (0.952)
  waiting for transfers between devices: 189 us -> 173 us
  blocking collectives: 15.4 us -> 0 us
  other arithmetic: 7.65 us -> 12.7 us
  matrix products: 39.2 us -> 43.8 us
  starting transfers between devices: 28.9 us -> 32.5 us
    all_gather x1, waiting for transfers between devices: 17.2 us -> 0.02 us  [local(): full_patches = lax.all_gather(patches, 'fsdp', axis=2, tiled=True)]
    all_to_all x1 -> x0, blocking collectives: 15.4 us -> none  [gather_blocks(): lax.all_to_all(spread, axis_name, split_axis=0, concat_axis=0, tiled=True)]
    all_to_all x1, starting transfers between devices: 3.78 us -> 8.12 us  [local(): lax.all_to_all(jnp.transpose(kv_weights, (2, 0, 1, 3)), 'fsdp', split_axi...]
    all_to_all x2, starting transfers between devices: 11.3 us -> 8.05 us  [gather_blocks(): lax.all_to_all(spread, axis_name, split_axis=0, concat_axis=0, tiled=True)]
    all_to_all x1, waiting for transfers between devices: 3.17 us -> 6.38 us  [local(): lax.all_to_all(outgoing, 'img', split_axis=0, concat_axis=0, tiled=True)]
    unnamed x36 -> x57, local copies, waits for them, and re-layouts: 4.66 us -> 6.53 us
  transfers between devices with their start and end apart: 9 -> 9, of which waited for: 7 -> 6; matrix products, arithmetic and copies ran while one was open for 16% -> 20% of each run, Pallas kernels for 0% -> 0%
where the time goes in v3:
time: 298 us; the launch traced here: 296 us
  waiting for transfers between devices  173 us (58%)
  matrix products  43.8 us (15%)
  starting transfers between devices  32.5 us (11%)
  local copies, waits for them, and re-layouts  19.6 us (7%)
  between operations  15 us (5%)
  other arithmetic  12.7 us (4%)
    reduce_scatter x1, waiting for transfers between devices, local(): lax.psum_scatter(lax.dot_general(cross_out, attended, (((0,), (0,)), ((),...  82.2 us
    all_to_all x1, waiting for transfers between devices, local(): lax.all_to_all(jnp.transpose(kv_weights, (2, 0, 1, 3)), 'fsdp', split_axi...  34.5 us
    all_to_all x2, waiting for transfers between devices, gather_blocks(): lax.all_to_all(spread, axis_name, split_axis=0, concat_axis=0, tiled=True)  26.2 us
    all_to_all x1, waiting for transfers between devices, local(): lax.all_to_all(head_part.reshape(parts, row_part, vis_width), 'fsdp', spl...  14.7 us
    dot_general x1, matrix products, local(): lax.dot_general(cross_query, gained, contract_first, preferred_element_ty...  11.3 us
    dot_general x2, matrix products, block_dot(): jnp.einsum('brk,bkc->brc', rows, cols, preferred_element_type=jnp.float32)  9.26 us
    all_to_all x1, starting transfers between devices, local(): lax.all_to_all(jnp.transpose(kv_weights, (2, 0, 1, 3)), 'fsdp', split_axi...  8.12 us
    all_to_all x2, starting transfers between devices, gather_blocks(): lax.all_to_all(spread, axis_name, split_axis=0, concat_axis=0, tiled=True)  8.05 us
  transfers between devices with their start and end apart: 9, of which 6 were waited for; matrix products, arithmetic and copies ran while one was open for 20% of the time, Pallas kernels for 0%

profile of v3, /device:TPU:0, one launch (start us, length us, event | category | flops | bytes accessed | tf_op | source)
XLA Modules:
  0.0 296.2 jit_solution(15240744373087057558)
XLA Ops:
  6.5 0.7 all-gather.2.cloned.1.call-update
  7.3 11.3 %fusion = bf16[8192,512]{0,1:T(8,128)(2,1)} fusion(bf16[512,8192]{1,0:T(8,128)(2,1)} %param.34, bf16[512,512]{1,0:T(8,128)(2,1)} %param.19, f32[512]{0:T(512)} %param.20), kind=kOutput, calls=%fused_computation.4 | convolution fusion | flops 4299948032 | bytes 17303552 | tf_op jit(solution)/shard_map/dot_general | solution.py:124
  18.7 1.3 copy-done.4
  20.0 0.5 copy.81
  20.4 0.5 copy.82
  20.9 0.2 maximum_bitcast_fusion
  21.1 3.1 %copy.63 = bf16[16,2,80,512]{3,2,1,0:T(8,128)(2,1)} copy(bf16[16,2,80,512]{3,0,2,1:T(8,128)(2,1)S(1)} %maximum_bitcast_fusion) | data formatting | bytes 5242880 | tf_op jit(solution)/shard_map/transpose | solution.py:114
  24.2 8.1 %all-to-all-start.1 = ((bf16[16,2,80,512]{3,2,1,0:T(8,128)(2,1)}), bf16[16,2,80,512]{3,2,1,0:T(8,128)(2,1)S(1)}, u32[]{:S(2)}, u32[]{:S(2)}) async-start(bf16[16,2,80,512]{3,2,1,0:T(8,128)(2,1)} %copy.63), calls=%async_computation.1 | async-start | bytes 5242880 | tf_op jit(solution)/shard_map/all_to_all | solution.py:113
  32.4 0.1 convert_reduce_fusion.2
  32.5 0.6 copy-done.17
  33.1 1.8 convolution_convert_fusion.8
  34.9 1.4 copy.62
  36.3 1.8 convolution_convert_fusion.9
  38.2 1.4 copy.60
  39.6 0.8 fusion.14
  40.4 1.3 compare_convert_fusion
  41.6 1.3 add_select_fusion.1
  43.0 34.5 %all-to-all-done.1 = bf16[16,2,80,512]{3,2,1,0:T(8,128)(2,1)S(1)} async-done(((bf16[16,2,80,512]{3,2,1,0:T(8,128)(2,1)}), bf16[16,2,80,512]{3,2,1,0:T(8,128)(2,1)S(1)}, u32[]{:S(2)}, u32[]{:S(2)}) %all-to-all-start.1) | async-done | bytes 2621472 | tf_op jit(solution)/shard_map/all_to_all | solution.py:113
  77.5 0.5 slice.20
  78.6 0.7 maximum_add_fusion
  79.3 0.6 broadcast_in_dim.12
  80.0 3.7 %all-to-all-start.2 = ((f32[16,1,592]{2,1,0:T(1,128)}), f32[16,1,592]{2,1,0:T(1,128)S(1)}, u32[]{:S(2)}, u32[]{:S(2)}) async-start(f32[16,1,592]{2,1,0:T(1,128)} %broadcast_in_dim.12), calls=%async_computation.2 | async-start | bytes 81920 | tf_op jit(solution)/shard_map/all_to_all | solution.py:67
  83.7 2.5 convert_reduce_fusion
  86.3 3.5 %convolution_convert_fusion.4 = bf16[4,256,96]{1,2,0:T(8,128)(2,1)} fusion(bf16[4,256,1280]{1,2,0:T(8,128)(2,1)} %all-gather.2.cloned.1.call-done, f32[1280]{0:T(1024)} %param.27, f32[4,256]{1,0:T(4,128)S(1)} %get-tuple-element.14, f32[4,256]{1,0:T(4,128)S(1)} %get-tuple-element.13, bf16[1280,96]{0,1:T(8,128)(2,1)} %param.30), kind=kOutput, calls=%fused_computation.33 | convolution fusion | flops 258310144 | bytes 3077120 | tf_op jit(solution)/shard_map/npv,vk->npk/dot_general | solution.py:138
  89.8 2.3 fusion.58
  92.1 3.0 convolution_convert_fusion.5
  95.1 0.3 convolution_convert_fusion.6
  95.5 1.2 convolution_convert_fusion.3
  96.6 0.6 copy-done.7
  97.2 7.2 %all-to-all-start = ((bf16[16,16,1280]{2,1,0:T(8,128)(2,1)}), bf16[16,16,1280]{2,1,0:T(8,128)(2,1)S(1)}, u32[]{:S(2)}, u32[]{:S(2)}) async-start(bf16[16,16,1280]{2,1,0:T(8,128)(2,1)} %bitcast.12), calls=%async_computation | async-start | bytes 1310720 | tf_op jit(solution)/shard_map/all_to_all | solution.py:167
  104.5 0.3 convert_reduce_fusion.3
  104.8 0.1 convolution_convert_fusion.10
  104.9 0.8 copy.92
  105.8 0.5 copy-done.8
  106.3 14.7 %all-to-all-done = bf16[16,16,1280]{2,1,0:T(8,128)(2,1)S(1)} async-done(((bf16[16,16,1280]{2,1,0:T(8,128)(2,1)}), bf16[16,16,1280]{2,1,0:T(8,128)(2,1)S(1)}, u32[]{:S(2)}, u32[]{:S(2)}) %all-to-all-start) | async-done | bytes 655392 | tf_op jit(solution)/shard_map/all_to_all | solution.py:167
  121.1 0.9 fusion.35
  122.1 0.9 multiply_convert_fusion.1
  122.9 0.1 reshape.222
  123.1 0.6 copy.91
  123.7 4.6 %all-to-all-start.3 = ((bf16[16,16,80]{2,1,0:T(8,128)(2,1)}), bf16[16,16,80]{2,1,0:T(8,128)(2,1)S(1)}, u32[]{:S(2)}, u32[]{:S(2)}) async-start(bf16[16,16,80]{2,1,0:T(8,128)(2,1)} %bitcast.95), calls=%async_computation.3 | async-start | bytes 131072 | tf_op jit(solution)/shard_map/all_to_all | solution.py:174
  128.3 7.8 %all-to-all-done.3 = bf16[16,16,80]{2,1,0:T(8,128)(2,1)S(1)} async-done(((bf16[16,16,80]{2,1,0:T(8,128)(2,1)}), bf16[16,16,80]{2,1,0:T(8,128)(2,1)S(1)}, u32[]{:S(2)}, u32[]{:S(2)}) %all-to-all-start.3) | async-done | bytes 40992 | tf_op jit(solution)/shard_map/all_to_all | solution.py:174
  136.1 0.2 reshape.229
  136.2 0.2 convolution_convert_fusion.2
  136.4 0.8 copy.66
  137.2 4.5 %all-to-all-start.4 = ((bf16[8,2,5120]{2,1,0:T(2,128)(2,1)}), bf16[8,2,5120]{2,1,0:T(2,128)(2,1)S(1)}, u32[]{:S(2)}, u32[]{:S(2)}) async-start(bf16[8,2,5120]{2,1,0:T(2,128)(2,1)} %copy.66), calls=%async_computation.4 | async-start | bytes 327680 | tf_op jit(solution)/shard_map/all_to_all | solution.py:183
  141.8 6.4 %all-to-all-done.4 = bf16[8,2,5120]{2,1,0:T(2,128)(2,1)S(1)} async-done(((bf16[8,2,5120]{2,1,0:T(2,128)(2,1)}), bf16[8,2,5120]{2,1,0:T(2,128)(2,1)S(1)}, u32[]{:S(2)}, u32[]{:S(2)}) %all-to-all-start.4) | async-done | bytes 163872 | tf_op jit(solution)/shard_map/all_to_all | solution.py:183
  148.2 0.3 fusion.2
  148.5 0.2 broadcast_in_dim.13
  148.8 1.2 broadcast_in_dim.14
  150.0 4.4 %all-to-all-start.5 = ((bf16[16,512,80]{1,2,0:T(8,128)(2,1)}), bf16[16,512,80]{1,2,0:T(8,128)(2,1)}, u32[]{:S(2)}, u32[]{:S(2)}) async-start(bf16[16,512,80]{1,2,0:T(8,128)(2,1)} %broadcast_in_dim.14), calls=%async_computation.5 | async-start | bytes 2621440 | tf_op jit(solution)/shard_map/all_to_all | solution.py:67
  154.5 26.2 %all-to-all-done.5 = bf16[16,512,80]{1,2,0:T(8,128)(2,1)} async-done(((bf16[16,512,80]{1,2,0:T(8,128)(2,1)}), bf16[16,512,80]{1,2,0:T(8,128)(2,1)}, u32[]{:S(2)}, u32[]{:S(2)}) %all-to-all-start.5) | async-done | bytes 1310752 | tf_op jit(solution)/shard_map/all_to_all | solution.py:67
  180.7 4.6 %reduce-precision_reduce_fusion.1 = bf16[512,512]{1,0:T(8,128)(2,1)} fusion(bf16[16,512,80]{1,2,0:T(8,128)(2,1)} %all-to-all-done.5, bf16[16,2,80,512]{3,2,1,0:T(8,128)(2,1)S(1)} %all-to-all-done.1), kind=kOutput, calls=%fused_computation.1 | convolution fusion | flops 679215104 | bytes 3145728 | tf_op jit(solution)/shard_map/brk,bkc->brc/dot_general | solution.py:71
  185.4 1.2 convert_element_type.175
  186.5 4.6 %reduce-precision_reduce_fusion = bf16[512,512]{1,0:T(8,128)(2,1)} fusion(bf16[16,512,80]{1,2,0:T(8,128)(2,1)} %all-to-all-done.5, bf16[16,2,80,512]{3,2,1,0:T(8,128)(2,1)S(1)} %all-to-all-done.1), kind=kOutput, calls=%fused_computation | convolution fusion | flops 679215104 | bytes 3145728 | tf_op jit(solution)/shard_map/brk,bkc->brc/dot_general | solution.py:71
  191.2 1.2 convert_element_type.182
  192.5 1.2 multiply_convert_fusion
  193.7 0.2 copy.77
  193.9 0.9 fusion.7
  194.8 1.0 fusion.10
  195.9 0.2 slice-done
  196.1 1.5 slice-done.1
  197.6 6.9 %fusion.1 = bf16[8192,512]{0,1:T(8,128)(2,1)} fusion(bf16[512,512]{1,0:T(8,128)(2,1)S(1)} %bitcast.106, bf16[512,8192]{1,0:T(8,128)(2,1)S(1)} %bitcast.99), kind=kOutput, calls=%fused_computation.5 | convolution fusion | flops 4299161600 | bytes 17301504 | tf_op jit(solution)/shard_map/dot_general | solution.py:208
  205.3 82.2 %reduce-scatter.5.cloned.1.call-done = bf16[512,512]{0,1:T(8,128)(2,1)} async-done(((bf16[8192,512]{0,1:T(8,128)(2,1)}), bf16[512,512]{0,1:T(8,128)(2,1)}) %reduce-scatter.5.cloned.1.call-update) | async-done | bytes 524304 | tf_op jit(solution)/shard_map/reduce_scatter | solution.py:207
  287.5 2.2 convert_add_fusion
  (77 shorter events, 0.9 us)
Async XLA Ops:
  6.5 88.9 %copy-start = (bf16[96,1280]{1,0:T(8,128)(2,1)S(1)}, bf16[96,1280]{1,0:T(8,128)(2,1)}, u32[]{:S(2)}) copy-start(bf16[96,1280]{1,0:T(8,128)(2,1)} %param.32) | copy-start | bytes 737284
  6.5 77.2 %all-gather.2.cloned.1.call-start = ((), (), s32[]{:S(2)}) async-start(), calls=%async_computation.8 | async-start | bytes 2785280 | tf_op jit(solution)/shard_map/all_gather | solution.py:131
  7.3 185.2 %reduce-scatter.3.cloned.1.call-start = ((), (), s32[]{:S(2)}) async-start(), calls=%async_computation.9 | async-start | bytes 8912896 | tf_op jit(solution)/shard_map/reduce_scatter | solution.py:123
  18.6 1.3 copy-start.4
  18.6 1.8 copy-start.5
  21.1 11.2 %copy-start.6 = (bf16[64,1280]{1,0:T(8,128)(2,1)S(1)}, bf16[64,1280]{1,0:T(8,128)(2,1)}, u32[]{:S(2)}) copy-start(bf16[64,1280]{1,0:T(8,128)(2,1)} %param.26) | copy-start | bytes 491524
  24.2 15.4 %copy-start.2 = (bf16[512,512]{1,0:T(8,128)(2,1)S(1)}, bf16[512,512]{1,0:T(8,128)(2,1)}, u32[]{:S(2)}) copy-start(bf16[512,512]{1,0:T(8,128)(2,1)} %param.19) | copy-start | bytes 1572868
  24.2 53.2 %all-to-all-start.1 = ((bf16[16,2,80,512]{3,2,1,0:T(8,128)(2,1)}), bf16[16,2,80,512]{3,2,1,0:T(8,128)(2,1)S(1)}, u32[]{:S(2)}, u32[]{:S(2)}) async-start(bf16[16,2,80,512]{3,2,1,0:T(8,128)(2,1)} %copy.63), calls=%async_computation.1 | async-start | bytes 5242880 | tf_op jit(solution)/shard_map/all_to_all | solution.py:113
  32.5 0.6 copy-start.17
  32.5 0.6 copy-start.19
  80.0 16.6 %all-to-all-start.2 = ((f32[16,1,592]{2,1,0:T(1,128)}), f32[16,1,592]{2,1,0:T(1,128)S(1)}, u32[]{:S(2)}, u32[]{:S(2)}) async-start(f32[16,1,592]{2,1,0:T(1,128)} %broadcast_in_dim.12), calls=%async_computation.2 | async-start | bytes 81920 | tf_op jit(solution)/shard_map/all_to_all | solution.py:67
  83.6 6.1 %copy-start.11 = (bf16[64,96]{0,1:T(8,128)(2,1)S(1)}, bf16[64,96]{0,1:T(8,128)(2,1)}, u32[]{:S(2)}) copy-start(bf16[64,96]{0,1:T(8,128)(2,1)} %copy.62) | copy-start | bytes 36868
  83.6 6.1 %copy-start.18 = (f32[64]{0:T(128)S(1)}, f32[64]{0:T(128)}, u32[]{:S(2)}) copy-start(f32[64]{0:T(128)} %copy-done.17) | copy-start | bytes 772
  83.7 6.1 %copy-start.20 = (f32[64]{0:T(128)S(1)}, f32[64]{0:T(128)}, u32[]{:S(2)}) copy-start(f32[64]{0:T(128)} %copy-done.19) | copy-start | bytes 772
  83.7 6.1 %copy-start.21 = (bf16[1280,96]{0,1:T(8,128)(2,1)S(1)}, bf16[1280,96]{0,1:T(8,128)(2,1)}, u32[]{:S(2)}) copy-start(bf16[1280,96]{0,1:T(8,128)(2,1)} %param.29) | copy-start | bytes 737284
  83.7 6.1 %copy-start.22 = (f32[1280]{0:T(1024)S(1)}, f32[1280]{0:T(1024)}, u32[]{:S(2)}) copy-start(f32[1280]{0:T(1024)} %param.28) | copy-start | bytes 15364
  86.2 5.9 %copy-start.23 = (f32[1280]{0:T(1024)S(1)}, f32[1280]{0:T(1024)}, u32[]{:S(2)}) copy-start(f32[1280]{0:T(1024)} %param.27) | copy-start | bytes 15364
  89.7 5.4 %copy-start.10 = (bf16[64,96]{0,1:T(8,128)(2,1)S(1)}, bf16[64,96]{0,1:T(8,128)(2,1)}, u32[]{:S(2)}) copy-start(bf16[64,96]{0,1:T(8,128)(2,1)} %copy.60) | copy-start | bytes 36868
  92.1 3.0 %copy-start.24 = (f32[4,1,64,320]{3,2,0,1:T(8,128)S(1)}, f32[4,1,64,320]{3,2,0,1:T(8,128)}, u32[]{:S(2)}) copy-start(f32[4,1,64,320]{3,2,0,1:T(8,128)} %get-tuple-element.20) | copy-start | bytes 983044
  92.1 12.4 %copy-start.12 = (s32[8,8]{1,0:T(8,128)S(1)}, s32[8,8]{1,0:T(8,128)}, u32[]{:S(2)}) copy-start(s32[8,8]{1,0:T(8,128)} %get-tuple-element.11) | copy-start | bytes 772
  92.1 12.7 %copy-start.13 = (s32[8,8]{1,0:T(8,128)S(1)}, s32[8,8]{1,0:T(8,128)}, u32[]{:S(2)}) copy-start(s32[8,8]{1,0:T(8,128)} %get-tuple-element.12) | copy-start | bytes 772
  92.1 12.7 %copy-start.16 = (bf16[8,8]{1,0:T(8,128)(2,1)S(1)}, bf16[8,8]{1,0:T(8,128)(2,1)}, u32[]{:S(2)}) copy-start(bf16[8,8]{1,0:T(8,128)(2,1)} %compare_convert_fusion) | copy-start | bytes 388
  96.6 0.6 copy-start.7
  96.6 57.8 %copy-start.14 = (s32[1,512]{1,0:T(1,128)S(1)}, s32[1,512]{1,0:T(1,128)}, u32[]{:S(2)}) copy-start(s32[1,512]{1,0:T(1,128)} %param.23) | copy-start | bytes 6148
  97.2 23.8 %all-to-all-start = ((bf16[16,16,1280]{2,1,0:T(8,128)(2,1)}), bf16[16,16,1280]{2,1,0:T(8,128)(2,1)S(1)}, u32[]{:S(2)}, u32[]{:S(2)}) async-start(bf16[16,16,1280]{2,1,0:T(8,128)(2,1)} %bitcast.12), calls=%async_computation | async-start | bytes 1310720 | tf_op jit(solution)/shard_map/all_to_all | solution.py:167
  105.7 0.6 copy-start.8
  121.1 33.3 %copy-start.9 = (f32[16,1,592]{2,0,1:T(8,128)S(1)}, f32[16,1,592]{2,0,1:T(8,128)}, u32[]{:S(2)}) copy-start(f32[16,1,592]{2,0,1:T(8,128)} %copy-done.8) | copy-start | bytes 113668
  123.7 12.3 %all-to-all-start.3 = ((bf16[16,16,80]{2,1,0:T(8,128)(2,1)}), bf16[16,16,80]{2,1,0:T(8,128)(2,1)S(1)}, u32[]{:S(2)}, u32[]{:S(2)}) async-start(bf16[16,16,80]{2,1,0:T(8,128)(2,1)} %bitcast.95), calls=%async_computation.3 | async-start | bytes 131072 | tf_op jit(solution)/shard_map/all_to_all | solution.py:174
  137.2 11.0 %all-to-all-start.4 = ((bf16[8,2,5120]{2,1,0:T(2,128)(2,1)}), bf16[8,2,5120]{2,1,0:T(2,128)(2,1)S(1)}, u32[]{:S(2)}, u32[]{:S(2)}) async-start(bf16[8,2,5120]{2,1,0:T(2,128)(2,1)} %copy.66), calls=%async_computation.4 | async-start | bytes 327680 | tf_op jit(solution)/shard_map/all_to_all | solution.py:183
  150.0 30.8 %all-to-all-start.5 = ((bf16[16,512,80]{1,2,0:T(8,128)(2,1)}), bf16[16,512,80]{1,2,0:T(8,128)(2,1)}, u32[]{:S(2)}, u32[]{:S(2)}) async-start(bf16[16,512,80]{1,2,0:T(8,128)(2,1)} %broadcast_in_dim.14), calls=%async_computation.5 | async-start | bytes 2621440 | tf_op jit(solution)/shard_map/all_to_all | solution.py:67
  154.4 133.1 %reduce-scatter.5.cloned.1.call-start = ((), (), s32[]{:S(2)}) async-start(), calls=%async_computation.10 | async-start | bytes 8912896 | tf_op jit(solution)/shard_map/reduce_scatter | solution.py:207
  193.9 2.2 slice-start
  194.8 2.8 slice-start.1
  204.5 85.2 %copy-start.1 = (bf16[96,1280]{1,0:T(8,128)(2,1)S(1)}, bf16[96,1280]{1,0:T(8,128)(2,1)}, u32[]{:S(2)}) copy-start(bf16[96,1280]{1,0:T(8,128)(2,1)} %param.32) | copy-start | bytes 737284
  204.5 0.7 copy-start.15
  204.5 83.0 %copy-start.3 = (bf16[512,512]{1,0:T(8,128)(2,1)S(1)}, bf16[512,512]{1,0:T(8,128)(2,1)}, u32[]{:S(2)}) copy-start(bf16[512,512]{1,0:T(8,128)(2,1)} %param.19) | copy-start | bytes 1572868
Sparse Core Ops, SparseCore 0:
  9.5 68.3 all-gather.1
  81.3 101.6 reduce-scatter.2
  204.7 82.7 reduce-scatter.4

commit v4 on v3

--- a/solution.py
+++ b/solution.py
@@ -109,13 +109,13 @@
     slot_count = wanted_images.shape[1]
     cross_heads = head_cols // HEAD
     contract_first = (((0,), (1,)), ((), ()))
-    kv_weights = jnp.stack([cross_key, cross_value], 0).reshape(2, feat_vis, parts, head_cols)
+    kv_weights = jnp.stack([cross_key, cross_value], 1).reshape(feat_vis, 2, parts, head_cols)
     kv_weights = lax.all_to_all(
         jnp.transpose(kv_weights, (2, 0, 1, 3)), "fsdp", split_axis=0, concat_axis=0, tiled=True
-    )
+    ).reshape(parts, feat_vis, 2 * head_cols)
     text_f = text_states.astype(jnp.float32)
     gained = (text_f * text_gain).astype(jnp.bfloat16)
-    after_weights = kv_weights[0, 0, 0, 0].astype(jnp.float32) * 0.0
+    after_weights = kv_weights[0, 0, 0].astype(jnp.float32) * 0.0
     stats = jnp.concatenate([jnp.sum(text_f * text_f, -1), final_gain], 0) + after_weights
     stats = gather_blocks(stats, "fsdp", parts)
     squares = jnp.sum(stats[:, :token_count], 0)
@@ -185,10 +185,10 @@
         slot_count * latent_count, feat_vis
     )
     slot_blocks = gather_blocks(slot_latents, "fsdp", parts)
-    slot_keys = block_dot(slot_blocks, kv_weights[:, 0]).astype(jnp.bfloat16)
-    slot_values = block_dot(slot_blocks, kv_weights[:, 1]).astype(jnp.bfloat16)
-    slot_keys = slot_keys.reshape(slot_count, latent_count, cross_heads, HEAD)
-    slot_values = slot_values.reshape(slot_count, latent_count, cross_heads, HEAD)
+    slot_kv = block_dot(slot_blocks, kv_weights).astype(jnp.bfloat16)
+    slot_kv = slot_kv.reshape(slot_count, latent_count, 2, cross_heads, HEAD)
+    slot_keys = slot_kv[:, :, 0]
+    slot_values = slot_kv[:, :, 1]
     token_scale = lax.rsqrt(squares / D + eps_rms)
     query_cols = (query_cols.astype(jnp.float32) * token_scale[None, :]).astype(jnp.bfloat16)
     query_heads = query_cols.reshape(cross_heads, HEAD, token_count)

time: 298 us -> 311 us (1.044)
  local copies, waits for them, and re-layouts: 19.6 us -> 25.7 us
  other arithmetic: 12.7 us -> 18.5 us
    transpose x1, other arithmetic: 0.24 us -> 6.84 us  [local(): jnp.transpose(kv_weights, (2, 0, 1, 3))]
    another operation x0 -> x2, local copies, waits for them, and re-layouts: none -> 5.04 us  [local(): jnp.stack([cross_key, cross_value], 1)]
    reshape x0 -> x1, local copies, waits for them, and re-layouts: none -> 3.48 us  [local(): kv_weights = lax.all_to_all(jnp.transpose(kv_weights, (2, 0, 1, 3)), 'fsd...]
    dot_general x2 -> x1, matrix products: 9.26 us -> 7.33 us  [block_dot(): jnp.einsum('brk,bkc->brc', rows, cols, preferred_element_type=jnp.float32)]
    unnamed x57 -> x66, local copies, waits for them, and re-layouts: 6.53 us -> 6.65 us
  transfers between devices with their start and end apart: 9 -> 9, of which waited for: 6 -> 6; matrix products, arithmetic and copies ran while one was open for 20% -> 22% of each run, Pallas kernels for 0% -> 0%
where the time goes in v4:
time: 311 us; the launch traced here: 310 us
  waiting for transfers between devices  175 us (56%)
  matrix products  41.3 us (13%)
  starting transfers between devices  33.7 us (11%)
  local copies, waits for them, and re-layouts  25.7 us (8%)
  other arithmetic  18.5 us (6%)
  between operations  15 us (5%)
    reduce_scatter x1, waiting for transfers between devices, local(): lax.psum_scatter(lax.dot_general(cross_out, attended, (((0,), (0,)), ((),...  82.5 us
    all_to_all x1, waiting for transfers between devices, local(): lax.all_to_all(jnp.transpose(kv_weights, (2, 0, 1, 3)), 'fsdp', split_axi...  36.5 us
    all_to_all x2, waiting for transfers between devices, gather_blocks(): lax.all_to_all(spread, axis_name, split_axis=0, concat_axis=0, tiled=True)  26.3 us
    all_to_all x1, waiting for transfers between devices, local(): lax.all_to_all(head_part.reshape(parts, row_part, vis_width), 'fsdp', spl...  14.9 us
    dot_general x1, matrix products, local(): lax.dot_general(cross_query, gained, contract_first, preferred_element_ty...  11.3 us
    all_to_all x1, starting transfers between devices, local(): lax.all_to_all(jnp.transpose(kv_weights, (2, 0, 1, 3)), 'fsdp', split_axi...  8.12 us
    all_to_all x2, starting transfers between devices, gather_blocks(): lax.all_to_all(spread, axis_name, split_axis=0, concat_axis=0, tiled=True)  8.06 us
    all_to_all x1, waiting for transfers between devices, local(): lax.all_to_all(jnp.transpose(resampled_rows.reshape(row_part, parts, feat...  7.99 us
  transfers between devices with their start and end apart: 9, of which 6 were waited for; matrix products, arithmetic and copies ran while one was open for 22% of the time, Pallas kernels for 0%

profile of v4, /device:TPU:0, one launch (start us, length us, event | category | flops | bytes accessed | tf_op | source)
XLA Modules:
  0.0 309.7 jit_solution(2584838720880811806)
XLA Ops:
  6.5 0.7 all-gather.2.cloned.1.call-update
  7.3 11.3 %fusion = bf16[8192,512]{0,1:T(8,128)(2,1)} fusion(bf16[512,8192]{1,0:T(8,128)(2,1)} %param.34, bf16[512,512]{1,0:T(8,128)(2,1)} %param.19, f32[512]{0:T(512)} %param.20), kind=kOutput, calls=%fused_computation.3 | convolution fusion | flops 4299948032 | bytes 17303552 | tf_op jit(solution)/shard_map/dot_general | solution.py:124
  18.7 1.3 copy-done.6
  20.0 0.5 copy.80
  20.4 2.5 copy.63
  23.0 0.5 copy.81
  23.4 2.5 copy.64
  26.0 6.8 %maximum_bitcast_fusion = bf16[16,80,2,512]{3,2,1,0:T(2,128)(2,1)} fusion(bf16[80,1,16,512]{3,1,0,2:T(2,128)(2,1)S(1)} %copy.64, bf16[80,1,16,512]{3,1,0,2:T(2,128)(2,1)S(1)} %copy.63), kind=kLoop, calls=%fused_computation.18 | loop fusion | flops 5242880 | bytes 5242880 | tf_op jit(solution)/shard_map/transpose | solution.py:114
  32.8 8.1 %all-to-all-start.1 = ((bf16[16,80,2,512]{3,2,1,0:T(2,128)(2,1)}), bf16[16,80,2,512]{3,2,1,0:T(2,128)(2,1)S(1)}, u32[]{:S(2)}, u32[]{:S(2)}) async-start(bf16[16,80,2,512]{3,2,1,0:T(2,128)(2,1)} %maximum_bitcast_fusion), calls=%async_computation.1 | async-start | bytes 5242880 | tf_op jit(solution)/shard_map/all_to_all | solution.py:113
  41.0 0.1 convert_reduce_fusion.2
  41.1 0.6 copy-done.21
  41.7 1.9 convolution_convert_fusion.8
  43.6 1.4 copy.62
  45.0 1.8 convolution_convert_fusion.9
  46.8 1.4 copy.60
  48.3 0.7 fusion.14
  49.0 1.3 compare_convert_fusion
  50.4 1.3 add_select_fusion.1
  51.6 36.5 %all-to-all-done.1 = bf16[16,80,2,512]{3,2,1,0:T(2,128)(2,1)S(1)} async-done(((bf16[16,80,2,512]{3,2,1,0:T(2,128)(2,1)}), bf16[16,80,2,512]{3,2,1,0:T(2,128)(2,1)S(1)}, u32[]{:S(2)}, u32[]{:S(2)}) %all-to-all-start.1) | async-done | bytes 2621472 | tf_op jit(solution)/shard_map/all_to_all | solution.py:113
  88.1 3.5 %reshape.222 = bf16[16,80,1024]{2,1,0:T(8,128)(2,1)} reshape(bf16[16,80,2,512]{3,2,1,0:T(2,128)(2,1)S(1)} %all-to-all-done.1) | data formatting | bytes 5242880 | tf_op jit(solution)/shard_map/reshape | solution.py:115
  91.6 1.3 slice.20
  93.6 0.6 broadcast_in_dim.12
  94.2 3.7 %all-to-all-start.2 = ((f32[16,1,592]{2,1,0:T(1,128)}), f32[16,1,592]{2,1,0:T(1,128)S(1)}, u32[]{:S(2)}, u32[]{:S(2)}) async-start(f32[16,1,592]{2,1,0:T(1,128)} %broadcast_in_dim.12), calls=%async_computation.2 | async-start | bytes 81920 | tf_op jit(solution)/shard_map/all_to_all | solution.py:67
  97.9 2.4 convert_reduce_fusion
  100.4 3.7 %convolution_convert_fusion.4 = bf16[4,256,96]{1,2,0:T(8,128)(2,1)} fusion(bf16[4,256,1280]{1,2,0:T(8,128)(2,1)} %all-gather.2.cloned.1.call-done, f32[1280]{0:T(1024)S(1)} %copy-done.27, f32[4,256]{1,0:T(4,128)S(1)} %get-tuple-element.16, f32[4,256]{1,0:T(4,128)S(1)} %get-tuple-element.15, bf16[1280,96]{0,1:T(8,128)(2,1)S(1)} %copy-done.25), kind=kOutput, calls=%fused_computation.30 | convolution fusion | flops 258310144 | bytes 3077120 | tf_op jit(solution)/shard_map/npv,vk->npk/dot_general | solution.py:138
  104.1 2.3 fusion.58
  106.5 2.0 convolution_convert_fusion.5
  108.6 0.3 convolution_convert_fusion.6
  108.9 1.2 convolution_convert_fusion.3
  110.1 0.6 copy-done.9
  110.7 7.3 %all-to-all-start = ((bf16[16,16,1280]{2,1,0:T(8,128)(2,1)}), bf16[16,16,1280]{2,1,0:T(8,128)(2,1)S(1)}, u32[]{:S(2)}, u32[]{:S(2)}) async-start(bf16[16,16,1280]{2,1,0:T(8,128)(2,1)} %bitcast.12), calls=%async_computation | async-start | bytes 1310720 | tf_op jit(solution)/shard_map/all_to_all | solution.py:167
  118.0 0.3 convert_reduce_fusion.3
  118.3 0.1 convolution_convert_fusion.10
  118.5 0.8 copy.91
  119.3 0.5 copy-done.10
  119.9 14.9 %all-to-all-done = bf16[16,16,1280]{2,1,0:T(8,128)(2,1)S(1)} async-done(((bf16[16,16,1280]{2,1,0:T(8,128)(2,1)}), bf16[16,16,1280]{2,1,0:T(8,128)(2,1)S(1)}, u32[]{:S(2)}, u32[]{:S(2)}) %all-to-all-start) | async-done | bytes 655392 | tf_op jit(solution)/shard_map/all_to_all | solution.py:167
  134.9 0.9 fusion.34
  135.8 0.9 multiply_convert_fusion.1
  136.7 0.1 reshape.223
  136.8 0.6 copy.90
  137.5 4.0 %all-to-all-start.3 = ((bf16[16,16,80]{2,1,0:T(8,128)(2,1)}), bf16[16,16,80]{2,1,0:T(8,128)(2,1)S(1)}, u32[]{:S(2)}, u32[]{:S(2)}) async-start(bf16[16,16,80]{2,1,0:T(8,128)(2,1)} %bitcast.92), calls=%async_computation.3 | async-start | bytes 131072 | tf_op jit(solution)/shard_map/all_to_all | solution.py:174
  141.4 8.0 %all-to-all-done.3 = bf16[16,16,80]{2,1,0:T(8,128)(2,1)S(1)} async-done(((bf16[16,16,80]{2,1,0:T(8,128)(2,1)}), bf16[16,16,80]{2,1,0:T(8,128)(2,1)S(1)}, u32[]{:S(2)}, u32[]{:S(2)}) %all-to-all-start.3) | async-done | bytes 40992 | tf_op jit(solution)/shard_map/all_to_all | solution.py:174
  149.4 0.2 reshape.230
  149.6 0.2 convolution_convert_fusion.2
  149.8 0.8 copy.67
  150.6 6.2 %all-to-all-start.4 = ((bf16[8,2,5120]{2,1,0:T(2,128)(2,1)}), bf16[8,2,5120]{2,1,0:T(2,128)(2,1)S(1)}, u32[]{:S(2)}, u32[]{:S(2)}) async-start(bf16[8,2,5120]{2,1,0:T(2,128)(2,1)} %copy.67), calls=%async_computation.4 | async-start | bytes 327680 | tf_op jit(solution)/shard_map/all_to_all | solution.py:183
  156.9 6.4 %all-to-all-done.4 = bf16[8,2,5120]{2,1,0:T(2,128)(2,1)S(1)} async-done(((bf16[8,2,5120]{2,1,0:T(2,128)(2,1)}), bf16[8,2,5120]{2,1,0:T(2,128)(2,1)S(1)}, u32[]{:S(2)}, u32[]{:S(2)}) %all-to-all-start.4) | async-done | bytes 163872 | tf_op jit(solution)/shard_map/all_to_all | solution.py:183
  163.3 0.3 fusion.2
  163.6 0.2 broadcast_in_dim.13
  163.9 1.2 broadcast_in_dim.14
  165.1 4.4 %all-to-all-start.5 = ((bf16[16,512,80]{1,2,0:T(8,128)(2,1)}), bf16[16,512,80]{1,2,0:T(8,128)(2,1)}, u32[]{:S(2)}, u32[]{:S(2)}) async-start(bf16[16,512,80]{1,2,0:T(8,128)(2,1)} %broadcast_in_dim.14), calls=%async_computation.5 | async-start | bytes 2621440 | tf_op jit(solution)/shard_map/all_to_all | solution.py:67
  169.6 26.3 %all-to-all-done.5 = bf16[16,512,80]{1,2,0:T(8,128)(2,1)} async-done(((bf16[16,512,80]{1,2,0:T(8,128)(2,1)}), bf16[16,512,80]{1,2,0:T(8,128)(2,1)}, u32[]{:S(2)}, u32[]{:S(2)}) %all-to-all-start.5) | async-done | bytes 1310752 | tf_op jit(solution)/shard_map/all_to_all | solution.py:67
  195.9 7.3 %reduce-precision_reduce_fusion = bf16[512,1024]{1,0:T(8,128)(2,1)} fusion(bf16[16,512,80]{1,2,0:T(8,128)(2,1)} %all-to-all-done.5, bf16[16,80,1024]{2,1,0:T(8,128)(2,1)S(1)} %copy-done.2), kind=kOutput, calls=%fused_computation | convolution fusion | flops 1358430208 | bytes 4980736 | tf_op jit(solution)/shard_map/brk,bkc->brc/dot_general | solution.py:71
  203.2 1.8 convert_element_type.168
  205.0 0.5 fusion.57
  205.7 1.2 multiply_convert_fusion
  206.9 0.2 copy.76
  207.1 0.9 fusion.7
  208.0 1.0 fusion.10
  209.1 0.2 slice-done
  209.3 1.5 slice-done.1
  210.8 6.9 %fusion.1 = bf16[8192,512]{0,1:T(8,128)(2,1)} fusion(bf16[512,512]{1,0:T(8,128)(2,1)S(1)} %bitcast.103, bf16[512,8192]{1,0:T(8,128)(2,1)S(1)} %bitcast.96), kind=kOutput, calls=%fused_computation.4 | convolution fusion | flops 4299161600 | bytes 17301504 | tf_op jit(solution)/shard_map/dot_general | solution.py:208
  218.5 82.5 %reduce-scatter.5.cloned.1.call-done = bf16[512,512]{0,1:T(8,128)(2,1)} async-done(((bf16[8192,512]{0,1:T(8,128)(2,1)}), bf16[512,512]{0,1:T(8,128)(2,1)}) %reduce-scatter.5.cloned.1.call-update) | async-done | bytes 524304 | tf_op jit(solution)/shard_map/reduce_scatter | solution.py:207
  300.9 2.2 convert_add_fusion
  (86 shorter events, 0.9 us)
Async XLA Ops:
  6.5 102.4 %copy-start = (bf16[96,1280]{1,0:T(8,128)(2,1)S(1)}, bf16[96,1280]{1,0:T(8,128)(2,1)}, u32[]{:S(2)}) copy-start(bf16[96,1280]{1,0:T(8,128)(2,1)} %param.32) | copy-start | bytes 737284
  6.5 91.4 %all-gather.2.cloned.1.call-start = ((), (), s32[]{:S(2)}) async-start(), calls=%async_computation.8 | async-start | bytes 2785280 | tf_op jit(solution)/shard_map/all_gather | solution.py:131
  7.3 198.4 %reduce-scatter.3.cloned.1.call-start = ((), (), s32[]{:S(2)}) async-start(), calls=%async_computation.9 | async-start | bytes 8912896 | tf_op jit(solution)/shard_map/reduce_scatter | solution.py:123
  18.7 1.3 copy-start.6
  18.7 4.3 %copy-start.7 = (bf16[80,8192]{1,0:T(8,128)(2,1)S(1)}, bf16[80,8192]{1,0:T(8,128)(2,1)}, u32[]{:S(2)}) copy-start(bf16[80,8192]{1,0:T(8,128)(2,1)} %param.36) | copy-start | bytes 3932164
  32.8 8.1 %copy-start.8 = (bf16[64,1280]{1,0:T(8,128)(2,1)S(1)}, bf16[64,1280]{1,0:T(8,128)(2,1)}, u32[]{:S(2)}) copy-start(bf16[64,1280]{1,0:T(8,128)(2,1)} %param.26) | copy-start | bytes 491524
  32.8 15.4 %copy-start.4 = (bf16[512,512]{1,0:T(8,128)(2,1)S(1)}, bf16[512,512]{1,0:T(8,128)(2,1)}, u32[]{:S(2)}) copy-start(bf16[512,512]{1,0:T(8,128)(2,1)} %param.19) | copy-start | bytes 1572868
  32.8 55.3 %all-to-all-start.1 = ((bf16[16,80,2,512]{3,2,1,0:T(2,128)(2,1)}), bf16[16,80,2,512]{3,2,1,0:T(2,128)(2,1)S(1)}, u32[]{:S(2)}, u32[]{:S(2)}) async-start(bf16[16,80,2,512]{3,2,1,0:T(2,128)(2,1)} %maximum_bitcast_fusion), calls=%async_computation.1 | async-start | bytes 5242880 | tf_op jit(solution)/shard_map/all_to_all | solution.py:113
  41.1 0.6 copy-start.21
  41.1 0.6 copy-start.23
  49.0 44.5 %copy-start.15 = (f32[512]{0:T(512)S(1)}, f32[512]{0:T(512)}, u32[]{:S(2)}) copy-start(f32[512]{0:T(512)} %fusion.14) | copy-start | bytes 6148
  49.0 44.5 %copy-start.20 = (f32[80]{0:T(128)S(1)}, f32[80]{0:T(128)}, u32[]{:S(2)}) copy-start(f32[80]{0:T(128)} %param.33) | copy-start | bytes 964
  49.0 51.4 %copy-start.25 = (bf16[1280,96]{0,1:T(8,128)(2,1)S(1)}, bf16[1280,96]{0,1:T(8,128)(2,1)}, u32[]{:S(2)}) copy-start(bf16[1280,96]{0,1:T(8,128)(2,1)} %param.30) | copy-start | bytes 737284
  49.0 51.4 %copy-start.27 = (f32[1280]{0:T(1024)S(1)}, f32[1280]{0:T(1024)}, u32[]{:S(2)}) copy-start(f32[1280]{0:T(1024)} %param.27) | copy-start | bytes 15364
  94.2 15.9 %all-to-all-start.2 = ((f32[16,1,592]{2,1,0:T(1,128)}), f32[16,1,592]{2,1,0:T(1,128)S(1)}, u32[]{:S(2)}, u32[]{:S(2)}) async-start(f32[16,1,592]{2,1,0:T(1,128)} %broadcast_in_dim.12), calls=%async_computation.2 | async-start | bytes 81920 | tf_op jit(solution)/shard_map/all_to_all | solution.py:67
  97.9 6.2 %copy-start.13 = (bf16[64,96]{0,1:T(8,128)(2,1)S(1)}, bf16[64,96]{0,1:T(8,128)(2,1)}, u32[]{:S(2)}) copy-start(bf16[64,96]{0,1:T(8,128)(2,1)} %copy.62) | copy-start | bytes 36868
  97.9 6.2 %copy-start.22 = (f32[64]{0:T(128)S(1)}, f32[64]{0:T(128)}, u32[]{:S(2)}) copy-start(f32[64]{0:T(128)} %copy-done.21) | copy-start | bytes 772
  97.9 6.2 %copy-start.24 = (f32[64]{0:T(128)S(1)}, f32[64]{0:T(128)}, u32[]{:S(2)}) copy-start(f32[64]{0:T(128)} %copy-done.23) | copy-start | bytes 772
  97.9 6.2 %copy-start.26 = (f32[1280]{0:T(1024)S(1)}, f32[1280]{0:T(1024)}, u32[]{:S(2)}) copy-start(f32[1280]{0:T(1024)} %param.28) | copy-start | bytes 15364
  100.4 6.1 %copy-start.3 = (bf16[4,256,1280]{1,2,0:T(8,128)(2,1)S(1)}, bf16[4,256,1280]{1,2,0:T(8,128)(2,1)}, u32[]{:S(2)}) copy-start(bf16[4,256,1280]{1,2,0:T(8,128)(2,1)} %all-gather.2.cloned.1.call-done) | copy-start | bytes 7864324
  104.1 4.5 %copy-start.12 = (bf16[64,96]{0,1:T(8,128)(2,1)S(1)}, bf16[64,96]{0,1:T(8,128)(2,1)}, u32[]{:S(2)}) copy-start(bf16[64,96]{0,1:T(8,128)(2,1)} %copy.60) | copy-start | bytes 36868
  106.5 2.1 copy-start.28
  106.5 11.5 %copy-start.14 = (s32[8,8]{1,0:T(8,128)S(1)}, s32[8,8]{1,0:T(8,128)}, u32[]{:S(2)}) copy-start(s32[8,8]{1,0:T(8,128)} %get-tuple-element.13) | copy-start | bytes 772
  106.5 11.8 %copy-start.16 = (s32[8,8]{1,0:T(8,128)S(1)}, s32[8,8]{1,0:T(8,128)}, u32[]{:S(2)}) copy-start(s32[8,8]{1,0:T(8,128)} %get-tuple-element.14) | copy-start | bytes 772
  106.5 11.8 %copy-start.19 = (bf16[8,8]{1,0:T(8,128)(2,1)S(1)}, bf16[8,8]{1,0:T(8,128)(2,1)}, u32[]{:S(2)}) copy-start(bf16[8,8]{1,0:T(8,128)(2,1)} %compare_convert_fusion) | copy-start | bytes 388
  110.1 0.6 copy-start.9
  110.1 59.4 %copy-start.17 = (s32[1,512]{1,0:T(1,128)S(1)}, s32[1,512]{1,0:T(1,128)}, u32[]{:S(2)}) copy-start(s32[1,512]{1,0:T(1,128)} %param.23) | copy-start | bytes 6148
  110.1 85.8 %copy-start.2 = (bf16[16,80,1024]{2,1,0:T(8,128)(2,1)S(1)}, bf16[16,80,1024]{2,1,0:T(8,128)(2,1)}, u32[]{:S(2)}) copy-start(bf16[16,80,1024]{2,1,0:T(8,128)(2,1)} %reshape.222) | copy-start | bytes 7864324
  110.7 24.1 %all-to-all-start = ((bf16[16,16,1280]{2,1,0:T(8,128)(2,1)}), bf16[16,16,1280]{2,1,0:T(8,128)(2,1)S(1)}, u32[]{:S(2)}, u32[]{:S(2)}) async-start(bf16[16,16,1280]{2,1,0:T(8,128)(2,1)} %bitcast.12), calls=%async_computation | async-start | bytes 1310720 | tf_op jit(solution)/shard_map/all_to_all | solution.py:167
  119.2 0.6 copy-start.10
  134.9 34.7 %copy-start.11 = (f32[16,1,592]{2,0,1:T(8,128)S(1)}, f32[16,1,592]{2,0,1:T(8,128)}, u32[]{:S(2)}) copy-start(f32[16,1,592]{2,0,1:T(8,128)} %copy-done.10) | copy-start | bytes 113668
  137.5 12.0 %all-to-all-start.3 = ((bf16[16,16,80]{2,1,0:T(8,128)(2,1)}), bf16[16,16,80]{2,1,0:T(8,128)(2,1)S(1)}, u32[]{:S(2)}, u32[]{:S(2)}) async-start(bf16[16,16,80]{2,1,0:T(8,128)(2,1)} %bitcast.92), calls=%async_computation.3 | async-start | bytes 131072 | tf_op jit(solution)/shard_map/all_to_all | solution.py:174
  150.6 12.7 %all-to-all-start.4 = ((bf16[8,2,5120]{2,1,0:T(2,128)(2,1)}), bf16[8,2,5120]{2,1,0:T(2,128)(2,1)S(1)}, u32[]{:S(2)}, u32[]{:S(2)}) async-start(bf16[8,2,5120]{2,1,0:T(2,128)(2,1)} %copy.67), calls=%async_computation.4 | async-start | bytes 327680 | tf_op jit(solution)/shard_map/all_to_all | solution.py:183
  165.1 30.8 %all-to-all-start.5 = ((bf16[16,512,80]{1,2,0:T(8,128)(2,1)}), bf16[16,512,80]{1,2,0:T(8,128)(2,1)}, u32[]{:S(2)}, u32[]{:S(2)}) async-start(bf16[16,512,80]{1,2,0:T(8,128)(2,1)} %broadcast_in_dim.14), calls=%async_computation.5 | async-start | bytes 2621440 | tf_op jit(solution)/shard_map/all_to_all | solution.py:67
  169.5 131.5 %reduce-scatter.5.cloned.1.call-start = ((), (), s32[]{:S(2)}) async-start(), calls=%async_computation.10 | async-start | bytes 8912896 | tf_op jit(solution)/shard_map/reduce_scatter | solution.py:207
  207.1 2.2 slice-start
  208.0 2.8 slice-start.1
  217.7 85.5 %copy-start.1 = (bf16[96,1280]{1,0:T(8,128)(2,1)S(1)}, bf16[96,1280]{1,0:T(8,128)(2,1)}, u32[]{:S(2)}) copy-start(bf16[96,1280]{1,0:T(8,128)(2,1)} %param.32) | copy-start | bytes 737284
  217.7 0.7 copy-start.18
  217.7 83.2 %copy-start.5 = (bf16[512,512]{1,0:T(8,128)(2,1)S(1)}, bf16[512,512]{1,0:T(8,128)(2,1)}, u32[]{:S(2)}) copy-start(bf16[512,512]{1,0:T(8,128)(2,1)} %param.19) | copy-start | bytes 1572868
Sparse Core Ops, SparseCore 0:
  9.5 78.1 all-gather.1
  91.1 103.7 reduce-scatter.2
  217.8 83.0 reduce-scatter.4

commit v5 on v3

--- a/solution.py
+++ b/solution.py
@@ -185,10 +185,11 @@
         slot_count * latent_count, feat_vis
     )
     slot_blocks = gather_blocks(slot_latents, "fsdp", parts)
-    slot_keys = block_dot(slot_blocks, kv_weights[:, 0]).astype(jnp.bfloat16)
-    slot_values = block_dot(slot_blocks, kv_weights[:, 1]).astype(jnp.bfloat16)
-    slot_keys = slot_keys.reshape(slot_count, latent_count, cross_heads, HEAD)
-    slot_values = slot_values.reshape(slot_count, latent_count, cross_heads, HEAD)
+    slot_kv = jnp.einsum("brk,bskc->brsc", slot_blocks, kv_weights, preferred_element_type=jnp.float32)
+    slot_kv = jnp.sum(lax.reduce_precision(slot_kv, exponent_bits=8, mantissa_bits=7), 0)
+    slot_kv = slot_kv.astype(jnp.bfloat16).reshape(slot_count, latent_count, 2, cross_heads, HEAD)
+    slot_keys = slot_kv[:, :, 0]
+    slot_values = slot_kv[:, :, 1]
     token_scale = lax.rsqrt(squares / D + eps_rms)
     query_cols = (query_cols.astype(jnp.float32) * token_scale[None, :]).astype(jnp.bfloat16)
     query_heads = query_cols.reshape(cross_heads, HEAD, token_count)

time: 298 us -> 296 us (level)
    transpose x1 -> x0, local copies, waits for them, and re-layouts: 3.07 us -> none  [local(): jnp.transpose(kv_weights, (2, 0, 1, 3))]
    dot_general x2 -> x1, matrix products: 9.26 us -> 7.41 us  [local(): jnp.einsum('brk,bskc->brsc', slot_blocks, kv_weights, preferred_element_t...]
    unnamed x57 -> x58, local copies, waits for them, and re-layouts: 6.53 us -> 6.64 us
  transfers between devices with their start and end apart: 9 -> 9, of which waited for: 6 -> 6; matrix products, arithmetic and copies ran while one was open for 20% -> 19% of each run, Pallas kernels for 0% -> 0%
where the time goes in v5:
time: 296 us; the launch traced here: 294 us
  waiting for transfers between devices  173 us (58%)
  matrix products  42.1 us (14%)
  starting transfers between devices  32.7 us (11%)
  local copies, waits for them, and re-layouts  17.4 us (6%)
  between operations  15.1 us (5%)
  other arithmetic  14.3 us (5%)
    reduce_scatter x1, waiting for transfers between devices, local(): lax.psum_scatter(lax.dot_general(cross_out, attended, (((0,), (0,)), ((),...  82.5 us
    all_to_all x1, waiting for transfers between devices, local(): lax.all_to_all(jnp.transpose(kv_weights, (2, 0, 1, 3)), 'fsdp', split_axi...  34.5 us
    all_to_all x2, waiting for transfers between devices, gather_blocks(): lax.all_to_all(spread, axis_name, split_axis=0, concat_axis=0, tiled=True)  26.1 us
    all_to_all x1, waiting for transfers between devices, local(): lax.all_to_all(head_part.reshape(parts, row_part, vis_width), 'fsdp', spl...  14.6 us
    dot_general x1, matrix products, local(): lax.dot_general(cross_query, gained, contract_first, preferred_element_ty...  11.3 us
    all_to_all x1, starting transfers between devices, local(): lax.all_to_all(jnp.transpose(kv_weights, (2, 0, 1, 3)), 'fsdp', split_axi...  8.12 us
    all_to_all x2, starting transfers between devices, gather_blocks(): lax.all_to_all(spread, axis_name, split_axis=0, concat_axis=0, tiled=True)  8.05 us
    all_to_all x1, waiting for transfers between devices, local(): lax.all_to_all(jnp.transpose(resampled_rows.reshape(row_part, parts, feat...  7.76 us
  transfers between devices with their start and end apart: 9, of which 6 were waited for; matrix products, arithmetic and copies ran while one was open for 19% of the time, Pallas kernels for 0%

profile of v5, /device:TPU:0, one launch (start us, length us, event | category | flops | bytes accessed | tf_op | source)
XLA Modules:
  0.0 294.2 jit_solution(12029103910525448522)
XLA Ops:
  6.5 0.7 all-gather.2.cloned.1.call-update
  7.3 11.3 %fusion = bf16[8192,512]{0,1:T(8,128)(2,1)} fusion(bf16[512,8192]{1,0:T(8,128)(2,1)} %param.34, bf16[512,512]{1,0:T(8,128)(2,1)} %param.19, f32[512]{0:T(512)} %param.20), kind=kOutput, calls=%fused_computation.3 | convolution fusion | flops 4299948032 | bytes 17303552 | tf_op jit(solution)/shard_map/dot_general | solution.py:124
  18.7 1.3 copy-done.4
  19.9 0.5 copy.79
  20.4 0.7 copy.61
  21.1 0.5 copy.80
  21.6 0.7 copy.62
  22.4 1.8 maximum_bitcast_fusion
  24.2 8.1 %all-to-all-start.1 = ((bf16[16,2,80,512]{3,2,1,0:T(8,128)(2,1)}), bf16[16,2,80,512]{3,2,1,0:T(8,128)(2,1)S(1)}, u32[]{:S(2)}, u32[]{:S(2)}) async-start(bf16[16,2,80,512]{3,2,1,0:T(8,128)(2,1)} %maximum_bitcast_fusion), calls=%async_computation.1 | async-start | bytes 5242880 | tf_op jit(solution)/shard_map/all_to_all | solution.py:113
  32.4 0.1 convert_reduce_fusion.2
  32.5 0.6 copy-done.17
  33.1 1.8 convolution_convert_fusion.8
  34.9 1.4 copy.60
  36.4 1.8 convolution_convert_fusion.9
  38.2 1.4 copy.58
  39.6 0.8 fusion.15
  40.4 1.3 compare_convert_fusion
  41.6 1.3 add_select_fusion.1
  42.9 34.5 %all-to-all-done.1 = bf16[16,2,80,512]{3,2,1,0:T(8,128)(2,1)S(1)} async-done(((bf16[16,2,80,512]{3,2,1,0:T(8,128)(2,1)}), bf16[16,2,80,512]{3,2,1,0:T(8,128)(2,1)S(1)}, u32[]{:S(2)}, u32[]{:S(2)}) %all-to-all-start.1) | async-done | bytes 2621472 | tf_op jit(solution)/shard_map/all_to_all | solution.py:113
  77.5 0.6 slice.20
  78.7 0.7 maximum_add_fusion
  79.4 0.6 broadcast_in_dim.12
  80.1 3.7 %all-to-all-start.2 = ((f32[16,1,592]{2,1,0:T(1,128)}), f32[16,1,592]{2,1,0:T(1,128)S(1)}, u32[]{:S(2)}, u32[]{:S(2)}) async-start(f32[16,1,592]{2,1,0:T(1,128)} %broadcast_in_dim.12), calls=%async_computation.2 | async-start | bytes 81920 | tf_op jit(solution)/shard_map/all_to_all | solution.py:67
  83.8 2.5 convert_reduce_fusion
  86.4 3.5 %convolution_convert_fusion.4 = bf16[4,256,96]{1,2,0:T(8,128)(2,1)} fusion(bf16[4,256,1280]{1,2,0:T(8,128)(2,1)} %all-gather.2.cloned.1.call-done, f32[1280]{0:T(1024)} %param.27, f32[4,256]{1,0:T(4,128)S(1)} %get-tuple-element.16, f32[4,256]{1,0:T(4,128)S(1)} %get-tuple-element.15, bf16[1280,96]{0,1:T(8,128)(2,1)} %param.30), kind=kOutput, calls=%fused_computation.31 | convolution fusion | flops 258310144 | bytes 3077120 | tf_op jit(solution)/shard_map/npv,vk->npk/dot_general | solution.py:138
  89.9 2.3 fusion.59
  92.2 3.0 %convolution_convert_fusion.5 = bf16[4,256,96]{1,2,0:T(8,128)(2,1)S(1)} fusion(bf16[4,256,1280]{1,2,0:T(8,128)(2,1)} %all-gather.2.cloned.1.call-done, f32[1280]{0:T(1024)S(1)} %copy-done.23, f32[4,256]{1,0:T(4,128)S(1)} %get-tuple-element.16, f32[4,256]{1,0:T(4,128)S(1)} %get-tuple-element.15, bf16[1280,96]{0,1:T(8,128)(2,1)} %param.31), kind=kOutput, calls=%fused_computation.32 | convolution fusion | flops 258310144 | bytes 3077120 | tf_op jit(solution)/shard_map/npv,vk->npk/dot_general | solution.py:141
  95.2 0.3 convolution_convert_fusion.6
  95.6 1.2 convolution_convert_fusion.3
  96.7 0.6 copy-done.7
  97.3 7.2 %all-to-all-start = ((bf16[16,16,1280]{2,1,0:T(8,128)(2,1)}), bf16[16,16,1280]{2,1,0:T(8,128)(2,1)S(1)}, u32[]{:S(2)}, u32[]{:S(2)}) async-start(bf16[16,16,1280]{2,1,0:T(8,128)(2,1)} %bitcast.12), calls=%async_computation | async-start | bytes 1310720 | tf_op jit(solution)/shard_map/all_to_all | solution.py:167
  104.5 0.3 convert_reduce_fusion.3
  104.9 0.1 convolution_convert_fusion.10
  105.0 0.8 copy.90
  105.9 0.5 copy-done.8
  106.4 14.6 %all-to-all-done = bf16[16,16,1280]{2,1,0:T(8,128)(2,1)S(1)} async-done(((bf16[16,16,1280]{2,1,0:T(8,128)(2,1)}), bf16[16,16,1280]{2,1,0:T(8,128)(2,1)S(1)}, u32[]{:S(2)}, u32[]{:S(2)}) %all-to-all-start) | async-done | bytes 655392 | tf_op jit(solution)/shard_map/all_to_all | solution.py:167
  121.1 0.9 fusion.35
  122.0 0.9 multiply_convert_fusion.1
  122.9 0.1 reshape.219
  123.1 0.6 copy.89
  123.7 4.5 %all-to-all-start.3 = ((bf16[16,16,80]{2,1,0:T(8,128)(2,1)}), bf16[16,16,80]{2,1,0:T(8,128)(2,1)S(1)}, u32[]{:S(2)}, u32[]{:S(2)}) async-start(bf16[16,16,80]{2,1,0:T(8,128)(2,1)} %bitcast.96), calls=%async_computation.3 | async-start | bytes 131072 | tf_op jit(solution)/shard_map/all_to_all | solution.py:174
  128.2 7.8 %all-to-all-done.3 = bf16[16,16,80]{2,1,0:T(8,128)(2,1)S(1)} async-done(((bf16[16,16,80]{2,1,0:T(8,128)(2,1)}), bf16[16,16,80]{2,1,0:T(8,128)(2,1)S(1)}, u32[]{:S(2)}, u32[]{:S(2)}) %all-to-all-start.3) | async-done | bytes 40992 | tf_op jit(solution)/shard_map/all_to_all | solution.py:174
  136.0 0.2 reshape.226
  136.2 0.2 convolution_convert_fusion.2
  136.3 0.8 copy.65
  137.2 4.8 %all-to-all-start.4 = ((bf16[8,2,5120]{2,1,0:T(2,128)(2,1)}), bf16[8,2,5120]{2,1,0:T(2,128)(2,1)S(1)}, u32[]{:S(2)}, u32[]{:S(2)}) async-start(bf16[8,2,5120]{2,1,0:T(2,128)(2,1)} %copy.65), calls=%async_computation.4 | async-start | bytes 327680 | tf_op jit(solution)/shard_map/all_to_all | solution.py:183
  142.0 6.4 %all-to-all-done.4 = bf16[8,2,5120]{2,1,0:T(2,128)(2,1)S(1)} async-done(((bf16[8,2,5120]{2,1,0:T(2,128)(2,1)}), bf16[8,2,5120]{2,1,0:T(2,128)(2,1)S(1)}, u32[]{:S(2)}, u32[]{:S(2)}) %all-to-all-start.4) | async-done | bytes 163872 | tf_op jit(solution)/shard_map/all_to_all | solution.py:183
  148.4 0.3 fusion.2
  148.7 0.2 broadcast_in_dim.13
  149.0 1.2 broadcast_in_dim.14
  150.2 4.4 %all-to-all-start.5 = ((bf16[16,512,80]{1,2,0:T(8,128)(2,1)}), bf16[16,512,80]{1,2,0:T(8,128)(2,1)}, u32[]{:S(2)}, u32[]{:S(2)}) async-start(bf16[16,512,80]{1,2,0:T(8,128)(2,1)} %broadcast_in_dim.14), calls=%async_computation.5 | async-start | bytes 2621440 | tf_op jit(solution)/shard_map/all_to_all | solution.py:67
  154.7 26.1 %all-to-all-done.5 = bf16[16,512,80]{1,2,0:T(8,128)(2,1)} async-done(((bf16[16,512,80]{1,2,0:T(8,128)(2,1)}), bf16[16,512,80]{1,2,0:T(8,128)(2,1)}, u32[]{:S(2)}, u32[]{:S(2)}) %all-to-all-start.5) | async-done | bytes 1310752 | tf_op jit(solution)/shard_map/all_to_all | solution.py:67
  180.8 7.4 %reduce-precision_reduce_fusion = bf16[512,2,512]{2,0,1:T(8,128)(2,1)} fusion(bf16[16,2,80,512]{3,2,1,0:T(8,128)(2,1)S(1)} %all-to-all-done.1, bf16[16,512,80]{1,2,0:T(8,128)(2,1)} %all-to-all-done.5), kind=kOutput, calls=%fused_computation | convolution fusion | flops 1358430208 | bytes 4980736 | tf_op jit(solution)/shard_map/brk,bskc->brsc/dot_general | solution.py:188
  188.2 1.3 convert_element_type.168
  189.6 0.4 fusion.58
  190.1 1.2 multiply_convert_fusion
  191.3 0.2 copy.75
  191.6 0.9 fusion.7
  192.5 1.0 fusion.11
  193.5 0.2 slice-done
  193.7 1.5 slice-done.1
  195.2 7.0 %fusion.1 = bf16[8192,512]{0,1:T(8,128)(2,1)} fusion(bf16[512,512]{1,0:T(8,128)(2,1)S(1)} %bitcast.107, bf16[512,8192]{1,0:T(8,128)(2,1)S(1)} %bitcast.100), kind=kOutput, calls=%fused_computation.4 | convolution fusion | flops 4299161600 | bytes 17301504 | tf_op jit(solution)/shard_map/dot_general | solution.py:209
  203.0 82.5 %reduce-scatter.5.cloned.1.call-done = bf16[512,512]{0,1:T(8,128)(2,1)} async-done(((bf16[8192,512]{0,1:T(8,128)(2,1)}), bf16[512,512]{0,1:T(8,128)(2,1)}) %reduce-scatter.5.cloned.1.call-update) | async-done | bytes 524304 | tf_op jit(solution)/shard_map/reduce_scatter | solution.py:208
  285.5 2.2 convert_add_fusion
  (77 shorter events, 0.9 us)
Async XLA Ops:
  6.5 89.0 %copy-start = (bf16[96,1280]{1,0:T(8,128)(2,1)S(1)}, bf16[96,1280]{1,0:T(8,128)(2,1)}, u32[]{:S(2)}) copy-start(bf16[96,1280]{1,0:T(8,128)(2,1)} %param.32) | copy-start | bytes 737284
  6.5 77.3 %all-gather.2.cloned.1.call-start = ((), (), s32[]{:S(2)}) async-start(), calls=%async_computation.8 | async-start | bytes 2785280 | tf_op jit(solution)/shard_map/all_gather | solution.py:131
  7.3 182.8 %reduce-scatter.3.cloned.1.call-start = ((), (), s32[]{:S(2)}) async-start(), calls=%async_computation.9 | async-start | bytes 8912896 | tf_op jit(solution)/shard_map/reduce_scatter | solution.py:123
  18.6 1.3 copy-start.4
  18.7 2.5 copy-start.5
  22.4 10.0 %copy-start.6 = (bf16[64,1280]{1,0:T(8,128)(2,1)S(1)}, bf16[64,1280]{1,0:T(8,128)(2,1)}, u32[]{:S(2)}) copy-start(bf16[64,1280]{1,0:T(8,128)(2,1)} %param.26) | copy-start | bytes 491524
  24.2 15.4 %copy-start.2 = (bf16[512,512]{1,0:T(8,128)(2,1)S(1)}, bf16[512,512]{1,0:T(8,128)(2,1)}, u32[]{:S(2)}) copy-start(bf16[512,512]{1,0:T(8,128)(2,1)} %param.19) | copy-start | bytes 1572868
  24.2 53.2 %all-to-all-start.1 = ((bf16[16,2,80,512]{3,2,1,0:T(8,128)(2,1)}), bf16[16,2,80,512]{3,2,1,0:T(8,128)(2,1)S(1)}, u32[]{:S(2)}, u32[]{:S(2)}) async-start(bf16[16,2,80,512]{3,2,1,0:T(8,128)(2,1)} %maximum_bitcast_fusion), calls=%async_computation.1 | async-start | bytes 5242880 | tf_op jit(solution)/shard_map/all_to_all | solution.py:113
  32.5 0.6 copy-start.17
  32.5 0.6 copy-start.19
  80.1 16.6 %all-to-all-start.2 = ((f32[16,1,592]{2,1,0:T(1,128)}), f32[16,1,592]{2,1,0:T(1,128)S(1)}, u32[]{:S(2)}, u32[]{:S(2)}) async-start(f32[16,1,592]{2,1,0:T(1,128)} %broadcast_in_dim.12), calls=%async_computation.2 | async-start | bytes 81920 | tf_op jit(solution)/shard_map/all_to_all | solution.py:67
  83.7 6.1 %copy-start.11 = (bf16[64,96]{0,1:T(8,128)(2,1)S(1)}, bf16[64,96]{0,1:T(8,128)(2,1)}, u32[]{:S(2)}) copy-start(bf16[64,96]{0,1:T(8,128)(2,1)} %copy.60) | copy-start | bytes 36868
  83.8 6.1 %copy-start.18 = (f32[64]{0:T(128)S(1)}, f32[64]{0:T(128)}, u32[]{:S(2)}) copy-start(f32[64]{0:T(128)} %copy-done.17) | copy-start | bytes 772
  83.8 6.1 %copy-start.20 = (f32[64]{0:T(128)S(1)}, f32[64]{0:T(128)}, u32[]{:S(2)}) copy-start(f32[64]{0:T(128)} %copy-done.19) | copy-start | bytes 772
  83.8 6.1 %copy-start.21 = (bf16[1280,96]{0,1:T(8,128)(2,1)S(1)}, bf16[1280,96]{0,1:T(8,128)(2,1)}, u32[]{:S(2)}) copy-start(bf16[1280,96]{0,1:T(8,128)(2,1)} %param.29) | copy-start | bytes 737284
  83.8 6.1 %copy-start.22 = (f32[1280]{0:T(1024)S(1)}, f32[1280]{0:T(1024)}, u32[]{:S(2)}) copy-start(f32[1280]{0:T(1024)} %param.28) | copy-start | bytes 15364
  86.3 5.9 %copy-start.23 = (f32[1280]{0:T(1024)S(1)}, f32[1280]{0:T(1024)}, u32[]{:S(2)}) copy-start(f32[1280]{0:T(1024)} %param.27) | copy-start | bytes 15364
  89.8 5.4 %copy-start.10 = (bf16[64,96]{0,1:T(8,128)(2,1)S(1)}, bf16[64,96]{0,1:T(8,128)(2,1)}, u32[]{:S(2)}) copy-start(bf16[64,96]{0,1:T(8,128)(2,1)} %copy.58) | copy-start | bytes 36868
  92.2 3.0 %copy-start.24 = (f32[4,1,64,320]{3,2,0,1:T(8,128)S(1)}, f32[4,1,64,320]{3,2,0,1:T(8,128)}, u32[]{:S(2)}) copy-start(f32[4,1,64,320]{3,2,0,1:T(8,128)} %get-tuple-element.22) | copy-start | bytes 983044
  92.2 12.3 %copy-start.12 = (s32[8,8]{1,0:T(8,128)S(1)}, s32[8,8]{1,0:T(8,128)}, u32[]{:S(2)}) copy-start(s32[8,8]{1,0:T(8,128)} %get-tuple-element.13) | copy-start | bytes 772
  92.2 12.6 %copy-start.13 = (s32[8,8]{1,0:T(8,128)S(1)}, s32[8,8]{1,0:T(8,128)}, u32[]{:S(2)}) copy-start(s32[8,8]{1,0:T(8,128)} %get-tuple-element.14) | copy-start | bytes 772
  92.2 12.6 %copy-start.16 = (bf16[8,8]{1,0:T(8,128)(2,1)S(1)}, bf16[8,8]{1,0:T(8,128)(2,1)}, u32[]{:S(2)}) copy-start(bf16[8,8]{1,0:T(8,128)(2,1)} %compare_convert_fusion) | copy-start | bytes 388
  96.7 0.6 copy-start.7
  96.7 57.9 %copy-start.14 = (s32[1,512]{1,0:T(1,128)S(1)}, s32[1,512]{1,0:T(1,128)}, u32[]{:S(2)}) copy-start(s32[1,512]{1,0:T(1,128)} %param.23) | copy-start | bytes 6148
  97.3 23.7 %all-to-all-start = ((bf16[16,16,1280]{2,1,0:T(8,128)(2,1)}), bf16[16,16,1280]{2,1,0:T(8,128)(2,1)S(1)}, u32[]{:S(2)}, u32[]{:S(2)}) async-start(bf16[16,16,1280]{2,1,0:T(8,128)(2,1)} %bitcast.12), calls=%async_computation | async-start | bytes 1310720 | tf_op jit(solution)/shard_map/all_to_all | solution.py:167
  105.8 0.6 copy-start.8
  121.1 33.5 %copy-start.9 = (f32[16,1,592]{2,0,1:T(8,128)S(1)}, f32[16,1,592]{2,0,1:T(8,128)}, u32[]{:S(2)}) copy-start(f32[16,1,592]{2,0,1:T(8,128)} %copy-done.8) | copy-start | bytes 113668
  123.7 12.3 %all-to-all-start.3 = ((bf16[16,16,80]{2,1,0:T(8,128)(2,1)}), bf16[16,16,80]{2,1,0:T(8,128)(2,1)S(1)}, u32[]{:S(2)}, u32[]{:S(2)}) async-start(bf16[16,16,80]{2,1,0:T(8,128)(2,1)} %bitcast.96), calls=%async_computation.3 | async-start | bytes 131072 | tf_op jit(solution)/shard_map/all_to_all | solution.py:174
  137.2 11.2 %all-to-all-start.4 = ((bf16[8,2,5120]{2,1,0:T(2,128)(2,1)}), bf16[8,2,5120]{2,1,0:T(2,128)(2,1)S(1)}, u32[]{:S(2)}, u32[]{:S(2)}) async-start(bf16[8,2,5120]{2,1,0:T(2,128)(2,1)} %copy.65), calls=%async_computation.4 | async-start | bytes 327680 | tf_op jit(solution)/shard_map/all_to_all | solution.py:183
  150.2 30.6 %all-to-all-start.5 = ((bf16[16,512,80]{1,2,0:T(8,128)(2,1)}), bf16[16,512,80]{1,2,0:T(8,128)(2,1)}, u32[]{:S(2)}, u32[]{:S(2)}) async-start(bf16[16,512,80]{1,2,0:T(8,128)(2,1)} %broadcast_in_dim.14), calls=%async_computation.5 | async-start | bytes 2621440 | tf_op jit(solution)/shard_map/all_to_all | solution.py:67
  154.6 130.9 %reduce-scatter.5.cloned.1.call-start = ((), (), s32[]{:S(2)}) async-start(), calls=%async_computation.10 | async-start | bytes 8912896 | tf_op jit(solution)/shard_map/reduce_scatter | solution.py:208
  191.5 2.2 slice-start
  192.4 2.8 slice-start.1
  202.2 85.5 %copy-start.1 = (bf16[96,1280]{1,0:T(8,128)(2,1)S(1)}, bf16[96,1280]{1,0:T(8,128)(2,1)}, u32[]{:S(2)}) copy-start(bf16[96,1280]{1,0:T(8,128)(2,1)} %param.32) | copy-start | bytes 737284
  202.2 0.7 copy-start.15
  202.2 83.2 %copy-start.3 = (bf16[512,512]{1,0:T(8,128)(2,1)S(1)}, bf16[512,512]{1,0:T(8,128)(2,1)}, u32[]{:S(2)}) copy-start(bf16[512,512]{1,0:T(8,128)(2,1)} %param.19) | copy-start | bytes 1572868
Sparse Core Ops, SparseCore 0:
  9.5 68.3 all-gather.1
  81.3 101.8 reduce-scatter.2
  202.4 83.0 reduce-scatter.4

commit v6 on v5

--- a/solution.py
+++ b/solution.py
@@ -109,13 +109,17 @@
     slot_count = wanted_images.shape[1]
     cross_heads = head_cols // HEAD
     contract_first = (((0,), (1,)), ((), ()))
-    kv_weights = jnp.stack([cross_key, cross_value], 0).reshape(2, feat_vis, parts, head_cols)
-    kv_weights = lax.all_to_all(
-        jnp.transpose(kv_weights, (2, 0, 1, 3)), "fsdp", split_axis=0, concat_axis=0, tiled=True
-    )
+    my_core = my_shard % 2
+    kv_stack = jnp.stack([cross_key, cross_value], 0)
+    my_kind = lax.dynamic_index_in_dim(kv_stack, my_core, 0, keepdims=False)
+    my_kind = jnp.transpose(my_kind.reshape(feat_vis, parts, head_cols), (1, 0, 2))
+    my_kind = lax.all_to_all(my_kind, "fsdp", split_axis=0, concat_axis=0, tiled=True)
+    core_pairs = [(j, j ^ 1) for j in range(lax.axis_size("img"))]
+    other_kind = lax.ppermute(my_kind, "img", core_pairs)
+    kv_weights = jnp.stack([my_kind, other_kind], 1)
     text_f = text_states.astype(jnp.float32)
     gained = (text_f * text_gain).astype(jnp.bfloat16)
-    after_weights = kv_weights[0, 0, 0, 0].astype(jnp.float32) * 0.0
+    after_weights = my_kind[0, 0, 0].astype(jnp.float32) * 0.0
     stats = jnp.concatenate([jnp.sum(text_f * text_f, -1), final_gain], 0) + after_weights
     stats = gather_blocks(stats, "fsdp", parts)
     squares = jnp.sum(stats[:, :token_count], 0)
@@ -188,8 +192,8 @@
     slot_kv = jnp.einsum("brk,bskc->brsc", slot_blocks, kv_weights, preferred_element_type=jnp.float32)
     slot_kv = jnp.sum(lax.reduce_precision(slot_kv, exponent_bits=8, mantissa_bits=7), 0)
     slot_kv = slot_kv.astype(jnp.bfloat16).reshape(slot_count, latent_count, 2, cross_heads, HEAD)
-    slot_keys = slot_kv[:, :, 0]
-    slot_values = slot_kv[:, :, 1]
+    slot_keys = lax.dynamic_index_in_dim(slot_kv, my_core, 2, keepdims=False)
+    slot_values = lax.dynamic_index_in_dim(slot_kv, 1 - my_core, 2, keepdims=False)
     token_scale = lax.rsqrt(squares / D + eps_rms)
     query_cols = (query_cols.astype(jnp.float32) * token_scale[None, :]).astype(jnp.bfloat16)
     query_heads = query_cols.reshape(cross_heads, HEAD, token_count)

time: 296 us -> 273 us (0.922)
  waiting for transfers between devices: 173 us -> 164 us
  other arithmetic: 14.3 us -> 8.61 us
  matrix products: 42.1 us -> 37.7 us
    all_to_all x1, waiting for transfers between devices: 34.5 us -> 17.5 us  [local(): lax.all_to_all(my_kind, 'fsdp', split_axis=0, concat_axis=0, tiled=True)]
    reduce_scatter x1, waiting for transfers between devices: 0.02 us -> 6.79 us  [local(): lax.psum_scatter(lax.dot_general(cross_query, gained, contract_first, pre...]
    all_to_all x2, waiting for transfers between devices: 26.1 us -> 20.8 us  [gather_blocks(): lax.all_to_all(spread, axis_name, split_axis=0, concat_axis=0, tiled=True)]
    all_gather x1, waiting for transfers between devices: 0.02 us -> 4.37 us  [local(): full_patches = lax.all_gather(patches, 'fsdp', axis=2, tiled=True)]
  transfers between devices with their start and end apart: 9 -> 10, of which waited for: 6 -> 8; matrix products, arithmetic and copies ran while one was open for 19% -> 16% of each run, Pallas kernels for 0% -> 0%
where the time goes in v6:
time: 273 us; the launch traced here: 272 us
  waiting for transfers between devices  164 us (60%)
  matrix products  37.7 us (14%)
  starting transfers between devices  32.4 us (12%)
  between operations  14.9 us (5%)
  local copies, waits for them, and re-layouts  14.7 us (5%)
  other arithmetic  8.61 us (3%)
    reduce_scatter x1, waiting for transfers between devices, local(): lax.psum_scatter(lax.dot_general(cross_out, attended, (((0,), (0,)), ((),...  84.7 us
    all_to_all x2, waiting for transfers between devices, gather_blocks(): lax.all_to_all(spread, axis_name, split_axis=0, concat_axis=0, tiled=True)  20.8 us
    all_to_all x1, waiting for transfers between devices, local(): lax.all_to_all(my_kind, 'fsdp', split_axis=0, concat_axis=0, tiled=True)  17.5 us
    all_to_all x1, waiting for transfers between devices, local(): lax.all_to_all(head_part.reshape(parts, row_part, vis_width), 'fsdp', spl...  15.1 us
    dot_general x1, matrix products, local(): lax.dot_general(cross_query, gained, contract_first, preferred_element_ty...  11.3 us
    all_to_all x2, starting transfers between devices, gather_blocks(): lax.all_to_all(spread, axis_name, split_axis=0, concat_axis=0, tiled=True)  8.54 us
    all_to_all x1, starting transfers between devices, local(): lax.all_to_all(my_kind, 'fsdp', split_axis=0, concat_axis=0, tiled=True)  8.02 us
    all_to_all x1, waiting for transfers between devices, local(): lax.all_to_all(jnp.transpose(resampled_rows.reshape(row_part, parts, feat...  7.75 us
  transfers between devices with their start and end apart: 10, of which 8 were waited for; matrix products, arithmetic and copies ran while one was open for 16% of the time, Pallas kernels for 0%

profile of v6, /device:TPU:0, one launch (start us, length us, event | category | flops | bytes accessed | tf_op | source)
XLA Modules:
  0.0 271.9 jit_solution(3627537051809307478)
XLA Ops:
  6.5 0.7 all-gather.2.cloned.1.call-update
  7.3 11.3 %fusion = bf16[8192,512]{0,1:T(8,128)(2,1)} fusion(bf16[512,8192]{1,0:T(8,128)(2,1)} %param.34, bf16[512,512]{1,0:T(8,128)(2,1)} %param.19, f32[512]{0:T(512)} %param.20), kind=kOutput, calls=%fused_computation.3 | convolution fusion | flops 4299948032 | bytes 17303552 | tf_op jit(solution)/shard_map/dot_general | solution.py:128
  18.7 1.3 copy-done.3
  20.0 0.4 copy-done.4
  20.4 0.5 fusion.13
  20.9 0.5 copy.78
  21.4 1.8 copy.90
  23.2 8.0 %all-to-all-start.1 = ((bf16[16,80,512]{2,1,0:T(8,128)(2,1)}), bf16[16,80,512]{2,1,0:T(8,128)(2,1)S(1)}, u32[]{:S(2)}, u32[]{:S(2)}) async-start(bf16[16,80,512]{2,1,0:T(8,128)(2,1)} %bitcast.98), calls=%async_computation.1 | async-start | bytes 2621440 | tf_op jit(solution)/shard_map/all_to_all | solution.py:116
  31.2 0.1 convert_reduce_fusion.2
  31.4 0.3 convolution_convert_fusion.8
  31.7 0.7 copy.61
  32.4 0.2 convolution_convert_fusion.9
  32.6 0.7 copy.59
  33.3 0.2 fusion.19
  33.5 0.6 compare_convert_fusion
  34.1 0.6 add_select_fusion.1
  34.7 17.5 %all-to-all-done.1 = bf16[16,80,512]{2,1,0:T(8,128)(2,1)S(1)} async-done(((bf16[16,80,512]{2,1,0:T(8,128)(2,1)}), bf16[16,80,512]{2,1,0:T(8,128)(2,1)S(1)}, u32[]{:S(2)}, u32[]{:S(2)}) %all-to-all-start.1) | async-done | bytes 1310752 | tf_op jit(solution)/shard_map/all_to_all | solution.py:116
  52.2 0.5 slice.12
  53.4 0.6 broadcast_in_dim.12
  54.0 4.1 %all-to-all-start.2 = ((f32[16,1,592]{2,1,0:T(1,128)}), f32[16,1,592]{2,1,0:T(1,128)}, u32[]{:S(2)}, u32[]{:S(2)}) async-start(f32[16,1,592]{2,1,0:T(1,128)} %broadcast_in_dim.12), calls=%async_computation.2 | async-start | bytes 81920 | tf_op jit(solution)/shard_map/all_to_all | solution.py:67
  58.1 4.4 %all-gather.2.cloned.1.call-done = bf16[4,256,1280]{1,2,0:T(8,128)(2,1)} async-done(((bf16[4,256,80]{1,2,0:T(8,128)(2,1)}), bf16[4,256,1280]{1,2,0:T(8,128)(2,1)}) %all-gather.2.cloned.1.call-update) | async-done | bytes 2621456 | tf_op jit(solution)/shard_map/all_gather | solution.py:135
  62.5 2.4 convert_reduce_fusion
  65.0 0.6 copy-done.13
  65.6 3.6 %convolution_convert_fusion.4 = bf16[4,256,96]{1,2,0:T(8,128)(2,1)} fusion(bf16[4,256,1280]{1,2,0:T(8,128)(2,1)} %all-gather.2.cloned.1.call-done, f32[1280]{0:T(1024)} %param.27, f32[4,256]{1,0:T(4,128)S(1)} %get-tuple-element.16, f32[4,256]{1,0:T(4,128)S(1)} %get-tuple-element.15, bf16[1280,96]{0,1:T(8,128)(2,1)} %param.30), kind=kOutput, calls=%fused_computation.37 | convolution fusion | flops 258310144 | bytes 3077120 | tf_op jit(solution)/shard_map/npv,vk->npk/dot_general | solution.py:142
  69.2 0.6 broadcast_in_dim.11
  69.9 3.0 %fusion.65 = (f32[4,64]{1,0:T(4,128)}, f32[4,1,64,320]{3,2,0,1:T(8,128)}) fusion(bf16[4,64,96]{1,2,0:T(8,128)(2,1)} %broadcast_in_dim.11, bf16[4,256,96]{1,2,0:T(8,128)(2,1)} %convolution_convert_fusion.4, bf16[1280,96]{0,1:T(8,128)(2,1)} %param.29, bf16[64,1280]{1,0:T(8,128)(2,1)S(1)} %copy-done.7, f32[1280]{0:T(1024)} %param.28, f32[64]{0:T(128)} %copy-done.20, ...), kind=kOutput, calls=%fused_computation.122 | convolution fusion | flops 32528128 | bytes 989696 | tf_op jit(solution)/shard_map/rhe,nkhe->nhrk/dot_general | solution.py:159
  72.9 2.0 convolution_convert_fusion.5
  75.0 0.3 convolution_convert_fusion.6
  75.3 1.2 convolution_convert_fusion.3
  76.5 5.2 %all-to-all-start = ((bf16[16,16,1280]{2,1,0:T(8,128)(2,1)}), bf16[16,16,1280]{2,1,0:T(8,128)(2,1)S(1)}, u32[]{:S(2)}, u32[]{:S(2)}) async-start(bf16[16,16,1280]{2,1,0:T(8,128)(2,1)} %bitcast.12), calls=%async_computation | async-start | bytes 1310720 | tf_op jit(solution)/shard_map/all_to_all | solution.py:171
  81.7 0.3 convert_reduce_fusion.3
  82.0 0.1 convolution_convert_fusion.10
  82.2 0.8 copy.92
  83.0 15.1 %all-to-all-done = bf16[16,16,1280]{2,1,0:T(8,128)(2,1)S(1)} async-done(((bf16[16,16,1280]{2,1,0:T(8,128)(2,1)}), bf16[16,16,1280]{2,1,0:T(8,128)(2,1)S(1)}, u32[]{:S(2)}, u32[]{:S(2)}) %all-to-all-start) | async-done | bytes 655392 | tf_op jit(solution)/shard_map/all_to_all | solution.py:171
  98.2 0.1 fusion.41
  98.5 0.1 reshape.219
  98.6 0.6 copy.91
  99.3 5.8 %all-to-all-start.3 = ((bf16[16,16,80]{2,1,0:T(8,128)(2,1)}), bf16[16,16,80]{2,1,0:T(8,128)(2,1)S(1)}, u32[]{:S(2)}, u32[]{:S(2)}) async-start(bf16[16,16,80]{2,1,0:T(8,128)(2,1)} %bitcast.99), calls=%async_computation.3 | async-start | bytes 131072 | tf_op jit(solution)/shard_map/all_to_all | solution.py:178
  105.1 7.8 %all-to-all-done.3 = bf16[16,16,80]{2,1,0:T(8,128)(2,1)S(1)} async-done(((bf16[16,16,80]{2,1,0:T(8,128)(2,1)}), bf16[16,16,80]{2,1,0:T(8,128)(2,1)S(1)}, u32[]{:S(2)}, u32[]{:S(2)}) %all-to-all-start.3) | async-done | bytes 40992 | tf_op jit(solution)/shard_map/all_to_all | solution.py:178
  112.8 0.2 reshape.226
  113.0 0.2 convolution_convert_fusion.2
  113.1 0.8 copy.65
  114.0 4.3 %all-to-all-start.4 = ((bf16[8,2,5120]{2,1,0:T(2,128)(2,1)}), bf16[8,2,5120]{2,1,0:T(2,128)(2,1)S(1)}, u32[]{:S(2)}, u32[]{:S(2)}) async-start(bf16[8,2,5120]{2,1,0:T(2,128)(2,1)} %copy.65), calls=%async_computation.4 | async-start | bytes 327680 | tf_op jit(solution)/shard_map/all_to_all | solution.py:187
  118.4 0.5 collective-permute-start
  118.9 5.8 %all-to-all-done.4 = bf16[8,2,5120]{2,1,0:T(2,128)(2,1)S(1)} async-done(((bf16[8,2,5120]{2,1,0:T(2,128)(2,1)}), bf16[8,2,5120]{2,1,0:T(2,128)(2,1)S(1)}, u32[]{:S(2)}, u32[]{:S(2)}) %all-to-all-start.4) | async-done | bytes 163872 | tf_op jit(solution)/shard_map/all_to_all | solution.py:187
  124.7 0.3 fusion.2
  125.0 0.2 broadcast_in_dim.13
  125.3 1.2 broadcast_in_dim.14
  126.5 4.4 %all-to-all-start.5 = ((bf16[16,512,80]{1,2,0:T(8,128)(2,1)}), bf16[16,512,80]{1,2,0:T(8,128)(2,1)}, u32[]{:S(2)}, u32[]{:S(2)}) async-start(bf16[16,512,80]{1,2,0:T(8,128)(2,1)} %broadcast_in_dim.14), calls=%async_computation.5 | async-start | bytes 2621440 | tf_op jit(solution)/shard_map/all_to_all | solution.py:67
  131.0 20.8 %all-to-all-done.5 = bf16[16,512,80]{1,2,0:T(8,128)(2,1)} async-done(((bf16[16,512,80]{1,2,0:T(8,128)(2,1)}), bf16[16,512,80]{1,2,0:T(8,128)(2,1)}, u32[]{:S(2)}, u32[]{:S(2)}) %all-to-all-start.5) | async-done | bytes 1310752 | tf_op jit(solution)/shard_map/all_to_all | solution.py:67
  151.8 6.3 %reduce-precision_reduce_fusion = bf16[512,2,512]{2,0,1:T(8,128)(2,1)S(1)} fusion(bf16[16,1,80,512]{3,2,1,0:T(8,128)(2,1)} %bitcast.23, bf16[16,1,80,512]{3,2,1,0:T(8,128)(2,1)S(1)} %bitcast.110, bf16[16,512,80]{1,2,0:T(8,128)(2,1)} %all-to-all-done.5), kind=kOutput, calls=%fused_computation | convolution fusion | flops 1363673088 | bytes 4980736 | tf_op jit(solution)/shard_map/brk,bskc->brsc/dot_general | solution.py:192
  158.2 0.3 convert_element_type.168
  158.5 0.4 constant_dynamic-slice_fusion.1
  158.9 0.1 copy.70
  159.0 6.8 %reduce-scatter.3.cloned.1.call-done = bf16[512,512]{0,1:T(8,128)(2,1)} async-done(((bf16[8192,512]{0,1:T(8,128)(2,1)}), bf16[512,512]{0,1:T(8,128)(2,1)}) %reduce-scatter.3.cloned.1.call-update) | async-done | bytes 524304 | tf_op jit(solution)/shard_map/reduce_scatter | solution.py:127
  165.8 1.2 multiply_convert_fusion
  167.0 0.2 copy.76
  167.2 0.9 fusion.7
  168.1 1.0 fusion.15
  169.2 0.2 slice-done
  169.4 1.5 slice-done.1
  170.9 6.9 %fusion.1 = bf16[8192,512]{0,1:T(8,128)(2,1)} fusion(bf16[512,512]{1,0:T(8,128)(2,1)S(1)} %bitcast.111, bf16[512,8192]{1,0:T(8,128)(2,1)S(1)} %bitcast.103), kind=kOutput, calls=%fused_computation.4 | convolution fusion | flops 4299161600 | bytes 17301504 | tf_op jit(solution)/shard_map/dot_general | solution.py:213
  178.5 84.7 %reduce-scatter.5.cloned.1.call-done = bf16[512,512]{0,1:T(8,128)(2,1)} async-done(((bf16[8192,512]{0,1:T(8,128)(2,1)}), bf16[512,512]{0,1:T(8,128)(2,1)}) %reduce-scatter.5.cloned.1.call-update) | async-done | bytes 524304 | tf_op jit(solution)/shard_map/reduce_scatter | solution.py:212
  263.2 2.2 convert_add_fusion
  (79 shorter events, 0.8 us)
Async XLA Ops:
  6.5 68.8 %copy-start = (bf16[96,1280]{1,0:T(8,128)(2,1)S(1)}, bf16[96,1280]{1,0:T(8,128)(2,1)}, u32[]{:S(2)}) copy-start(bf16[96,1280]{1,0:T(8,128)(2,1)} %param.32) | copy-start | bytes 737284
  6.5 56.0 %all-gather.2.cloned.1.call-start = ((), (), s32[]{:S(2)}) async-start(), calls=%async_computation.8 | async-start | bytes 2785280 | tf_op jit(solution)/shard_map/all_gather | solution.py:135
  7.3 158.5 %reduce-scatter.3.cloned.1.call-start = ((), (), s32[]{:S(2)}) async-start(), calls=%async_computation.9 | async-start | bytes 8912896 | tf_op jit(solution)/shard_map/reduce_scatter | solution.py:127
  18.6 1.3 copy-start.3
  18.6 1.7 copy-start.4
  20.8 10.4 %copy-start.7 = (bf16[64,1280]{1,0:T(8,128)(2,1)S(1)}, bf16[64,1280]{1,0:T(8,128)(2,1)}, u32[]{:S(2)}) copy-start(bf16[64,1280]{1,0:T(8,128)(2,1)} %param.26) | copy-start | bytes 491524
  20.8 10.5 %copy-start.21 = (bf16[1280,96]{0,1:T(8,128)(2,1)S(1)}, bf16[1280,96]{0,1:T(8,128)(2,1)}, u32[]{:S(2)}) copy-start(bf16[1280,96]{0,1:T(8,128)(2,1)} %param.30) | copy-start | bytes 737284
  20.9 10.5 %copy-start.23 = (f32[1280]{0:T(1024)S(1)}, f32[1280]{0:T(1024)}, u32[]{:S(2)}) copy-start(f32[1280]{0:T(1024)} %param.28) | copy-start | bytes 15364
  20.9 11.5 %copy-start.22 = (bf16[1280,96]{0,1:T(8,128)(2,1)S(1)}, bf16[1280,96]{0,1:T(8,128)(2,1)}, u32[]{:S(2)}) copy-start(bf16[1280,96]{0,1:T(8,128)(2,1)} %param.31) | copy-start | bytes 737284
  20.9 12.5 %copy-start.2 = (bf16[512,512]{1,0:T(8,128)(2,1)S(1)}, bf16[512,512]{1,0:T(8,128)(2,1)}, u32[]{:S(2)}) copy-start(bf16[512,512]{1,0:T(8,128)(2,1)} %param.19) | copy-start | bytes 1572868
  21.4 12.2 %copy-start.11 = (s32[8,8]{1,0:T(8,128)S(1)}, s32[8,8]{1,0:T(8,128)}, u32[]{:S(2)}) copy-start(s32[8,8]{1,0:T(8,128)} %param.24) | copy-start | bytes 772
  21.4 32.0 %copy-start.18 = (f32[80]{0:T(128)S(1)}, f32[80]{0:T(128)}, u32[]{:S(2)}) copy-start(f32[80]{0:T(128)} %param.33) | copy-start | bytes 964
  23.2 29.1 %all-to-all-start.1 = ((bf16[16,80,512]{2,1,0:T(8,128)(2,1)}), bf16[16,80,512]{2,1,0:T(8,128)(2,1)S(1)}, u32[]{:S(2)}, u32[]{:S(2)}) async-start(bf16[16,80,512]{2,1,0:T(8,128)(2,1)} %bitcast.98), calls=%async_computation.1 | async-start | bytes 2621440 | tf_op jit(solution)/shard_map/all_to_all | solution.py:116
  31.4 31.2 %copy-start.19 = (f32[64]{0:T(128)}, f32[64]{0:T(128)S(1)}, u32[]{:S(2)}) copy-start(f32[64]{0:T(128)S(1)} %get-tuple-element.19) | copy-start | bytes 772
  31.4 31.1 %copy-start.20 = (f32[64]{0:T(128)}, f32[64]{0:T(128)S(1)}, u32[]{:S(2)}) copy-start(f32[64]{0:T(128)S(1)} %get-tuple-element.20) | copy-start | bytes 772
  52.2 10.3 %copy-start.5 = (bf16[16,80,512]{2,1,0:T(8,128)(2,1)}, bf16[16,80,512]{2,1,0:T(8,128)(2,1)S(1)}, u32[]{:S(2)}) copy-start(bf16[16,80,512]{2,1,0:T(8,128)(2,1)S(1)} %all-to-all-done.1) | copy-start | bytes 3932164
  54.0 22.5 %all-to-all-start.2 = ((f32[16,1,592]{2,1,0:T(1,128)}), f32[16,1,592]{2,1,0:T(1,128)}, u32[]{:S(2)}, u32[]{:S(2)}) async-start(f32[16,1,592]{2,1,0:T(1,128)} %broadcast_in_dim.12), calls=%async_computation.2 | async-start | bytes 81920 | tf_op jit(solution)/shard_map/all_to_all | solution.py:67
  62.5 6.7 %copy-start.9 = (bf16[64,96]{0,1:T(8,128)(2,1)S(1)}, bf16[64,96]{0,1:T(8,128)(2,1)}, u32[]{:S(2)}) copy-start(bf16[64,96]{0,1:T(8,128)(2,1)} %copy.61) | copy-start | bytes 36868
  65.0 7.9 %copy-start.1 = (bf16[4,256,1280]{1,2,0:T(8,128)(2,1)S(1)}, bf16[4,256,1280]{1,2,0:T(8,128)(2,1)}, u32[]{:S(2)}) copy-start(bf16[4,256,1280]{1,2,0:T(8,128)(2,1)} %all-gather.2.cloned.1.call-done) | copy-start | bytes 7864324
  65.0 0.6 copy-start.13
  65.0 4.2 %copy-start.14 = (f32[4,256]{1,0:T(4,128)}, f32[4,256]{1,0:T(4,128)S(1)}, u32[]{:S(2)}) copy-start(f32[4,256]{1,0:T(4,128)S(1)} %get-tuple-element.16) | copy-start | bytes 12292
  72.8 2.1 copy-start.8
  72.8 2.1 copy-start.24
  72.9 2.1 copy-start.25
  74.9 6.8 %copy-start.10 = (s32[8,8]{1,0:T(8,128)S(1)}, s32[8,8]{1,0:T(8,128)}, u32[]{:S(2)}) copy-start(s32[8,8]{1,0:T(8,128)} %get-tuple-element.13) | copy-start | bytes 772
  74.9 7.1 %copy-start.12 = (s32[8,8]{1,0:T(8,128)S(1)}, s32[8,8]{1,0:T(8,128)}, u32[]{:S(2)}) copy-start(s32[8,8]{1,0:T(8,128)} %get-tuple-element.14) | copy-start | bytes 772
  74.9 7.1 %copy-start.17 = (bf16[8,8]{1,0:T(8,128)(2,1)S(1)}, bf16[8,8]{1,0:T(8,128)(2,1)}, u32[]{:S(2)}) copy-start(bf16[8,8]{1,0:T(8,128)(2,1)} %compare_convert_fusion) | copy-start | bytes 388
  75.0 43.4 %copy-start.6 = (bf16[16,80,512]{2,1,0:T(8,128)(2,1)S(1)}, bf16[16,80,512]{2,1,0:T(8,128)(2,1)}, u32[]{:S(2)}) copy-start(bf16[16,80,512]{2,1,0:T(8,128)(2,1)} %copy-done.5) | copy-start | bytes 3932164
  76.5 54.5 %copy-start.15 = (s32[1,512]{1,0:T(1,128)S(1)}, s32[1,512]{1,0:T(1,128)}, u32[]{:S(2)}) copy-start(s32[1,512]{1,0:T(1,128)} %param.23) | copy-start | bytes 6148
  76.5 21.6 %all-to-all-start = ((bf16[16,16,1280]{2,1,0:T(8,128)(2,1)}), bf16[16,16,1280]{2,1,0:T(8,128)(2,1)S(1)}, u32[]{:S(2)}, u32[]{:S(2)}) async-start(bf16[16,16,1280]{2,1,0:T(8,128)(2,1)} %bitcast.12), calls=%async_computation | async-start | bytes 1310720 | tf_op jit(solution)/shard_map/all_to_all | solution.py:171
  99.3 13.6 %all-to-all-start.3 = ((bf16[16,16,80]{2,1,0:T(8,128)(2,1)}), bf16[16,16,80]{2,1,0:T(8,128)(2,1)S(1)}, u32[]{:S(2)}, u32[]{:S(2)}) async-start(bf16[16,16,80]{2,1,0:T(8,128)(2,1)} %bitcast.99), calls=%async_computation.3 | async-start | bytes 131072 | tf_op jit(solution)/shard_map/all_to_all | solution.py:178
  114.0 10.8 %all-to-all-start.4 = ((bf16[8,2,5120]{2,1,0:T(2,128)(2,1)}), bf16[8,2,5120]{2,1,0:T(2,128)(2,1)S(1)}, u32[]{:S(2)}, u32[]{:S(2)}) async-start(bf16[8,2,5120]{2,1,0:T(2,128)(2,1)} %copy.65), calls=%async_computation.4 | async-start | bytes 327680 | tf_op jit(solution)/shard_map/all_to_all | solution.py:187
  118.4 12.7 %collective-permute-start = (bf16[16,80,512]{2,1,0:T(8,128)(2,1)S(1)}, bf16[16,80,512]{2,1,0:T(8,128)(2,1)}, u32[]{:S(2)}, u32[]{:S(2)}) collective-permute-start(bf16[16,80,512]{2,1,0:T(8,128)(2,1)S(1)} %copy-done.6), channel_id=1, source_target_pairs={{0,16},{16,0},{32,48},{48,32},{64,80},{80,64},{96,112},{112,96},{1... | collective-permute-start | bytes 3932168 | tf_op jit(solution)/shard_map/ppermute | solution.py:118
  126.5 25.3 %all-to-all-start.5 = ((bf16[16,512,80]{1,2,0:T(8,128)(2,1)}), bf16[16,512,80]{1,2,0:T(8,128)(2,1)}, u32[]{:S(2)}, u32[]{:S(2)}) async-start(bf16[16,512,80]{1,2,0:T(8,128)(2,1)} %broadcast_in_dim.14), calls=%async_computation.5 | async-start | bytes 2621440 | tf_op jit(solution)/shard_map/all_to_all | solution.py:67
  130.9 132.3 %reduce-scatter.5.cloned.1.call-start = ((), (), s32[]{:S(2)}) async-start(), calls=%async_computation.10 | async-start | bytes 8912896 | tf_op jit(solution)/shard_map/reduce_scatter | solution.py:212
  167.2 2.2 slice-start
  168.1 2.8 %slice-start.1 = ((s8[8388608]{0:T(1024)(128)(4,1)}), s8[4194304]{0:T(1024)(128)(4,1)S(1)}, s32[]{:S(2)}) async-start(s8[8388608]{0:T(1024)(128)(4,1)} %bitcast.102), calls=%async_computation.12 | async-start | bytes 8388608
  177.8 0.7 copy-start.16
Sparse Core Ops, SparseCore 0:
  9.5 52.9 all-gather.1
  65.9 99.8 reduce-scatter.2
  177.9 85.1 reduce-scatter.4

commit v7 on v6

--- a/solution.py
+++ b/solution.py
@@ -111,7 +111,9 @@
     contract_first = (((0,), (1,)), ((), ()))
     my_core = my_shard % 2
     kv_stack = jnp.stack([cross_key, cross_value], 0)
-    my_kind = lax.dynamic_index_in_dim(kv_stack, my_core, 0, keepdims=False)
+    patch_blocks = gather_blocks(patches, "fsdp", parts)
+    after_patches = patch_blocks[0, 0, 0, 0] * 0
+    my_kind = lax.dynamic_index_in_dim(kv_stack, my_core, 0, keepdims=False) + after_patches
     my_kind = jnp.transpose(my_kind.reshape(feat_vis, parts, head_cols), (1, 0, 2))
     my_kind = lax.all_to_all(my_kind, "fsdp", split_axis=0, concat_axis=0, tiled=True)
     core_pairs = [(j, j ^ 1) for j in range(lax.axis_size("img"))]
@@ -132,7 +134,9 @@
         scatter_dimension=0,
         tiled=True,
     )
-    full_patches = lax.all_gather(patches, "fsdp", axis=2, tiled=True)
+    full_patches = jnp.transpose(patch_blocks, (1, 2, 0, 3)).reshape(
+        image_count, patch_count, vis_width
+    )
     context = layer_norm(full_patches, context_gain).astype(jnp.bfloat16)
     latent_normed = layer_norm(latent_init, latent_gain).astype(jnp.bfloat16)
     res_q_rows = jnp.dot(latent_normed, res_query, preferred_element_type=jnp.float32).astype(

time: 273 us -> 307 us (1.12)
  waiting for transfers between devices: 164 us -> 190 us
  starting transfers between devices: 32.4 us -> 38.7 us
    all_to_all x2 -> x3, waiting for transfers between devices: 20.8 us -> 66.3 us  [gather_blocks(): lax.all_to_all(spread, axis_name, split_axis=0, concat_axis=0, tiled=True)]
    all_to_all x2 -> x3, starting transfers between devices: 8.54 us -> 16.3 us  [gather_blocks(): lax.all_to_all(spread, axis_name, split_axis=0, concat_axis=0, tiled=True)]
    reduce_scatter x1, waiting for transfers between devices: 6.79 us -> 0.02 us  [local(): lax.psum_scatter(lax.dot_general(cross_query, gained, contract_first, pre...]
    all_to_all x1, waiting for transfers between devices: 15.1 us -> 10.6 us  [local(): lax.all_to_all(head_part.reshape(parts, row_part, vis_width), 'fsdp', spl...]
    all_gather x1 -> x0, waiting for transfers between devices: 4.37 us -> none  [local(): full_patches = lax.all_gather(patches, 'fsdp', axis=2, tiled=True)]
    reduce_scatter x1, waiting for transfers between devices: 84.7 us -> 81.4 us  [local(): lax.psum_scatter(lax.dot_general(cross_out, attended, (((0,), (0,)), ((),...]
  transfers between devices with their start and end apart: 10 -> 10, of which waited for: 8 -> 8; matrix products, arithmetic and copies ran while one was open for 16% -> 11% of each run, Pallas kernels for 0% -> 0%
where the time goes in v7:
time: 307 us; the launch traced here: 306 us
  waiting for transfers between devices  190 us (62%)
  starting transfers between devices  38.7 us (13%)
  matrix products  37.1 us (12%)
  local copies, waits for them, and re-layouts  16.1 us (5%)
  between operations  16 us (5%)
  other arithmetic  8.46 us (3%)
    reduce_scatter x1, waiting for transfers between devices, local(): lax.psum_scatter(lax.dot_general(cross_out, attended, (((0,), (0,)), ((),...  81.4 us
    all_to_all x3, waiting for transfers between devices, gather_blocks(): lax.all_to_all(spread, axis_name, split_axis=0, concat_axis=0, tiled=True)  66.3 us
    all_to_all x1, waiting for transfers between devices, local(): lax.all_to_all(my_kind, 'fsdp', split_axis=0, concat_axis=0, tiled=True)  18 us
    all_to_all x3, starting transfers between devices, gather_blocks(): lax.all_to_all(spread, axis_name, split_axis=0, concat_axis=0, tiled=True)  16.3 us
    dot_general x1, matrix products, local(): lax.dot_general(cross_query, gained, contract_first, preferred_element_ty...  11.4 us
    all_to_all x1, waiting for transfers between devices, local(): lax.all_to_all(head_part.reshape(parts, row_part, vis_width), 'fsdp', spl...  10.6 us
    all_to_all x1, starting transfers between devices, local(): lax.all_to_all(head_part.reshape(parts, row_part, vis_width), 'fsdp', spl...  7.77 us
    all_to_all x1, waiting for transfers between devices, local(): lax.all_to_all(jnp.transpose(resampled_rows.reshape(row_part, parts, feat...  7.48 us
  transfers between devices with their start and end apart: 10, of which 8 were waited for; matrix products, arithmetic and copies ran while one was open for 11% of the time, Pallas kernels for 0%

profile of v7, /device:TPU:0, one launch (start us, length us, event | category | flops | bytes accessed | tf_op | source)
XLA Modules:
  0.0 305.9 jit_solution(17589763367009017962)
XLA Ops:
  6.5 11.4 %fusion = bf16[8192,512]{0,1:T(8,128)(2,1)} fusion(bf16[512,8192]{1,0:T(8,128)(2,1)} %param.34, bf16[512,512]{1,0:T(8,128)(2,1)} %param.19, f32[512]{0:T(512)} %param.20), kind=kOutput, calls=%fused_computation.3 | convolution fusion | flops 4299948032 | bytes 17303552 | tf_op jit(solution)/shard_map/dot_general | solution.py:130
  17.9 0.9 copy-done.8
  18.8 1.8 broadcast_in_dim.12
  20.7 8.1 %all-to-all-start = ((bf16[16,4,256,80]{2,3,1,0:T(8,128)(2,1)}), bf16[16,4,256,80]{2,3,1,0:T(8,128)(2,1)S(1)}, u32[]{:S(2)}, u32[]{:S(2)}) async-start(bf16[16,4,256,80]{2,3,1,0:T(8,128)(2,1)} %broadcast_in_dim.12), calls=%async_computation | async-start | bytes 5242880 | tf_op jit(solution)/shard_map/all_to_all | solution.py:67
  28.8 0.1 convert_reduce_fusion.1
  29.0 1.0 convolution_convert_fusion.8
  30.0 0.7 copy.65
  30.7 1.6 convolution_convert_fusion.9
  32.3 0.8 copy.63
  33.1 0.6 add_select_fusion.1
  33.7 37.9 %all-to-all-done = bf16[16,4,256,80]{2,3,1,0:T(8,128)(2,1)S(1)} async-done(((bf16[16,4,256,80]{2,3,1,0:T(8,128)(2,1)}), bf16[16,4,256,80]{2,3,1,0:T(8,128)(2,1)S(1)}, u32[]{:S(2)}, u32[]{:S(2)}) %all-to-all-start) | async-done | bytes 2621472 | tf_op jit(solution)/shard_map/all_to_all | solution.py:67
  71.6 0.7 bitcast_reduce_fusion
  72.3 0.8 fusion.5
  73.1 1.6 copy-done.2
  74.7 1.2 convolution_convert_fusion.4
  75.9 2.4 fusion.64
  78.3 2.4 convolution_convert_fusion.5
  80.7 0.3 convolution_convert_fusion.6
  81.1 1.2 convolution_convert_fusion.3
  82.2 7.8 %all-to-all-start.1 = ((bf16[16,16,1280]{2,1,0:T(8,128)(2,1)}), bf16[16,16,1280]{2,1,0:T(8,128)(2,1)S(1)}, u32[]{:S(2)}, u32[]{:S(2)}) async-start(bf16[16,16,1280]{2,1,0:T(8,128)(2,1)} %bitcast.123), calls=%async_computation.1 | async-start | bytes 1310720 | tf_op jit(solution)/shard_map/all_to_all | solution.py:175
  90.0 0.6 slice.16
  91.3 1.9 fusion.14
  93.1 0.5 copy.82
  93.6 1.9 copy.97
  95.5 10.6 %all-to-all-done.1 = bf16[16,16,1280]{2,1,0:T(8,128)(2,1)S(1)} async-done(((bf16[16,16,1280]{2,1,0:T(8,128)(2,1)}), bf16[16,16,1280]{2,1,0:T(8,128)(2,1)S(1)}, u32[]{:S(2)}, u32[]{:S(2)}) %all-to-all-start.1) | async-done | bytes 655392 | tf_op jit(solution)/shard_map/all_to_all | solution.py:175
  106.1 5.3 %all-to-all-start.2 = ((bf16[16,80,512]{2,1,0:T(8,128)(2,1)}), bf16[16,80,512]{2,1,0:T(8,128)(2,1)S(1)}, u32[]{:S(2)}, u32[]{:S(2)}) async-start(bf16[16,80,512]{2,1,0:T(8,128)(2,1)} %bitcast.115), calls=%async_computation.2 | async-start | bytes 2621440 | tf_op jit(solution)/shard_map/all_to_all | solution.py:118
  111.4 0.3 convert_reduce_fusion.2
  111.7 0.2 fusion.20
  112.0 0.1 convolution_convert_fusion.10
  112.2 0.1 fusion.40
  112.3 18.0 %all-to-all-done.2 = bf16[16,80,512]{2,1,0:T(8,128)(2,1)S(1)} async-done(((bf16[16,80,512]{2,1,0:T(8,128)(2,1)}), bf16[16,80,512]{2,1,0:T(8,128)(2,1)S(1)}, u32[]{:S(2)}, u32[]{:S(2)}) %all-to-all-start.2) | async-done | bytes 1310752 | tf_op jit(solution)/shard_map/all_to_all | solution.py:118
  130.3 0.5 slice.17
  131.5 0.6 broadcast_in_dim.15
  132.1 3.8 %all-to-all-start.3 = ((f32[16,1,592]{2,1,0:T(1,128)}), f32[16,1,592]{2,1,0:T(1,128)S(1)}, u32[]{:S(2)}, u32[]{:S(2)}) async-start(f32[16,1,592]{2,1,0:T(1,128)} %broadcast_in_dim.15), calls=%async_computation.3 | async-start | bytes 81920 | tf_op jit(solution)/shard_map/all_to_all | solution.py:67
  136.0 7.7 %all-to-all-done.3 = f32[16,1,592]{2,1,0:T(1,128)S(1)} async-done(((f32[16,1,592]{2,1,0:T(1,128)}), f32[16,1,592]{2,1,0:T(1,128)S(1)}, u32[]{:S(2)}, u32[]{:S(2)}) %all-to-all-start.3) | async-done | bytes 37920 | tf_op jit(solution)/shard_map/all_to_all | solution.py:67
  143.9 0.1 reshape.224
  144.0 0.6 copy.98
  144.6 3.7 %all-to-all-start.4 = ((bf16[16,16,80]{2,1,0:T(8,128)(2,1)}), bf16[16,16,80]{2,1,0:T(8,128)(2,1)S(1)}, u32[]{:S(2)}, u32[]{:S(2)}) async-start(bf16[16,16,80]{2,1,0:T(8,128)(2,1)} %bitcast.116), calls=%async_computation.4 | async-start | bytes 131072 | tf_op jit(solution)/shard_map/all_to_all | solution.py:182
  148.4 7.5 %all-to-all-done.4 = bf16[16,16,80]{2,1,0:T(8,128)(2,1)S(1)} async-done(((bf16[16,16,80]{2,1,0:T(8,128)(2,1)}), bf16[16,16,80]{2,1,0:T(8,128)(2,1)S(1)}, u32[]{:S(2)}, u32[]{:S(2)}) %all-to-all-start.4) | async-done | bytes 40992 | tf_op jit(solution)/shard_map/all_to_all | solution.py:182
  155.8 0.2 reshape.232
  156.0 0.2 convolution_convert_fusion.2
  156.2 0.8 copy.69
  157.0 5.0 %all-to-all-start.5 = ((bf16[8,2,5120]{2,1,0:T(2,128)(2,1)}), bf16[8,2,5120]{2,1,0:T(2,128)(2,1)S(1)}, u32[]{:S(2)}, u32[]{:S(2)}) async-start(bf16[8,2,5120]{2,1,0:T(2,128)(2,1)} %copy.69), calls=%async_computation.5 | async-start | bytes 327680 | tf_op jit(solution)/shard_map/all_to_all | solution.py:191
  162.1 0.5 collective-permute-start
  162.6 5.8 %all-to-all-done.5 = bf16[8,2,5120]{2,1,0:T(2,128)(2,1)S(1)} async-done(((bf16[8,2,5120]{2,1,0:T(2,128)(2,1)}), bf16[8,2,5120]{2,1,0:T(2,128)(2,1)S(1)}, u32[]{:S(2)}, u32[]{:S(2)}) %all-to-all-start.5) | async-done | bytes 163872 | tf_op jit(solution)/shard_map/all_to_all | solution.py:191
  168.5 0.3 fusion.2
  168.7 0.2 broadcast_in_dim.16
  168.9 0.1 copy.71
  169.1 1.2 broadcast_in_dim.17
  170.2 4.4 %all-to-all-start.6 = ((bf16[16,512,80]{1,2,0:T(8,128)(2,1)}), bf16[16,512,80]{1,2,0:T(8,128)(2,1)}, u32[]{:S(2)}, u32[]{:S(2)}) async-start(bf16[16,512,80]{1,2,0:T(8,128)(2,1)} %broadcast_in_dim.17), calls=%async_computation.6 | async-start | bytes 2621440 | tf_op jit(solution)/shard_map/all_to_all | solution.py:67
  174.8 20.7 %all-to-all-done.6 = bf16[16,512,80]{1,2,0:T(8,128)(2,1)} async-done(((bf16[16,512,80]{1,2,0:T(8,128)(2,1)}), bf16[16,512,80]{1,2,0:T(8,128)(2,1)}, u32[]{:S(2)}, u32[]{:S(2)}) %all-to-all-start.6) | async-done | bytes 1310752 | tf_op jit(solution)/shard_map/all_to_all | solution.py:67
  195.5 6.4 %reduce-precision_reduce_fusion = bf16[512,2,512]{2,0,1:T(8,128)(2,1)S(1)} fusion(bf16[16,1,80,512]{3,2,1,0:T(8,128)(2,1)} %bitcast.26, bf16[16,1,80,512]{3,2,1,0:T(8,128)(2,1)S(1)} %bitcast.128, bf16[16,512,80]{1,2,0:T(8,128)(2,1)} %all-to-all-done.6), kind=kOutput, calls=%fused_computation | convolution fusion | flops 1363673088 | bytes 4980736 | tf_op jit(solution)/shard_map/brk,bskc->brsc/dot_general | solution.py:196
  201.9 0.3 convert_element_type.182
  202.1 0.4 constant_dynamic-slice_fusion.1
  202.6 0.1 copy.74
  202.7 1.2 multiply_convert_fusion
  203.9 0.2 copy.80
  204.1 0.9 fusion.7
  205.1 1.0 fusion.16
  206.1 0.2 slice-done
  206.3 1.5 slice-done.1
  207.8 6.9 %fusion.1 = bf16[8192,512]{0,1:T(8,128)(2,1)} fusion(bf16[512,512]{1,0:T(8,128)(2,1)S(1)} %bitcast.129, bf16[512,8192]{1,0:T(8,128)(2,1)S(1)} %bitcast.120), kind=kOutput, calls=%fused_computation.4 | convolution fusion | flops 4299161600 | bytes 17301504 | tf_op jit(solution)/shard_map/dot_general | solution.py:217
  215.5 81.4 %reduce-scatter.5.cloned.1.call-done = bf16[512,512]{0,1:T(8,128)(2,1)} async-done(((bf16[8192,512]{0,1:T(8,128)(2,1)}), bf16[512,512]{0,1:T(8,128)(2,1)}) %reduce-scatter.5.cloned.1.call-update) | async-done | bytes 524304 | tf_op jit(solution)/shard_map/reduce_scatter | solution.py:216
  296.9 2.2 convert_add_fusion
  (67 shorter events, 0.7 us)
Async XLA Ops:
  6.5 74.5 %copy-start = (bf16[96,1280]{1,0:T(8,128)(2,1)S(1)}, bf16[96,1280]{1,0:T(8,128)(2,1)}, u32[]{:S(2)}) copy-start(bf16[96,1280]{1,0:T(8,128)(2,1)} %param.32) | copy-start | bytes 737284
  6.5 196.2 %reduce-scatter.3.cloned.1.call-start = ((), (), s32[]{:S(2)}) async-start(), calls=%async_computation.9 | async-start | bytes 8912896 | tf_op jit(solution)/shard_map/reduce_scatter | solution.py:129
  17.9 0.9 copy-start.8
  20.7 8.2 %copy-start.4 = (bf16[64,1280]{1,0:T(8,128)(2,1)S(1)}, bf16[64,1280]{1,0:T(8,128)(2,1)}, u32[]{:S(2)}) copy-start(bf16[64,1280]{1,0:T(8,128)(2,1)} %param.26) | copy-start | bytes 491524
  20.7 8.4 %copy-start.6 = (bf16[1280,96]{0,1:T(8,128)(2,1)S(1)}, bf16[1280,96]{0,1:T(8,128)(2,1)}, u32[]{:S(2)}) copy-start(bf16[1280,96]{0,1:T(8,128)(2,1)} %param.30) | copy-start | bytes 737284
  20.7 10.1 %copy-start.7 = (bf16[1280,96]{0,1:T(8,128)(2,1)S(1)}, bf16[1280,96]{0,1:T(8,128)(2,1)}, u32[]{:S(2)}) copy-start(bf16[1280,96]{0,1:T(8,128)(2,1)} %param.31) | copy-start | bytes 737284
  20.7 12.4 %copy-start.10 = (s32[8,8]{1,0:T(8,128)S(1)}, s32[8,8]{1,0:T(8,128)}, u32[]{:S(2)}) copy-start(s32[8,8]{1,0:T(8,128)} %param.24) | copy-start | bytes 772
  20.7 50.9 %all-to-all-start = ((bf16[16,4,256,80]{2,3,1,0:T(8,128)(2,1)}), bf16[16,4,256,80]{2,3,1,0:T(8,128)(2,1)S(1)}, u32[]{:S(2)}, u32[]{:S(2)}) async-start(bf16[16,4,256,80]{2,3,1,0:T(8,128)(2,1)} %broadcast_in_dim.12), calls=%async_computation | async-start | bytes 5242880 | tf_op jit(solution)/shard_map/all_to_all | solution.py:67
  29.0 1.7 copy-start.16
  29.0 1.7 copy-start.17
  71.6 0.7 copy-start.11
  73.1 1.6 copy-start.2
  74.7 1.2 copy-start.9
  78.3 2.4 copy-start.18
  82.2 23.9 %all-to-all-start.1 = ((bf16[16,16,1280]{2,1,0:T(8,128)(2,1)}), bf16[16,16,1280]{2,1,0:T(8,128)(2,1)S(1)}, u32[]{:S(2)}, u32[]{:S(2)}) async-start(bf16[16,16,1280]{2,1,0:T(8,128)(2,1)} %bitcast.123), calls=%async_computation.1 | async-start | bytes 1310720 | tf_op jit(solution)/shard_map/all_to_all | solution.py:175
  93.6 18.1 %copy-start.3 = (bf16[512,512]{1,0:T(8,128)(2,1)S(1)}, bf16[512,512]{1,0:T(8,128)(2,1)}, u32[]{:S(2)}) copy-start(bf16[512,512]{1,0:T(8,128)(2,1)} %param.19) | copy-start | bytes 1572868
  93.6 18.3 %copy-start.12 = (s32[8,8]{1,0:T(8,128)S(1)}, s32[8,8]{1,0:T(8,128)}, u32[]{:S(2)}) copy-start(s32[8,8]{1,0:T(8,128)} %get-tuple-element.14) | copy-start | bytes 772
  95.5 16.7 %copy-start.5 = (bf16[64,1280]{1,0:T(8,128)(2,1)S(1)}, bf16[64,1280]{1,0:T(8,128)(2,1)}, u32[]{:S(2)}) copy-start(bf16[64,1280]{1,0:T(8,128)(2,1)} %param.26) | copy-start | bytes 491524
  95.5 35.9 %copy-start.15 = (f32[80]{0:T(128)S(1)}, f32[80]{0:T(128)}, u32[]{:S(2)}) copy-start(f32[80]{0:T(128)} %param.33) | copy-start | bytes 964
  106.1 24.2 %all-to-all-start.2 = ((bf16[16,80,512]{2,1,0:T(8,128)(2,1)}), bf16[16,80,512]{2,1,0:T(8,128)(2,1)S(1)}, u32[]{:S(2)}, u32[]{:S(2)}) async-start(bf16[16,80,512]{2,1,0:T(8,128)(2,1)} %bitcast.115), calls=%async_computation.2 | async-start | bytes 2621440 | tf_op jit(solution)/shard_map/all_to_all | solution.py:118
  132.1 11.6 %all-to-all-start.3 = ((f32[16,1,592]{2,1,0:T(1,128)}), f32[16,1,592]{2,1,0:T(1,128)S(1)}, u32[]{:S(2)}, u32[]{:S(2)}) async-start(f32[16,1,592]{2,1,0:T(1,128)} %broadcast_in_dim.15), calls=%async_computation.3 | async-start | bytes 81920 | tf_op jit(solution)/shard_map/all_to_all | solution.py:67
  144.6 11.2 %all-to-all-start.4 = ((bf16[16,16,80]{2,1,0:T(8,128)(2,1)}), bf16[16,16,80]{2,1,0:T(8,128)(2,1)S(1)}, u32[]{:S(2)}, u32[]{:S(2)}) async-start(bf16[16,16,80]{2,1,0:T(8,128)(2,1)} %bitcast.116), calls=%async_computation.4 | async-start | bytes 131072 | tf_op jit(solution)/shard_map/all_to_all | solution.py:182
  156.2 18.5 %copy-start.13 = (s32[1,512]{1,0:T(1,128)S(1)}, s32[1,512]{1,0:T(1,128)}, u32[]{:S(2)}) copy-start(s32[1,512]{1,0:T(1,128)} %param.23) | copy-start | bytes 6148
  157.0 11.5 %all-to-all-start.5 = ((bf16[8,2,5120]{2,1,0:T(2,128)(2,1)}), bf16[8,2,5120]{2,1,0:T(2,128)(2,1)S(1)}, u32[]{:S(2)}, u32[]{:S(2)}) async-start(bf16[8,2,5120]{2,1,0:T(2,128)(2,1)} %copy.69), calls=%async_computation.5 | async-start | bytes 327680 | tf_op jit(solution)/shard_map/all_to_all | solution.py:191
  162.1 12.7 %collective-permute-start = (bf16[16,80,512]{2,1,0:T(8,128)(2,1)S(1)}, bf16[16,80,512]{2,1,0:T(8,128)(2,1)}, u32[]{:S(2)}, u32[]{:S(2)}) collective-permute-start(bf16[16,80,512]{2,1,0:T(8,128)(2,1)S(1)} %all-to-all-done.2), channel_id=1, source_target_pairs={{0,16},{16,0},{32,48},{48,32},{64,80},{80,64},{96,112},{112,96},{1... | collective-permute-start | bytes 3932168 | tf_op jit(solution)/shard_map/ppermute | solution.py:120
  170.2 25.3 %all-to-all-start.6 = ((bf16[16,512,80]{1,2,0:T(8,128)(2,1)}), bf16[16,512,80]{1,2,0:T(8,128)(2,1)}, u32[]{:S(2)}, u32[]{:S(2)}) async-start(bf16[16,512,80]{1,2,0:T(8,128)(2,1)} %broadcast_in_dim.17), calls=%async_computation.6 | async-start | bytes 2621440 | tf_op jit(solution)/shard_map/all_to_all | solution.py:67
  174.6 122.3 %reduce-scatter.5.cloned.1.call-start = ((), (), s32[]{:S(2)}) async-start(), calls=%async_computation.10 | async-start | bytes 8912896 | tf_op jit(solution)/shard_map/reduce_scatter | solution.py:216
  204.1 2.2 slice-start
  205.0 2.8 slice-start.1
  214.7 0.7 copy-start.14
  214.7 84.4 %copy-start.1 = (bf16[96,1280]{1,0:T(8,128)(2,1)S(1)}, bf16[96,1280]{1,0:T(8,128)(2,1)}, u32[]{:S(2)}) copy-start(bf16[96,1280]{1,0:T(8,128)(2,1)} %param.32) | copy-start | bytes 737284
Sparse Core Ops, SparseCore 0:
  18.1 131.5 reduce-scatter.2
  214.8 82.0 reduce-scatter.4

commit v8 on v6

--- a/solution.py
+++ b/solution.py
@@ -119,7 +119,7 @@
     kv_weights = jnp.stack([my_kind, other_kind], 1)
     text_f = text_states.astype(jnp.float32)
     gained = (text_f * text_gain).astype(jnp.bfloat16)
-    after_weights = my_kind[0, 0, 0].astype(jnp.float32) * 0.0
+    after_weights = other_kind[0, 0, 0].astype(jnp.float32) * 0.0
     stats = jnp.concatenate([jnp.sum(text_f * text_f, -1), final_gain], 0) + after_weights
     stats = gather_blocks(stats, "fsdp", parts)
     squares = jnp.sum(stats[:, :token_count], 0)

time: 273 us -> 274 us (level)
  blocking collectives: 0 us -> 28 us
  waiting for transfers between devices: 164 us -> 146 us
  starting transfers between devices: 32.4 us -> 22.7 us
    all_to_all x0 -> x1, blocking collectives: none -> 28 us  [local(): lax.all_to_all(my_kind, 'fsdp', split_axis=0, concat_axis=0, tiled=True)]
    all_to_all x1 -> x0, waiting for transfers between devices: 17.5 us -> none  [local(): lax.all_to_all(my_kind, 'fsdp', split_axis=0, concat_axis=0, tiled=True)]
    all_to_all x1 -> x0, starting transfers between devices: 8.02 us -> none  [local(): lax.all_to_all(my_kind, 'fsdp', split_axis=0, concat_axis=0, tiled=True)]
  transfers between devices with their start and end apart: 10 -> 9, of which waited for: 8 -> 7; matrix products, arithmetic and copies ran while one was open for 16% -> 16% of each run, Pallas kernels for 0% -> 0%
where the time goes in v8:
time: 274 us; the launch traced here: 273 us
  waiting for transfers between devices  146 us (53%)
  matrix products  37.8 us (14%)
  blocking collectives  28 us (10%)
  starting transfers between devices  22.7 us (8%)
  between operations  15 us (5%)
  local copies, waits for them, and re-layouts  14.4 us (5%)
  other arithmetic  8.6 us (3%)
    reduce_scatter x1, waiting for transfers between devices, local(): lax.psum_scatter(lax.dot_general(cross_out, attended, (((0,), (0,)), ((),...  85 us
    all_to_all x1, blocking collectives, local(): lax.all_to_all(my_kind, 'fsdp', split_axis=0, concat_axis=0, tiled=True)  28 us
    all_to_all x2, waiting for transfers between devices, gather_blocks(): lax.all_to_all(spread, axis_name, split_axis=0, concat_axis=0, tiled=True)  20.8 us
    all_to_all x1, waiting for transfers between devices, local(): lax.all_to_all(head_part.reshape(parts, row_part, vis_width), 'fsdp', spl...  15.8 us
    dot_general x1, matrix products, local(): lax.dot_general(cross_query, gained, contract_first, preferred_element_ty...  11.3 us
    all_to_all x2, starting transfers between devices, gather_blocks(): lax.all_to_all(spread, axis_name, split_axis=0, concat_axis=0, tiled=True)  8.53 us
    all_to_all x1, waiting for transfers between devices, local(): lax.all_to_all(jnp.transpose(resampled_rows.reshape(row_part, parts, feat...  7.75 us
    reduce_scatter x1, waiting for transfers between devices, local(): lax.psum_scatter(lax.dot_general(cross_query, gained, contract_first, pre...  7.12 us
  transfers between devices with their start and end apart: 9, of which 7 were waited for; matrix products, arithmetic and copies ran while one was open for 16% of the time, Pallas kernels for 0%

profile of v8, /device:TPU:0, one launch (start us, length us, event | category | flops | bytes accessed | tf_op | source)
XLA Modules:
  0.0 272.8 jit_solution(13779959871654608227)
XLA Ops:
  6.5 0.7 all-gather.2.cloned.1.call-update
  7.3 11.3 %fusion = bf16[8192,512]{0,1:T(8,128)(2,1)} fusion(bf16[512,8192]{1,0:T(8,128)(2,1)} %param.34, bf16[512,512]{1,0:T(8,128)(2,1)} %param.19, f32[512]{0:T(512)} %param.20), kind=kOutput, calls=%fused_computation.3 | convolution fusion | flops 4299948032 | bytes 17303552 | tf_op jit(solution)/shard_map/dot_general | solution.py:128
  18.7 1.3 copy-done.3
  19.9 0.4 copy-done.4
  20.3 0.5 fusion.13
  20.9 0.5 copy.78
  21.4 0.7 copy.90
  22.1 28.0 %all_to_all.34 = bf16[16,80,512]{2,1,0:T(8,128)(2,1)S(1)} all-to-all(bf16[16,80,512]{2,1,0:T(8,128)(2,1)S(1)} %bitcast.105), channel_id=1, replica_groups=mesh['img'=8,'fsdp'=16] {'fsdp'}, dimensions={0} | all-to-all | bytes 2621440 | tf_op jit(solution)/shard_map/all_to_all | solution.py:116
  50.1 0.1 convert_reduce_fusion.2
  50.3 0.3 convolution_convert_fusion.8
  50.6 0.7 copy.61
  51.3 0.2 convolution_convert_fusion.9
  51.6 0.7 copy.59
  52.3 0.2 fusion.19
  52.5 0.6 compare_convert_fusion
  53.1 0.6 add_select_fusion.1
  53.7 1.3 slice.12
  55.7 0.6 broadcast_in_dim.12
  56.3 4.1 %all-to-all-start.2 = ((f32[16,1,592]{2,1,0:T(1,128)}), f32[16,1,592]{2,1,0:T(1,128)}, u32[]{:S(2)}, u32[]{:S(2)}) async-start(f32[16,1,592]{2,1,0:T(1,128)} %broadcast_in_dim.12), calls=%async_computation.2 | async-start | bytes 81920 | tf_op jit(solution)/shard_map/all_to_all | solution.py:67
  60.4 2.7 all-gather.2.cloned.1.call-done
  63.2 2.4 convert_reduce_fusion
  65.7 0.6 copy-done.13
  66.2 3.6 %convolution_convert_fusion.4 = bf16[4,256,96]{1,2,0:T(8,128)(2,1)} fusion(bf16[4,256,1280]{1,2,0:T(8,128)(2,1)} %all-gather.2.cloned.1.call-done, f32[1280]{0:T(1024)} %param.27, f32[4,256]{1,0:T(4,128)S(1)} %get-tuple-element.16, f32[4,256]{1,0:T(4,128)S(1)} %get-tuple-element.15, bf16[1280,96]{0,1:T(8,128)(2,1)} %param.30), kind=kOutput, calls=%fused_computation.37 | convolution fusion | flops 258310144 | bytes 3077120 | tf_op jit(solution)/shard_map/npv,vk->npk/dot_general | solution.py:142
  69.9 0.6 broadcast_in_dim.11
  70.5 3.0 %fusion.65 = (f32[4,64]{1,0:T(4,128)}, f32[4,1,64,320]{3,2,0,1:T(8,128)}) fusion(bf16[4,64,96]{1,2,0:T(8,128)(2,1)} %broadcast_in_dim.11, bf16[4,256,96]{1,2,0:T(8,128)(2,1)} %convolution_convert_fusion.4, bf16[1280,96]{0,1:T(8,128)(2,1)} %param.29, bf16[64,1280]{1,0:T(8,128)(2,1)S(1)} %copy-done.7, f32[1280]{0:T(1024)} %param.28, f32[64]{0:T(128)} %copy-done.20, ...), kind=kOutput, calls=%fused_computation.122 | convolution fusion | flops 32528128 | bytes 989696 | tf_op jit(solution)/shard_map/rhe,nkhe->nhrk/dot_general | solution.py:159
  73.5 2.0 convolution_convert_fusion.5
  75.6 0.3 convolution_convert_fusion.6
  76.0 1.2 convolution_convert_fusion.3
  77.1 4.9 %all-to-all-start = ((bf16[16,16,1280]{2,1,0:T(8,128)(2,1)}), bf16[16,16,1280]{2,1,0:T(8,128)(2,1)S(1)}, u32[]{:S(2)}, u32[]{:S(2)}) async-start(bf16[16,16,1280]{2,1,0:T(8,128)(2,1)} %bitcast.12), calls=%async_computation | async-start | bytes 1310720 | tf_op jit(solution)/shard_map/all_to_all | solution.py:171
  82.1 0.3 convert_reduce_fusion.3
  82.4 0.1 convolution_convert_fusion.10
  82.5 0.8 copy.92
  83.4 15.8 %all-to-all-done = bf16[16,16,1280]{2,1,0:T(8,128)(2,1)S(1)} async-done(((bf16[16,16,1280]{2,1,0:T(8,128)(2,1)}), bf16[16,16,1280]{2,1,0:T(8,128)(2,1)S(1)}, u32[]{:S(2)}, u32[]{:S(2)}) %all-to-all-start) | async-done | bytes 655392 | tf_op jit(solution)/shard_map/all_to_all | solution.py:171
  99.2 0.1 convert_reduce_fusion.1
  99.3 0.1 fusion.41
  99.6 0.1 reshape.219
  99.7 0.6 copy.91
  100.3 4.7 %all-to-all-start.3 = ((bf16[16,16,80]{2,1,0:T(8,128)(2,1)}), bf16[16,16,80]{2,1,0:T(8,128)(2,1)S(1)}, u32[]{:S(2)}, u32[]{:S(2)}) async-start(bf16[16,16,80]{2,1,0:T(8,128)(2,1)} %bitcast.99), calls=%async_computation.3 | async-start | bytes 131072 | tf_op jit(solution)/shard_map/all_to_all | solution.py:178
  105.0 7.7 %all-to-all-done.3 = bf16[16,16,80]{2,1,0:T(8,128)(2,1)S(1)} async-done(((bf16[16,16,80]{2,1,0:T(8,128)(2,1)}), bf16[16,16,80]{2,1,0:T(8,128)(2,1)S(1)}, u32[]{:S(2)}, u32[]{:S(2)}) %all-to-all-start.3) | async-done | bytes 40992 | tf_op jit(solution)/shard_map/all_to_all | solution.py:178
  112.8 0.2 reshape.226
  112.9 0.2 convolution_convert_fusion.2
  113.1 0.8 copy.65
  114.0 4.5 %all-to-all-start.4 = ((bf16[8,2,5120]{2,1,0:T(2,128)(2,1)}), bf16[8,2,5120]{2,1,0:T(2,128)(2,1)S(1)}, u32[]{:S(2)}, u32[]{:S(2)}) async-start(bf16[8,2,5120]{2,1,0:T(2,128)(2,1)} %copy.65), calls=%async_computation.4 | async-start | bytes 327680 | tf_op jit(solution)/shard_map/all_to_all | solution.py:187
  118.5 6.4 %all-to-all-done.4 = bf16[8,2,5120]{2,1,0:T(2,128)(2,1)S(1)} async-done(((bf16[8,2,5120]{2,1,0:T(2,128)(2,1)}), bf16[8,2,5120]{2,1,0:T(2,128)(2,1)S(1)}, u32[]{:S(2)}, u32[]{:S(2)}) %all-to-all-start.4) | async-done | bytes 163872 | tf_op jit(solution)/shard_map/all_to_all | solution.py:187
  124.9 0.3 fusion.2
  125.2 0.2 broadcast_in_dim.13
  125.4 0.1 copy.67
  125.5 1.2 broadcast_in_dim.14
  126.7 4.4 %all-to-all-start.5 = ((bf16[16,512,80]{1,2,0:T(8,128)(2,1)}), bf16[16,512,80]{1,2,0:T(8,128)(2,1)}, u32[]{:S(2)}, u32[]{:S(2)}) async-start(bf16[16,512,80]{1,2,0:T(8,128)(2,1)} %broadcast_in_dim.14), calls=%async_computation.5 | async-start | bytes 2621440 | tf_op jit(solution)/shard_map/all_to_all | solution.py:67
  131.2 20.8 %all-to-all-done.5 = bf16[16,512,80]{1,2,0:T(8,128)(2,1)} async-done(((bf16[16,512,80]{1,2,0:T(8,128)(2,1)}), bf16[16,512,80]{1,2,0:T(8,128)(2,1)}, u32[]{:S(2)}, u32[]{:S(2)}) %all-to-all-start.5) | async-done | bytes 1310752 | tf_op jit(solution)/shard_map/all_to_all | solution.py:67
  151.9 6.4 %reduce-precision_reduce_fusion = bf16[512,2,512]{2,0,1:T(8,128)(2,1)S(1)} fusion(bf16[16,1,80,512]{3,2,1,0:T(8,128)(2,1)} %bitcast.23, bf16[16,1,80,512]{3,2,1,0:T(8,128)(2,1)S(1)} %bitcast.111, bf16[16,512,80]{1,2,0:T(8,128)(2,1)} %all-to-all-done.5), kind=kOutput, calls=%fused_computation | convolution fusion | flops 1363673088 | bytes 4980736 | tf_op jit(solution)/shard_map/brk,bskc->brsc/dot_general | solution.py:192
  158.3 0.3 convert_element_type.168
  158.6 0.4 constant_dynamic-slice_fusion.1
  159.0 0.1 copy.70
  159.1 7.1 %reduce-scatter.3.cloned.1.call-done = bf16[512,512]{0,1:T(8,128)(2,1)} async-done(((bf16[8192,512]{0,1:T(8,128)(2,1)}), bf16[512,512]{0,1:T(8,128)(2,1)}) %reduce-scatter.3.cloned.1.call-update) | async-done | bytes 524304 | tf_op jit(solution)/shard_map/reduce_scatter | solution.py:127
  166.2 1.2 multiply_convert_fusion
  167.5 0.2 copy.76
  167.7 0.9 fusion.7
  168.6 1.0 fusion.15
  169.6 0.2 slice-done
  169.9 1.5 slice-done.1
  171.4 7.0 %fusion.1 = bf16[8192,512]{0,1:T(8,128)(2,1)} fusion(bf16[512,512]{1,0:T(8,128)(2,1)S(1)} %bitcast.112, bf16[512,8192]{1,0:T(8,128)(2,1)S(1)} %bitcast.103), kind=kOutput, calls=%fused_computation.4 | convolution fusion | flops 4299161600 | bytes 17301504 | tf_op jit(solution)/shard_map/dot_general | solution.py:213
  179.0 85.0 %reduce-scatter.5.cloned.1.call-done = bf16[512,512]{0,1:T(8,128)(2,1)} async-done(((bf16[8192,512]{0,1:T(8,128)(2,1)}), bf16[512,512]{0,1:T(8,128)(2,1)}) %reduce-scatter.5.cloned.1.call-update) | async-done | bytes 524304 | tf_op jit(solution)/shard_map/reduce_scatter | solution.py:212
  264.1 2.2 convert_add_fusion
  (78 shorter events, 0.6 us)
Async XLA Ops:
  6.5 69.4 %copy-start = (bf16[96,1280]{1,0:T(8,128)(2,1)S(1)}, bf16[96,1280]{1,0:T(8,128)(2,1)}, u32[]{:S(2)}) copy-start(bf16[96,1280]{1,0:T(8,128)(2,1)} %param.32) | copy-start | bytes 737284
  6.5 56.6 %all-gather.2.cloned.1.call-start = ((), (), s32[]{:S(2)}) async-start(), calls=%async_computation.8 | async-start | bytes 2785280 | tf_op jit(solution)/shard_map/all_gather | solution.py:135
  7.3 159.0 %reduce-scatter.3.cloned.1.call-start = ((), (), s32[]{:S(2)}) async-start(), calls=%async_computation.9 | async-start | bytes 8912896 | tf_op jit(solution)/shard_map/reduce_scatter | solution.py:127
  18.6 1.3 copy-start.3
  18.6 1.7 copy-start.4
  20.8 29.3 %copy-start.7 = (bf16[64,1280]{1,0:T(8,128)(2,1)S(1)}, bf16[64,1280]{1,0:T(8,128)(2,1)}, u32[]{:S(2)}) copy-start(bf16[64,1280]{1,0:T(8,128)(2,1)} %param.26) | copy-start | bytes 491524
  20.8 29.5 %copy-start.21 = (bf16[1280,96]{0,1:T(8,128)(2,1)S(1)}, bf16[1280,96]{0,1:T(8,128)(2,1)}, u32[]{:S(2)}) copy-start(bf16[1280,96]{0,1:T(8,128)(2,1)} %param.30) | copy-start | bytes 737284
  20.8 29.5 %copy-start.23 = (f32[1280]{0:T(1024)S(1)}, f32[1280]{0:T(1024)}, u32[]{:S(2)}) copy-start(f32[1280]{0:T(1024)} %param.28) | copy-start | bytes 15364
  20.9 30.5 %copy-start.22 = (bf16[1280,96]{0,1:T(8,128)(2,1)S(1)}, bf16[1280,96]{0,1:T(8,128)(2,1)}, u32[]{:S(2)}) copy-start(bf16[1280,96]{0,1:T(8,128)(2,1)} %param.31) | copy-start | bytes 737284
  20.9 31.4 %copy-start.2 = (bf16[512,512]{1,0:T(8,128)(2,1)S(1)}, bf16[512,512]{1,0:T(8,128)(2,1)}, u32[]{:S(2)}) copy-start(bf16[512,512]{1,0:T(8,128)(2,1)} %param.19) | copy-start | bytes 1572868
  21.3 31.1 %copy-start.11 = (s32[8,8]{1,0:T(8,128)S(1)}, s32[8,8]{1,0:T(8,128)}, u32[]{:S(2)}) copy-start(s32[8,8]{1,0:T(8,128)} %param.24) | copy-start | bytes 772
  21.4 34.3 %copy-start.18 = (f32[80]{0:T(128)S(1)}, f32[80]{0:T(128)}, u32[]{:S(2)}) copy-start(f32[80]{0:T(128)} %param.33) | copy-start | bytes 964
  50.1 13.0 %copy-start.5 = (bf16[16,80,512]{2,1,0:T(8,128)(2,1)}, bf16[16,80,512]{2,1,0:T(8,128)(2,1)S(1)}, u32[]{:S(2)}) copy-start(bf16[16,80,512]{2,1,0:T(8,128)(2,1)S(1)} %all_to_all.34) | copy-start | bytes 3932164
  50.1 3.5 %collective-permute-start = (bf16[16,80,512]{2,1,0:T(8,128)(2,1)S(1)}, bf16[16,80,512]{2,1,0:T(8,128)(2,1)}, u32[]{:S(2)}, u32[]{:S(2)}) collective-permute-start(bf16[16,80,512]{2,1,0:T(8,128)(2,1)S(1)} %all_to_all.34), channel_id=1, source_target_pairs={{0,16},{16,0},{32,48},{48,32},{64,80},{80,64},{96,112},{112,96},{1... | collective-permute-start | bytes 3932168 | tf_op jit(solution)/shard_map/ppermute | solution.py:118
  50.3 12.9 %copy-start.19 = (f32[64]{0:T(128)}, f32[64]{0:T(128)S(1)}, u32[]{:S(2)}) copy-start(f32[64]{0:T(128)S(1)} %get-tuple-element.19) | copy-start | bytes 772
  50.3 12.8 %copy-start.20 = (f32[64]{0:T(128)}, f32[64]{0:T(128)S(1)}, u32[]{:S(2)}) copy-start(f32[64]{0:T(128)S(1)} %get-tuple-element.20) | copy-start | bytes 772
  56.3 20.8 %all-to-all-start.2 = ((f32[16,1,592]{2,1,0:T(1,128)}), f32[16,1,592]{2,1,0:T(1,128)}, u32[]{:S(2)}, u32[]{:S(2)}) async-start(f32[16,1,592]{2,1,0:T(1,128)} %broadcast_in_dim.12), calls=%async_computation.2 | async-start | bytes 81920 | tf_op jit(solution)/shard_map/all_to_all | solution.py:67
  63.2 6.7 %copy-start.9 = (bf16[64,96]{0,1:T(8,128)(2,1)S(1)}, bf16[64,96]{0,1:T(8,128)(2,1)}, u32[]{:S(2)}) copy-start(bf16[64,96]{0,1:T(8,128)(2,1)} %copy.61) | copy-start | bytes 36868
  65.6 7.9 %copy-start.1 = (bf16[4,256,1280]{1,2,0:T(8,128)(2,1)S(1)}, bf16[4,256,1280]{1,2,0:T(8,128)(2,1)}, u32[]{:S(2)}) copy-start(bf16[4,256,1280]{1,2,0:T(8,128)(2,1)} %all-gather.2.cloned.1.call-done) | copy-start | bytes 7864324
  65.6 0.6 copy-start.13
  65.6 4.2 %copy-start.14 = (f32[4,256]{1,0:T(4,128)}, f32[4,256]{1,0:T(4,128)S(1)}, u32[]{:S(2)}) copy-start(f32[4,256]{1,0:T(4,128)S(1)} %get-tuple-element.16) | copy-start | bytes 12292
  73.5 2.1 copy-start.8
  73.5 2.1 copy-start.24
  73.5 2.1 copy-start.25
  75.6 6.5 %copy-start.10 = (s32[8,8]{1,0:T(8,128)S(1)}, s32[8,8]{1,0:T(8,128)}, u32[]{:S(2)}) copy-start(s32[8,8]{1,0:T(8,128)} %get-tuple-element.13) | copy-start | bytes 772
  75.6 6.8 %copy-start.12 = (s32[8,8]{1,0:T(8,128)S(1)}, s32[8,8]{1,0:T(8,128)}, u32[]{:S(2)}) copy-start(s32[8,8]{1,0:T(8,128)} %get-tuple-element.14) | copy-start | bytes 772
  75.6 6.8 %copy-start.17 = (bf16[8,8]{1,0:T(8,128)(2,1)S(1)}, bf16[8,8]{1,0:T(8,128)(2,1)}, u32[]{:S(2)}) copy-start(bf16[8,8]{1,0:T(8,128)(2,1)} %compare_convert_fusion) | copy-start | bytes 388
  77.1 54.0 %copy-start.15 = (s32[1,512]{1,0:T(1,128)S(1)}, s32[1,512]{1,0:T(1,128)}, u32[]{:S(2)}) copy-start(s32[1,512]{1,0:T(1,128)} %param.23) | copy-start | bytes 6148
  77.1 74.8 %copy-start.6 = (bf16[16,80,512]{2,1,0:T(8,128)(2,1)S(1)}, bf16[16,80,512]{2,1,0:T(8,128)(2,1)}, u32[]{:S(2)}) copy-start(bf16[16,80,512]{2,1,0:T(8,128)(2,1)} %copy-done.5) | copy-start | bytes 3932164
  77.1 22.1 %all-to-all-start = ((bf16[16,16,1280]{2,1,0:T(8,128)(2,1)}), bf16[16,16,1280]{2,1,0:T(8,128)(2,1)S(1)}, u32[]{:S(2)}, u32[]{:S(2)}) async-start(bf16[16,16,1280]{2,1,0:T(8,128)(2,1)} %bitcast.12), calls=%async_computation | async-start | bytes 1310720 | tf_op jit(solution)/shard_map/all_to_all | solution.py:171
  100.3 12.5 %all-to-all-start.3 = ((bf16[16,16,80]{2,1,0:T(8,128)(2,1)}), bf16[16,16,80]{2,1,0:T(8,128)(2,1)S(1)}, u32[]{:S(2)}, u32[]{:S(2)}) async-start(bf16[16,16,80]{2,1,0:T(8,128)(2,1)} %bitcast.99), calls=%async_computation.3 | async-start | bytes 131072 | tf_op jit(solution)/shard_map/all_to_all | solution.py:178
  114.0 11.0 %all-to-all-start.4 = ((bf16[8,2,5120]{2,1,0:T(2,128)(2,1)}), bf16[8,2,5120]{2,1,0:T(2,128)(2,1)S(1)}, u32[]{:S(2)}, u32[]{:S(2)}) async-start(bf16[8,2,5120]{2,1,0:T(2,128)(2,1)} %copy.65), calls=%async_computation.4 | async-start | bytes 327680 | tf_op jit(solution)/shard_map/all_to_all | solution.py:187
  126.7 25.3 %all-to-all-start.5 = ((bf16[16,512,80]{1,2,0:T(8,128)(2,1)}), bf16[16,512,80]{1,2,0:T(8,128)(2,1)}, u32[]{:S(2)}, u32[]{:S(2)}) async-start(bf16[16,512,80]{1,2,0:T(8,128)(2,1)} %broadcast_in_dim.14), calls=%async_computation.5 | async-start | bytes 2621440 | tf_op jit(solution)/shard_map/all_to_all | solution.py:67
  131.1 133.0 %reduce-scatter.5.cloned.1.call-start = ((), (), s32[]{:S(2)}) async-start(), calls=%async_computation.10 | async-start | bytes 8912896 | tf_op jit(solution)/shard_map/reduce_scatter | solution.py:212
  167.7 2.2 slice-start
  168.6 2.8 %slice-start.1 = ((s8[8388608]{0:T(1024)(128)(4,1)}), s8[4194304]{0:T(1024)(128)(4,1)S(1)}, s32[]{:S(2)}) async-start(s8[8388608]{0:T(1024)(128)(4,1)} %bitcast.102), calls=%async_computation.12 | async-start | bytes 8388608
  178.3 0.7 copy-start.16
Sparse Core Ops, SparseCore 0:
  9.5 53.6 all-gather.1
  66.6 99.6 reduce-scatter.2
  178.5 85.5 reduce-scatter.4

commit v9 on v6

--- a/solution.py
+++ b/solution.py
@@ -194,12 +194,11 @@
     slot_kv = slot_kv.astype(jnp.bfloat16).reshape(slot_count, latent_count, 2, cross_heads, HEAD)
     slot_keys = lax.dynamic_index_in_dim(slot_kv, my_core, 2, keepdims=False)
     slot_values = lax.dynamic_index_in_dim(slot_kv, 1 - my_core, 2, keepdims=False)
-    token_scale = lax.rsqrt(squares / D + eps_rms)
-    query_cols = (query_cols.astype(jnp.float32) * token_scale[None, :]).astype(jnp.bfloat16)
+    token_scale = lax.rsqrt(squares / D + eps_rms) * HEAD ** (-0.5)
     query_heads = query_cols.reshape(cross_heads, HEAD, token_count)
     scores = jnp.einsum(
         "het,crhe->htcr", query_heads, slot_keys, preferred_element_type=jnp.float32
-    ) * HEAD ** (-0.5)
+    ) * token_scale[None, :, None, None]
     slot_hot = (token_slot[0][:, None] == jnp.arange(slot_count, dtype=jnp.int32)[None, :]).astype(
         jnp.float32
     )

time: 273 us -> 273 us (level)
  no operation moved by 1% of the time
where the time goes in v9:
time: 273 us; the launch traced here: 272 us
  waiting for transfers between devices  164 us (60%)
  matrix products  37.7 us (14%)
  starting transfers between devices  32.4 us (12%)
  local copies, waits for them, and re-layouts  15.8 us (6%)
  between operations  14.9 us (5%)
  other arithmetic  7.41 us (3%)
    reduce_scatter x1, waiting for transfers between devices, local(): lax.psum_scatter(lax.dot_general(cross_out, attended, (((0,), (0,)), ((),...  84.7 us
    all_to_all x2, waiting for transfers between devices, gather_blocks(): lax.all_to_all(spread, axis_name, split_axis=0, concat_axis=0, tiled=True)  20.8 us
    all_to_all x1, waiting for transfers between devices, local(): lax.all_to_all(my_kind, 'fsdp', split_axis=0, concat_axis=0, tiled=True)  17.5 us
    all_to_all x1, waiting for transfers between devices, local(): lax.all_to_all(head_part.reshape(parts, row_part, vis_width), 'fsdp', spl...  15.1 us
    dot_general x1, matrix products, local(): lax.dot_general(cross_query, gained, contract_first, preferred_element_ty...  11.3 us
    all_to_all x2, starting transfers between devices, gather_blocks(): lax.all_to_all(spread, axis_name, split_axis=0, concat_axis=0, tiled=True)  8.54 us
    all_to_all x1, starting transfers between devices, local(): lax.all_to_all(my_kind, 'fsdp', split_axis=0, concat_axis=0, tiled=True)  8.02 us
    all_to_all x1, waiting for transfers between devices, local(): lax.all_to_all(jnp.transpose(resampled_rows.reshape(row_part, parts, feat...  7.75 us
  transfers between devices with their start and end apart: 10, of which 8 were waited for; matrix products, arithmetic and copies ran while one was open for 16% of the time, Pallas kernels for 0%

profile of v9, /device:TPU:0, one launch (start us, length us, event | category | flops | bytes accessed | tf_op | source)
XLA Modules:
  0.0 271.8 jit_solution(2217666034777424624)
XLA Ops:
  6.5 0.7 all-gather.2.cloned.1.call-update
  7.3 11.3 %fusion = bf16[8192,512]{0,1:T(8,128)(2,1)} fusion(bf16[512,8192]{1,0:T(8,128)(2,1)} %param.34, bf16[512,512]{1,0:T(8,128)(2,1)} %param.19, f32[512]{0:T(512)} %param.20), kind=kOutput, calls=%fused_computation.3 | convolution fusion | flops 4299948032 | bytes 17303552 | tf_op jit(solution)/shard_map/dot_general | solution.py:128
  18.7 1.3 copy-done.3
  20.0 0.4 copy-done.4
  20.4 0.5 fusion.13
  20.9 0.5 copy.78
  21.4 1.8 copy.90
  23.2 8.0 %all-to-all-start.1 = ((bf16[16,80,512]{2,1,0:T(8,128)(2,1)}), bf16[16,80,512]{2,1,0:T(8,128)(2,1)S(1)}, u32[]{:S(2)}, u32[]{:S(2)}) async-start(bf16[16,80,512]{2,1,0:T(8,128)(2,1)} %bitcast.98), calls=%async_computation.1 | async-start | bytes 2621440 | tf_op jit(solution)/shard_map/all_to_all | solution.py:116
  31.2 0.1 convert_reduce_fusion.2
  31.4 0.3 convolution_convert_fusion.8
  31.7 0.7 copy.61
  32.4 0.2 convolution_convert_fusion.9
  32.6 0.7 copy.59
  33.3 0.2 fusion.19
  33.5 0.6 compare_convert_fusion
  34.1 0.6 add_select_fusion.1
  34.7 17.5 %all-to-all-done.1 = bf16[16,80,512]{2,1,0:T(8,128)(2,1)S(1)} async-done(((bf16[16,80,512]{2,1,0:T(8,128)(2,1)}), bf16[16,80,512]{2,1,0:T(8,128)(2,1)S(1)}, u32[]{:S(2)}, u32[]{:S(2)}) %all-to-all-start.1) | async-done | bytes 1310752 | tf_op jit(solution)/shard_map/all_to_all | solution.py:116
  52.2 0.5 slice.12
  53.4 0.6 broadcast_in_dim.12
  54.0 4.1 %all-to-all-start.2 = ((f32[16,1,592]{2,1,0:T(1,128)}), f32[16,1,592]{2,1,0:T(1,128)}, u32[]{:S(2)}, u32[]{:S(2)}) async-start(f32[16,1,592]{2,1,0:T(1,128)} %broadcast_in_dim.12), calls=%async_computation.2 | async-start | bytes 81920 | tf_op jit(solution)/shard_map/all_to_all | solution.py:67
  58.1 4.4 %all-gather.2.cloned.1.call-done = bf16[4,256,1280]{1,2,0:T(8,128)(2,1)} async-done(((bf16[4,256,80]{1,2,0:T(8,128)(2,1)}), bf16[4,256,1280]{1,2,0:T(8,128)(2,1)}) %all-gather.2.cloned.1.call-update) | async-done | bytes 2621456 | tf_op jit(solution)/shard_map/all_gather | solution.py:135
  62.5 2.4 convert_reduce_fusion
  65.0 0.6 copy-done.13
  65.6 3.6 %convolution_convert_fusion.4 = bf16[4,256,96]{1,2,0:T(8,128)(2,1)} fusion(bf16[4,256,1280]{1,2,0:T(8,128)(2,1)} %all-gather.2.cloned.1.call-done, f32[1280]{0:T(1024)} %param.27, f32[4,256]{1,0:T(4,128)S(1)} %get-tuple-element.16, f32[4,256]{1,0:T(4,128)S(1)} %get-tuple-element.15, bf16[1280,96]{0,1:T(8,128)(2,1)} %param.30), kind=kOutput, calls=%fused_computation.37 | convolution fusion | flops 258310144 | bytes 3077120 | tf_op jit(solution)/shard_map/npv,vk->npk/dot_general | solution.py:142
  69.2 0.6 broadcast_in_dim.11
  69.9 3.0 %fusion.64 = (f32[4,64]{1,0:T(4,128)}, f32[4,1,64,320]{3,2,0,1:T(8,128)}) fusion(bf16[4,64,96]{1,2,0:T(8,128)(2,1)} %broadcast_in_dim.11, bf16[4,256,96]{1,2,0:T(8,128)(2,1)} %convolution_convert_fusion.4, bf16[1280,96]{0,1:T(8,128)(2,1)} %param.29, bf16[64,1280]{1,0:T(8,128)(2,1)S(1)} %copy-done.7, f32[1280]{0:T(1024)} %param.28, f32[64]{0:T(128)} %copy-done.20, ...), kind=kOutput, calls=%fused_computation.120 | convolution fusion | flops 32528128 | bytes 989696 | tf_op jit(solution)/shard_map/rhe,nkhe->nhrk/dot_general | solution.py:159
  72.9 2.0 convolution_convert_fusion.5
  75.0 0.3 convolution_convert_fusion.6
  75.3 1.2 convolution_convert_fusion.3
  76.5 5.2 %all-to-all-start = ((bf16[16,16,1280]{2,1,0:T(8,128)(2,1)}), bf16[16,16,1280]{2,1,0:T(8,128)(2,1)S(1)}, u32[]{:S(2)}, u32[]{:S(2)}) async-start(bf16[16,16,1280]{2,1,0:T(8,128)(2,1)} %bitcast.12), calls=%async_computation | async-start | bytes 1310720 | tf_op jit(solution)/shard_map/all_to_all | solution.py:171
  81.7 0.3 convert_reduce_fusion.3
  82.0 0.1 convolution_convert_fusion.10
  82.2 0.8 copy.92
  83.0 15.1 %all-to-all-done = bf16[16,16,1280]{2,1,0:T(8,128)(2,1)S(1)} async-done(((bf16[16,16,1280]{2,1,0:T(8,128)(2,1)}), bf16[16,16,1280]{2,1,0:T(8,128)(2,1)S(1)}, u32[]{:S(2)}, u32[]{:S(2)}) %all-to-all-start) | async-done | bytes 655392 | tf_op jit(solution)/shard_map/all_to_all | solution.py:171
  98.2 0.1 fusion.41
  98.5 0.1 reshape.220
  98.6 0.6 copy.91
  99.3 5.8 %all-to-all-start.3 = ((bf16[16,16,80]{2,1,0:T(8,128)(2,1)}), bf16[16,16,80]{2,1,0:T(8,128)(2,1)S(1)}, u32[]{:S(2)}, u32[]{:S(2)}) async-start(bf16[16,16,80]{2,1,0:T(8,128)(2,1)} %bitcast.99), calls=%async_computation.3 | async-start | bytes 131072 | tf_op jit(solution)/shard_map/all_to_all | solution.py:178
  105.1 7.8 %all-to-all-done.3 = bf16[16,16,80]{2,1,0:T(8,128)(2,1)S(1)} async-done(((bf16[16,16,80]{2,1,0:T(8,128)(2,1)}), bf16[16,16,80]{2,1,0:T(8,128)(2,1)S(1)}, u32[]{:S(2)}, u32[]{:S(2)}) %all-to-all-start.3) | async-done | bytes 40992 | tf_op jit(solution)/shard_map/all_to_all | solution.py:178
  112.8 0.2 reshape.227
  113.0 0.2 convolution_convert_fusion.2
  113.1 0.8 copy.65
  114.0 4.3 %all-to-all-start.4 = ((bf16[8,2,5120]{2,1,0:T(2,128)(2,1)}), bf16[8,2,5120]{2,1,0:T(2,128)(2,1)S(1)}, u32[]{:S(2)}, u32[]{:S(2)}) async-start(bf16[8,2,5120]{2,1,0:T(2,128)(2,1)} %copy.65), calls=%async_computation.4 | async-start | bytes 327680 | tf_op jit(solution)/shard_map/all_to_all | solution.py:187
  118.4 0.5 collective-permute-start
  118.9 5.8 %all-to-all-done.4 = bf16[8,2,5120]{2,1,0:T(2,128)(2,1)S(1)} async-done(((bf16[8,2,5120]{2,1,0:T(2,128)(2,1)}), bf16[8,2,5120]{2,1,0:T(2,128)(2,1)S(1)}, u32[]{:S(2)}, u32[]{:S(2)}) %all-to-all-start.4) | async-done | bytes 163872 | tf_op jit(solution)/shard_map/all_to_all | solution.py:187
  124.7 0.3 fusion.2
  125.0 0.2 broadcast_in_dim.13
  125.2 0.1 copy.67
  125.3 1.2 broadcast_in_dim.14
  126.5 4.4 %all-to-all-start.5 = ((bf16[16,512,80]{1,2,0:T(8,128)(2,1)}), bf16[16,512,80]{1,2,0:T(8,128)(2,1)}, u32[]{:S(2)}, u32[]{:S(2)}) async-start(bf16[16,512,80]{1,2,0:T(8,128)(2,1)} %broadcast_in_dim.14), calls=%async_computation.5 | async-start | bytes 2621440 | tf_op jit(solution)/shard_map/all_to_all | solution.py:67
  131.0 20.8 %all-to-all-done.5 = bf16[16,512,80]{1,2,0:T(8,128)(2,1)} async-done(((bf16[16,512,80]{1,2,0:T(8,128)(2,1)}), bf16[16,512,80]{1,2,0:T(8,128)(2,1)}, u32[]{:S(2)}, u32[]{:S(2)}) %all-to-all-start.5) | async-done | bytes 1310752 | tf_op jit(solution)/shard_map/all_to_all | solution.py:67
  151.8 6.3 %reduce-precision_reduce_fusion = bf16[512,2,512]{2,0,1:T(8,128)(2,1)S(1)} fusion(bf16[16,1,80,512]{3,2,1,0:T(8,128)(2,1)} %bitcast.23, bf16[16,1,80,512]{3,2,1,0:T(8,128)(2,1)S(1)} %bitcast.110, bf16[16,512,80]{1,2,0:T(8,128)(2,1)} %all-to-all-done.5), kind=kOutput, calls=%fused_computation | convolution fusion | flops 1363673088 | bytes 4980736 | tf_op jit(solution)/shard_map/brk,bskc->brsc/dot_general | solution.py:192
  158.2 0.3 convert_element_type.162
  158.5 0.4 constant_dynamic-slice_fusion.1
  158.9 0.1 copy.70
  159.0 6.8 %reduce-scatter.3.cloned.1.call-done = bf16[512,512]{0,1:T(8,128)(2,1)} async-done(((bf16[8192,512]{0,1:T(8,128)(2,1)}), bf16[512,512]{0,1:T(8,128)(2,1)}) %reduce-scatter.3.cloned.1.call-update) | async-done | bytes 524304 | tf_op jit(solution)/shard_map/reduce_scatter | solution.py:127
  165.8 1.3 copy.76
  167.1 0.9 fusion.7
  168.0 1.0 fusion.15
  169.0 0.2 slice-done
  169.2 1.5 slice-done.1
  170.7 6.9 %fusion.1 = bf16[8192,512]{0,1:T(8,128)(2,1)} fusion(bf16[512,512]{1,0:T(8,128)(2,1)S(1)} %bitcast.111, bf16[512,8192]{1,0:T(8,128)(2,1)S(1)} %bitcast.103), kind=kOutput, calls=%fused_computation.4 | convolution fusion | flops 4299161600 | bytes 17301504 | tf_op jit(solution)/shard_map/dot_general | solution.py:212
  178.3 84.7 %reduce-scatter.5.cloned.1.call-done = bf16[512,512]{0,1:T(8,128)(2,1)} async-done(((bf16[8192,512]{0,1:T(8,128)(2,1)}), bf16[512,512]{0,1:T(8,128)(2,1)}) %reduce-scatter.5.cloned.1.call-update) | async-done | bytes 524304 | tf_op jit(solution)/shard_map/reduce_scatter | solution.py:211
  263.0 2.2 convert_add_fusion
  (78 shorter events, 0.7 us)
Async XLA Ops:
  6.5 68.8 %copy-start = (bf16[96,1280]{1,0:T(8,128)(2,1)S(1)}, bf16[96,1280]{1,0:T(8,128)(2,1)}, u32[]{:S(2)}) copy-start(bf16[96,1280]{1,0:T(8,128)(2,1)} %param.32) | copy-start | bytes 737284
  6.5 56.0 %all-gather.2.cloned.1.call-start = ((), (), s32[]{:S(2)}) async-start(), calls=%async_computation.8 | async-start | bytes 2785280 | tf_op jit(solution)/shard_map/all_gather | solution.py:135
  7.3 158.5 %reduce-scatter.3.cloned.1.call-start = ((), (), s32[]{:S(2)}) async-start(), calls=%async_computation.9 | async-start | bytes 8912896 | tf_op jit(solution)/shard_map/reduce_scatter | solution.py:127
  18.6 1.3 copy-start.3
  18.6 1.7 copy-start.4
  20.8 10.4 %copy-start.7 = (bf16[64,1280]{1,0:T(8,128)(2,1)S(1)}, bf16[64,1280]{1,0:T(8,128)(2,1)}, u32[]{:S(2)}) copy-start(bf16[64,1280]{1,0:T(8,128)(2,1)} %param.26) | copy-start | bytes 491524
  20.8 10.5 %copy-start.21 = (bf16[1280,96]{0,1:T(8,128)(2,1)S(1)}, bf16[1280,96]{0,1:T(8,128)(2,1)}, u32[]{:S(2)}) copy-start(bf16[1280,96]{0,1:T(8,128)(2,1)} %param.30) | copy-start | bytes 737284
  20.9 10.5 %copy-start.23 = (f32[1280]{0:T(1024)S(1)}, f32[1280]{0:T(1024)}, u32[]{:S(2)}) copy-start(f32[1280]{0:T(1024)} %param.28) | copy-start | bytes 15364
  20.9 11.5 %copy-start.22 = (bf16[1280,96]{0,1:T(8,128)(2,1)S(1)}, bf16[1280,96]{0,1:T(8,128)(2,1)}, u32[]{:S(2)}) copy-start(bf16[1280,96]{0,1:T(8,128)(2,1)} %param.31) | copy-start | bytes 737284
  20.9 12.5 %copy-start.2 = (bf16[512,512]{1,0:T(8,128)(2,1)S(1)}, bf16[512,512]{1,0:T(8,128)(2,1)}, u32[]{:S(2)}) copy-start(bf16[512,512]{1,0:T(8,128)(2,1)} %param.19) | copy-start | bytes 1572868
  21.4 12.2 %copy-start.11 = (s32[8,8]{1,0:T(8,128)S(1)}, s32[8,8]{1,0:T(8,128)}, u32[]{:S(2)}) copy-start(s32[8,8]{1,0:T(8,128)} %param.24) | copy-start | bytes 772
  21.4 32.0 %copy-start.18 = (f32[80]{0:T(128)S(1)}, f32[80]{0:T(128)}, u32[]{:S(2)}) copy-start(f32[80]{0:T(128)} %param.33) | copy-start | bytes 964
  23.2 29.1 %all-to-all-start.1 = ((bf16[16,80,512]{2,1,0:T(8,128)(2,1)}), bf16[16,80,512]{2,1,0:T(8,128)(2,1)S(1)}, u32[]{:S(2)}, u32[]{:S(2)}) async-start(bf16[16,80,512]{2,1,0:T(8,128)(2,1)} %bitcast.98), calls=%async_computation.1 | async-start | bytes 2621440 | tf_op jit(solution)/shard_map/all_to_all | solution.py:116
  31.4 31.2 %copy-start.19 = (f32[64]{0:T(128)}, f32[64]{0:T(128)S(1)}, u32[]{:S(2)}) copy-start(f32[64]{0:T(128)S(1)} %get-tuple-element.19) | copy-start | bytes 772
  31.4 31.1 %copy-start.20 = (f32[64]{0:T(128)}, f32[64]{0:T(128)S(1)}, u32[]{:S(2)}) copy-start(f32[64]{0:T(128)S(1)} %get-tuple-element.20) | copy-start | bytes 772
  52.2 10.3 %copy-start.5 = (bf16[16,80,512]{2,1,0:T(8,128)(2,1)}, bf16[16,80,512]{2,1,0:T(8,128)(2,1)S(1)}, u32[]{:S(2)}) copy-start(bf16[16,80,512]{2,1,0:T(8,128)(2,1)S(1)} %all-to-all-done.1) | copy-start | bytes 3932164
  54.0 22.5 %all-to-all-start.2 = ((f32[16,1,592]{2,1,0:T(1,128)}), f32[16,1,592]{2,1,0:T(1,128)}, u32[]{:S(2)}, u32[]{:S(2)}) async-start(f32[16,1,592]{2,1,0:T(1,128)} %broadcast_in_dim.12), calls=%async_computation.2 | async-start | bytes 81920 | tf_op jit(solution)/shard_map/all_to_all | solution.py:67
  62.5 6.7 %copy-start.9 = (bf16[64,96]{0,1:T(8,128)(2,1)S(1)}, bf16[64,96]{0,1:T(8,128)(2,1)}, u32[]{:S(2)}) copy-start(bf16[64,96]{0,1:T(8,128)(2,1)} %copy.61) | copy-start | bytes 36868
  65.0 7.9 %copy-start.1 = (bf16[4,256,1280]{1,2,0:T(8,128)(2,1)S(1)}, bf16[4,256,1280]{1,2,0:T(8,128)(2,1)}, u32[]{:S(2)}) copy-start(bf16[4,256,1280]{1,2,0:T(8,128)(2,1)} %all-gather.2.cloned.1.call-done) | copy-start | bytes 7864324
  65.0 0.6 copy-start.13
  65.0 4.2 %copy-start.14 = (f32[4,256]{1,0:T(4,128)}, f32[4,256]{1,0:T(4,128)S(1)}, u32[]{:S(2)}) copy-start(f32[4,256]{1,0:T(4,128)S(1)} %get-tuple-element.16) | copy-start | bytes 12292
  72.8 2.1 copy-start.8
  72.8 2.1 copy-start.24
  72.9 2.1 copy-start.25
  74.9 6.8 %copy-start.10 = (s32[8,8]{1,0:T(8,128)S(1)}, s32[8,8]{1,0:T(8,128)}, u32[]{:S(2)}) copy-start(s32[8,8]{1,0:T(8,128)} %get-tuple-element.13) | copy-start | bytes 772
  74.9 7.1 %copy-start.12 = (s32[8,8]{1,0:T(8,128)S(1)}, s32[8,8]{1,0:T(8,128)}, u32[]{:S(2)}) copy-start(s32[8,8]{1,0:T(8,128)} %get-tuple-element.14) | copy-start | bytes 772
  74.9 7.1 %copy-start.17 = (bf16[8,8]{1,0:T(8,128)(2,1)S(1)}, bf16[8,8]{1,0:T(8,128)(2,1)}, u32[]{:S(2)}) copy-start(bf16[8,8]{1,0:T(8,128)(2,1)} %compare_convert_fusion) | copy-start | bytes 388
  74.9 43.4 %copy-start.6 = (bf16[16,80,512]{2,1,0:T(8,128)(2,1)S(1)}, bf16[16,80,512]{2,1,0:T(8,128)(2,1)}, u32[]{:S(2)}) copy-start(bf16[16,80,512]{2,1,0:T(8,128)(2,1)} %copy-done.5) | copy-start | bytes 3932164
  76.5 54.5 %copy-start.15 = (s32[1,512]{1,0:T(1,128)S(1)}, s32[1,512]{1,0:T(1,128)}, u32[]{:S(2)}) copy-start(s32[1,512]{1,0:T(1,128)} %param.23) | copy-start | bytes 6148
  76.5 21.6 %all-to-all-start = ((bf16[16,16,1280]{2,1,0:T(8,128)(2,1)}), bf16[16,16,1280]{2,1,0:T(8,128)(2,1)S(1)}, u32[]{:S(2)}, u32[]{:S(2)}) async-start(bf16[16,16,1280]{2,1,0:T(8,128)(2,1)} %bitcast.12), calls=%async_computation | async-start | bytes 1310720 | tf_op jit(solution)/shard_map/all_to_all | solution.py:171
  99.3 13.6 %all-to-all-start.3 = ((bf16[16,16,80]{2,1,0:T(8,128)(2,1)}), bf16[16,16,80]{2,1,0:T(8,128)(2,1)S(1)}, u32[]{:S(2)}, u32[]{:S(2)}) async-start(bf16[16,16,80]{2,1,0:T(8,128)(2,1)} %bitcast.99), calls=%async_computation.3 | async-start | bytes 131072 | tf_op jit(solution)/shard_map/all_to_all | solution.py:178
  114.0 10.8 %all-to-all-start.4 = ((bf16[8,2,5120]{2,1,0:T(2,128)(2,1)}), bf16[8,2,5120]{2,1,0:T(2,128)(2,1)S(1)}, u32[]{:S(2)}, u32[]{:S(2)}) async-start(bf16[8,2,5120]{2,1,0:T(2,128)(2,1)} %copy.65), calls=%async_computation.4 | async-start | bytes 327680 | tf_op jit(solution)/shard_map/all_to_all | solution.py:187
  118.4 12.7 %collective-permute-start = (bf16[16,80,512]{2,1,0:T(8,128)(2,1)S(1)}, bf16[16,80,512]{2,1,0:T(8,128)(2,1)}, u32[]{:S(2)}, u32[]{:S(2)}) collective-permute-start(bf16[16,80,512]{2,1,0:T(8,128)(2,1)S(1)} %copy-done.6), channel_id=1, source_target_pairs={{0,16},{16,0},{32,48},{48,32},{64,80},{80,64},{96,112},{112,96},{1... | collective-permute-start | bytes 3932168 | tf_op jit(solution)/shard_map/ppermute | solution.py:118
  126.5 25.3 %all-to-all-start.5 = ((bf16[16,512,80]{1,2,0:T(8,128)(2,1)}), bf16[16,512,80]{1,2,0:T(8,128)(2,1)}, u32[]{:S(2)}, u32[]{:S(2)}) async-start(bf16[16,512,80]{1,2,0:T(8,128)(2,1)} %broadcast_in_dim.14), calls=%async_computation.5 | async-start | bytes 2621440 | tf_op jit(solution)/shard_map/all_to_all | solution.py:67
  130.9 132.1 %reduce-scatter.5.cloned.1.call-start = ((), (), s32[]{:S(2)}) async-start(), calls=%async_computation.10 | async-start | bytes 8912896 | tf_op jit(solution)/shard_map/reduce_scatter | solution.py:211
  167.0 2.2 slice-start
  168.0 2.8 %slice-start.1 = ((s8[8388608]{0:T(1024)(128)(4,1)}), s8[4194304]{0:T(1024)(128)(4,1)S(1)}, s32[]{:S(2)}) async-start(s8[8388608]{0:T(1024)(128)(4,1)} %bitcast.102), calls=%async_computation.12 | async-start | bytes 8388608
  177.6 0.7 copy-start.16
Sparse Core Ops, SparseCore 0:
  9.5 52.9 all-gather.1
  65.9 99.8 reduce-scatter.2
  177.8 85.1 reduce-scatter.4

commit v10 on v6

--- a/solution.py
+++ b/solution.py
@@ -111,7 +111,9 @@
     contract_first = (((0,), (1,)), ((), ()))
     my_core = my_shard % 2
     kv_stack = jnp.stack([cross_key, cross_value], 0)
-    my_kind = lax.dynamic_index_in_dim(kv_stack, my_core, 0, keepdims=False)
+    full_patches = lax.all_gather(patches, "fsdp", axis=2, tiled=True)
+    after_patches = full_patches[0, 0, 0] * 0
+    my_kind = lax.dynamic_index_in_dim(kv_stack, my_core, 0, keepdims=False) + after_patches
     my_kind = jnp.transpose(my_kind.reshape(feat_vis, parts, head_cols), (1, 0, 2))
     my_kind = lax.all_to_all(my_kind, "fsdp", split_axis=0, concat_axis=0, tiled=True)
     core_pairs = [(j, j ^ 1) for j in range(lax.axis_size("img"))]
@@ -132,7 +134,6 @@
         scatter_dimension=0,
         tiled=True,
     )
-    full_patches = lax.all_gather(patches, "fsdp", axis=2, tiled=True)
     context = layer_norm(full_patches, context_gain).astype(jnp.bfloat16)
     latent_normed = layer_norm(latent_init, latent_gain).astype(jnp.bfloat16)
     res_q_rows = jnp.dot(latent_normed, res_query, preferred_element_type=jnp.float32).astype(

time: 273 us -> 298 us (1.092)
  waiting for transfers between devices: 164 us -> 196 us
  starting transfers between devices: 32.4 us -> 27.5 us
    all_gather x1, waiting for transfers between devices: 4.37 us -> 37.6 us  [local(): full_patches = lax.all_gather(patches, 'fsdp', axis=2, tiled=True)]
    all_to_all x2, waiting for transfers between devices: 20.8 us -> 28.4 us  [gather_blocks(): lax.all_to_all(spread, axis_name, split_axis=0, concat_axis=0, tiled=True)]
    reduce_scatter x1, waiting for transfers between devices: 6.79 us -> 0.02 us  [local(): lax.psum_scatter(lax.dot_general(cross_query, gained, contract_first, pre...]
    all_to_all x1, waiting for transfers between devices: 17.5 us -> 23.4 us  [local(): lax.all_to_all(my_kind, 'fsdp', split_axis=0, concat_axis=0, tiled=True)]
    all_to_all x1, waiting for transfers between devices: 15.1 us -> 10.9 us  [local(): lax.all_to_all(head_part.reshape(parts, row_part, vis_width), 'fsdp', spl...]
    all_to_all x1, starting transfers between devices: 8.02 us -> 4.68 us  [local(): lax.all_to_all(my_kind, 'fsdp', split_axis=0, concat_axis=0, tiled=True)]
    reduce_scatter x1, waiting for transfers between devices: 84.7 us -> 81.5 us  [local(): lax.psum_scatter(lax.dot_general(cross_out, attended, (((0,), (0,)), ((),...]
  transfers between devices with their start and end apart: 10 -> 10, of which waited for: 8 -> 8; matrix products, arithmetic and copies ran while one was open for 16% -> 14% of each run, Pallas kernels for 0% -> 0%
where the time goes in v10:
time: 298 us; the launch traced here: 297 us
  waiting for transfers between devices  196 us (66%)
  matrix products  37.5 us (13%)
  starting transfers between devices  27.5 us (9%)
  between operations  15.6 us (5%)
  local copies, waits for them, and re-layouts  11.9 us (4%)
  other arithmetic  8.82 us (3%)
    reduce_scatter x1, waiting for transfers between devices, local(): lax.psum_scatter(lax.dot_general(cross_out, attended, (((0,), (0,)), ((),...  81.5 us
    all_gather x1, waiting for transfers between devices, local(): full_patches = lax.all_gather(patches, 'fsdp', axis=2, tiled=True)  37.6 us
    all_to_all x2, waiting for transfers between devices, gather_blocks(): lax.all_to_all(spread, axis_name, split_axis=0, concat_axis=0, tiled=True)  28.4 us
    all_to_all x1, waiting for transfers between devices, local(): lax.all_to_all(my_kind, 'fsdp', split_axis=0, concat_axis=0, tiled=True)  23.4 us
    dot_general x1, matrix products, local(): lax.dot_general(cross_query, gained, contract_first, preferred_element_ty...  11.3 us
    all_to_all x1, waiting for transfers between devices, local(): lax.all_to_all(head_part.reshape(parts, row_part, vis_width), 'fsdp', spl...  10.9 us
    all_to_all x2, starting transfers between devices, gather_blocks(): lax.all_to_all(spread, axis_name, split_axis=0, concat_axis=0, tiled=True)  9.62 us
    all_to_all x1, waiting for transfers between devices, local(): lax.all_to_all(jnp.transpose(resampled_rows.reshape(row_part, parts, feat...  7.59 us
  transfers between devices with their start and end apart: 10, of which 8 were waited for; matrix products, arithmetic and copies ran while one was open for 14% of the time, Pallas kernels for 0%

profile of v10, /device:TPU:0, one launch (start us, length us, event | category | flops | bytes accessed | tf_op | source)
XLA Modules:
  0.0 297.1 jit_solution(14661173686827522630)
XLA Ops:
  6.5 0.7 all-gather.2.cloned.1.call-update
  7.3 11.3 %fusion = bf16[8192,512]{0,1:T(8,128)(2,1)} fusion(bf16[512,8192]{1,0:T(8,128)(2,1)} %param.34, bf16[512,512]{1,0:T(8,128)(2,1)} %param.19, f32[512]{0:T(512)} %param.20), kind=kOutput, calls=%fused_computation.3 | convolution fusion | flops 4299948032 | bytes 17303552 | tf_op jit(solution)/shard_map/dot_general | solution.py:130
  18.7 0.8 copy-done.3
  19.6 0.1 convert_reduce_fusion.2
  19.7 0.3 convolution_convert_fusion.8
  20.0 0.1 copy.61
  20.1 0.3 convolution_convert_fusion.9
  20.4 0.1 copy.59
  20.5 37.6 %all-gather.2.cloned.1.call-done = bf16[4,256,1280]{1,2,0:T(8,128)(2,1)} async-done(((bf16[4,256,80]{1,2,0:T(8,128)(2,1)}), bf16[4,256,1280]{1,2,0:T(8,128)(2,1)}) %all-gather.2.cloned.1.call-update) | async-done | bytes 2621456 | tf_op jit(solution)/shard_map/all_gather | solution.py:114
  58.2 2.4 convert_reduce_fusion
  60.6 3.6 %convolution_convert_fusion.4 = bf16[4,256,96]{1,2,0:T(8,128)(2,1)} fusion(bf16[4,256,1280]{1,2,0:T(8,128)(2,1)} %all-gather.2.cloned.1.call-done, f32[1280]{0:T(1024)S(1)} %copy-done.12, f32[4,256]{1,0:T(4,128)S(1)} %get-tuple-element.16, f32[4,256]{1,0:T(4,128)S(1)} %get-tuple-element.15, bf16[1280,96]{0,1:T(8,128)(2,1)S(1)} %copy-done.9), kind=kOutput, calls=%fused_computation.38 | convolution fusion | flops 258310144 | bytes 3077120 | tf_op jit(solution)/shard_map/npv,vk->npk/dot_general | solution.py:143
  64.3 2.3 fusion.66
  66.6 2.0 convolution_convert_fusion.5
  68.7 0.3 convolution_convert_fusion.6
  69.0 1.2 convolution_convert_fusion.3
  70.2 4.8 %all-to-all-start = ((bf16[16,16,1280]{2,1,0:T(8,128)(2,1)}), bf16[16,16,1280]{2,1,0:T(8,128)(2,1)S(1)}, u32[]{:S(2)}, u32[]{:S(2)}) async-start(bf16[16,16,1280]{2,1,0:T(8,128)(2,1)} %bitcast.107), calls=%async_computation | async-start | bytes 1310720 | tf_op jit(solution)/shard_map/all_to_all | solution.py:172
  75.0 0.6 slice.16
  76.2 1.9 fusion.14
  78.1 0.5 copy.78
  78.6 1.8 copy.90
  80.4 10.9 %all-to-all-done = bf16[16,16,1280]{2,1,0:T(8,128)(2,1)S(1)} async-done(((bf16[16,16,1280]{2,1,0:T(8,128)(2,1)}), bf16[16,16,1280]{2,1,0:T(8,128)(2,1)S(1)}, u32[]{:S(2)}, u32[]{:S(2)}) %all-to-all-start) | async-done | bytes 655392 | tf_op jit(solution)/shard_map/all_to_all | solution.py:172
  91.3 4.7 %all-to-all-start.1 = ((bf16[16,80,512]{2,1,0:T(8,128)(2,1)}), bf16[16,80,512]{2,1,0:T(8,128)(2,1)}, u32[]{:S(2)}, u32[]{:S(2)}) async-start(bf16[16,80,512]{2,1,0:T(8,128)(2,1)} %bitcast.99), calls=%async_computation.1 | async-start | bytes 2621440 | tf_op jit(solution)/shard_map/all_to_all | solution.py:118
  96.0 0.3 convert_reduce_fusion.3
  96.3 0.2 fusion.20
  96.5 0.1 convolution_convert_fusion.10
  96.7 0.1 convert_reduce_fusion.1
  96.8 0.1 fusion.42
  96.9 23.4 %all-to-all-done.1 = bf16[16,80,512]{2,1,0:T(8,128)(2,1)} async-done(((bf16[16,80,512]{2,1,0:T(8,128)(2,1)}), bf16[16,80,512]{2,1,0:T(8,128)(2,1)}, u32[]{:S(2)}, u32[]{:S(2)}) %all-to-all-start.1) | async-done | bytes 1310752 | tf_op jit(solution)/shard_map/all_to_all | solution.py:118
  120.3 1.2 slice.17
  122.1 0.6 broadcast_in_dim.12
  122.8 5.9 %all-to-all-start.2 = ((f32[16,1,592]{2,1,0:T(1,128)}), f32[16,1,592]{2,1,0:T(1,128)S(1)}, u32[]{:S(2)}, u32[]{:S(2)}) async-start(f32[16,1,592]{2,1,0:T(1,128)} %broadcast_in_dim.12), calls=%async_computation.2 | async-start | bytes 81920 | tf_op jit(solution)/shard_map/all_to_all | solution.py:67
  128.7 7.7 %all-to-all-done.2 = f32[16,1,592]{2,1,0:T(1,128)S(1)} async-done(((f32[16,1,592]{2,1,0:T(1,128)}), f32[16,1,592]{2,1,0:T(1,128)S(1)}, u32[]{:S(2)}, u32[]{:S(2)}) %all-to-all-start.2) | async-done | bytes 37920 | tf_op jit(solution)/shard_map/all_to_all | solution.py:67
  136.5 0.1 mul.213
  136.5 0.1 multiply_convert_fusion.1
  136.6 0.1 reshape.220
  136.7 0.6 copy.91
  137.4 3.5 %all-to-all-start.3 = ((bf16[16,16,80]{2,1,0:T(8,128)(2,1)}), bf16[16,16,80]{2,1,0:T(8,128)(2,1)S(1)}, u32[]{:S(2)}, u32[]{:S(2)}) async-start(bf16[16,16,80]{2,1,0:T(8,128)(2,1)} %bitcast.100), calls=%async_computation.3 | async-start | bytes 131072 | tf_op jit(solution)/shard_map/all_to_all | solution.py:179
  140.9 7.6 %all-to-all-done.3 = bf16[16,16,80]{2,1,0:T(8,128)(2,1)S(1)} async-done(((bf16[16,16,80]{2,1,0:T(8,128)(2,1)}), bf16[16,16,80]{2,1,0:T(8,128)(2,1)S(1)}, u32[]{:S(2)}, u32[]{:S(2)}) %all-to-all-start.3) | async-done | bytes 40992 | tf_op jit(solution)/shard_map/all_to_all | solution.py:179
  148.5 0.2 reshape.227
  148.7 0.2 convolution_convert_fusion.2
  148.8 0.8 copy.65
  149.7 4.1 %all-to-all-start.4 = ((bf16[8,2,5120]{2,1,0:T(2,128)(2,1)}), bf16[8,2,5120]{2,1,0:T(2,128)(2,1)S(1)}, u32[]{:S(2)}, u32[]{:S(2)}) async-start(bf16[8,2,5120]{2,1,0:T(2,128)(2,1)} %copy.65), calls=%async_computation.4 | async-start | bytes 327680 | tf_op jit(solution)/shard_map/all_to_all | solution.py:188
  153.8 0.1 fusion.52
  153.9 0.7 collective-permute-start
  154.6 5.7 %all-to-all-done.4 = bf16[8,2,5120]{2,1,0:T(2,128)(2,1)S(1)} async-done(((bf16[8,2,5120]{2,1,0:T(2,128)(2,1)}), bf16[8,2,5120]{2,1,0:T(2,128)(2,1)S(1)}, u32[]{:S(2)}, u32[]{:S(2)}) %all-to-all-start.4) | async-done | bytes 163872 | tf_op jit(solution)/shard_map/all_to_all | solution.py:188
  160.2 0.3 fusion.2
  160.5 0.2 broadcast_in_dim.13
  160.7 0.1 copy.67
  160.8 1.2 broadcast_in_dim.14
  162.0 3.7 %all-to-all-start.5 = ((bf16[16,512,80]{1,2,0:T(8,128)(2,1)}), bf16[16,512,80]{1,2,0:T(8,128)(2,1)S(1)}, u32[]{:S(2)}, u32[]{:S(2)}) async-start(bf16[16,512,80]{1,2,0:T(8,128)(2,1)} %broadcast_in_dim.14), calls=%async_computation.5 | async-start | bytes 2621440 | tf_op jit(solution)/shard_map/all_to_all | solution.py:67
  165.8 20.7 %all-to-all-done.5 = bf16[16,512,80]{1,2,0:T(8,128)(2,1)S(1)} async-done(((bf16[16,512,80]{1,2,0:T(8,128)(2,1)}), bf16[16,512,80]{1,2,0:T(8,128)(2,1)S(1)}, u32[]{:S(2)}, u32[]{:S(2)}) %all-to-all-start.5) | async-done | bytes 1310752 | tf_op jit(solution)/shard_map/all_to_all | solution.py:67
  186.5 6.8 %reduce-precision_reduce_fusion = bf16[512,2,512]{2,0,1:T(8,128)(2,1)S(1)} fusion(bf16[16,1,80,512]{3,2,1,0:T(8,128)(2,1)} %bitcast.24, bf16[16,1,80,512]{3,2,1,0:T(8,128)(2,1)} %bitcast.23, bf16[16,512,80]{1,2,0:T(8,128)(2,1)S(1)} %all-to-all-done.5), kind=kOutput, calls=%fused_computation | convolution fusion | flops 1363673088 | bytes 4980736 | tf_op jit(solution)/shard_map/brk,bskc->brsc/dot_general | solution.py:193
  193.3 0.3 convert_element_type.168
  193.6 0.4 constant_dynamic-slice_fusion.1
  194.0 0.1 copy.70
  194.1 1.2 multiply_convert_fusion
  195.3 0.2 copy.76
  195.6 0.9 fusion.7
  196.5 1.0 fusion.16
  197.5 0.2 slice-done
  197.7 1.5 slice-done.1
  199.2 6.9 %fusion.1 = bf16[8192,512]{0,1:T(8,128)(2,1)} fusion(bf16[512,512]{1,0:T(8,128)(2,1)S(1)} %bitcast.112, bf16[512,8192]{1,0:T(8,128)(2,1)S(1)} %bitcast.104), kind=kOutput, calls=%fused_computation.4 | convolution fusion | flops 4299161600 | bytes 17301504 | tf_op jit(solution)/shard_map/dot_general | solution.py:214
  206.9 81.5 %reduce-scatter.5.cloned.1.call-done = bf16[512,512]{0,1:T(8,128)(2,1)} async-done(((bf16[8192,512]{0,1:T(8,128)(2,1)}), bf16[512,512]{0,1:T(8,128)(2,1)}) %reduce-scatter.5.cloned.1.call-update) | async-done | bytes 524304 | tf_op jit(solution)/shard_map/reduce_scatter | solution.py:213
  288.4 2.2 convert_add_fusion
  (56 shorter events, 0.4 us)
Async XLA Ops:
  6.5 62.5 %copy-start = (bf16[96,1280]{1,0:T(8,128)(2,1)S(1)}, bf16[96,1280]{1,0:T(8,128)(2,1)}, u32[]{:S(2)}) copy-start(bf16[96,1280]{1,0:T(8,128)(2,1)} %param.32) | copy-start | bytes 737284
  6.5 51.6 %all-gather.2.cloned.1.call-start = ((), (), s32[]{:S(2)}) async-start(), calls=%async_computation.8 | async-start | bytes 2785280 | tf_op jit(solution)/shard_map/all_gather | solution.py:114
  7.3 186.9 %reduce-scatter.3.cloned.1.call-start = ((), (), s32[]{:S(2)}) async-start(), calls=%async_computation.9 | async-start | bytes 8912896 | tf_op jit(solution)/shard_map/reduce_scatter | solution.py:129
  18.6 0.9 copy-start.3
  18.6 1.1 copy-start.9
  18.6 1.1 copy-start.11
  18.7 1.5 copy-start.10
  18.7 1.8 copy-start.5
  18.7 42.0 %copy-start.12 = (f32[1280]{0:T(1024)S(1)}, f32[1280]{0:T(1024)}, u32[]{:S(2)}) copy-start(f32[1280]{0:T(1024)} %param.27) | copy-start | bytes 15364
  60.6 6.0 %copy-start.1 = (bf16[4,256,1280]{1,2,0:T(8,128)(2,1)S(1)}, bf16[4,256,1280]{1,2,0:T(8,128)(2,1)}, u32[]{:S(2)}) copy-start(bf16[4,256,1280]{1,2,0:T(8,128)(2,1)} %all-gather.2.cloned.1.call-done) | copy-start | bytes 7864324
  66.6 2.1 copy-start.13
  70.2 21.1 %all-to-all-start = ((bf16[16,16,1280]{2,1,0:T(8,128)(2,1)}), bf16[16,16,1280]{2,1,0:T(8,128)(2,1)S(1)}, u32[]{:S(2)}, u32[]{:S(2)}) async-start(bf16[16,16,1280]{2,1,0:T(8,128)(2,1)} %bitcast.107), calls=%async_computation | async-start | bytes 1310720 | tf_op jit(solution)/shard_map/all_to_all | solution.py:172
  78.1 18.2 %copy-start.2 = (bf16[512,512]{1,0:T(8,128)(2,1)S(1)}, bf16[512,512]{1,0:T(8,128)(2,1)}, u32[]{:S(2)}) copy-start(bf16[512,512]{1,0:T(8,128)(2,1)} %param.19) | copy-start | bytes 1572868
  78.1 18.7 %copy-start.4 = (bf16[64,1280]{1,0:T(8,128)(2,1)S(1)}, bf16[64,1280]{1,0:T(8,128)(2,1)}, u32[]{:S(2)}) copy-start(bf16[64,1280]{1,0:T(8,128)(2,1)} %param.26) | copy-start | bytes 491524
  78.1 44.0 %copy-start.8 = (f32[80]{0:T(128)S(1)}, f32[80]{0:T(128)}, u32[]{:S(2)}) copy-start(f32[80]{0:T(128)} %param.33) | copy-start | bytes 964
  91.3 29.0 %all-to-all-start.1 = ((bf16[16,80,512]{2,1,0:T(8,128)(2,1)}), bf16[16,80,512]{2,1,0:T(8,128)(2,1)}, u32[]{:S(2)}, u32[]{:S(2)}) async-start(bf16[16,80,512]{2,1,0:T(8,128)(2,1)} %bitcast.99), calls=%async_computation.1 | async-start | bytes 2621440 | tf_op jit(solution)/shard_map/all_to_all | solution.py:118
  96.0 69.8 %copy-start.6 = (s32[1,512]{1,0:T(1,128)S(1)}, s32[1,512]{1,0:T(1,128)}, u32[]{:S(2)}) copy-start(s32[1,512]{1,0:T(1,128)} %param.23) | copy-start | bytes 6148
  122.8 13.7 %all-to-all-start.2 = ((f32[16,1,592]{2,1,0:T(1,128)}), f32[16,1,592]{2,1,0:T(1,128)S(1)}, u32[]{:S(2)}, u32[]{:S(2)}) async-start(f32[16,1,592]{2,1,0:T(1,128)} %broadcast_in_dim.12), calls=%async_computation.2 | async-start | bytes 81920 | tf_op jit(solution)/shard_map/all_to_all | solution.py:67
  137.4 11.1 %all-to-all-start.3 = ((bf16[16,16,80]{2,1,0:T(8,128)(2,1)}), bf16[16,16,80]{2,1,0:T(8,128)(2,1)S(1)}, u32[]{:S(2)}, u32[]{:S(2)}) async-start(bf16[16,16,80]{2,1,0:T(8,128)(2,1)} %bitcast.100), calls=%async_computation.3 | async-start | bytes 131072 | tf_op jit(solution)/shard_map/all_to_all | solution.py:179
  149.7 10.6 %all-to-all-start.4 = ((bf16[8,2,5120]{2,1,0:T(2,128)(2,1)}), bf16[8,2,5120]{2,1,0:T(2,128)(2,1)S(1)}, u32[]{:S(2)}, u32[]{:S(2)}) async-start(bf16[8,2,5120]{2,1,0:T(2,128)(2,1)} %copy.65), calls=%async_computation.4 | async-start | bytes 327680 | tf_op jit(solution)/shard_map/all_to_all | solution.py:188
  153.9 12.0 %collective-permute-start = (bf16[16,80,512]{2,1,0:T(8,128)(2,1)}, bf16[16,80,512]{2,1,0:T(8,128)(2,1)}, u32[]{:S(2)}, u32[]{:S(2)}) collective-permute-start(bf16[16,80,512]{2,1,0:T(8,128)(2,1)} %all-to-all-done.1), channel_id=1, source_target_pairs={{0,16},{16,0},{32,48},{48,32},{64,80},{80,64},{96,112},{112,96},{1... | collective-permute-start | bytes 3932168 | tf_op jit(solution)/shard_map/ppermute | solution.py:120
  162.0 24.5 %all-to-all-start.5 = ((bf16[16,512,80]{1,2,0:T(8,128)(2,1)}), bf16[16,512,80]{1,2,0:T(8,128)(2,1)S(1)}, u32[]{:S(2)}, u32[]{:S(2)}) async-start(bf16[16,512,80]{1,2,0:T(8,128)(2,1)} %broadcast_in_dim.14), calls=%async_computation.5 | async-start | bytes 2621440 | tf_op jit(solution)/shard_map/all_to_all | solution.py:67
  165.7 122.7 %reduce-scatter.5.cloned.1.call-start = ((), (), s32[]{:S(2)}) async-start(), calls=%async_computation.10 | async-start | bytes 8912896 | tf_op jit(solution)/shard_map/reduce_scatter | solution.py:213
  195.5 2.2 slice-start
  196.5 2.8 slice-start.1
  206.2 0.7 copy-start.7
Sparse Core Ops, SparseCore 0:
  9.5 48.6 all-gather.1
  61.6 102.3 reduce-scatter.2
  206.3 82.0 reduce-scatter.4

commit v11 on v5

--- a/solution.py
+++ b/solution.py
@@ -109,10 +109,21 @@
     slot_count = wanted_images.shape[1]
     cross_heads = head_cols // HEAD
     contract_first = (((0,), (1,)), ((), ()))
-    kv_weights = jnp.stack([cross_key, cross_value], 0).reshape(2, feat_vis, parts, head_cols)
-    kv_weights = lax.all_to_all(
-        jnp.transpose(kv_weights, (2, 0, 1, 3)), "fsdp", split_axis=0, concat_axis=0, tiled=True
-    )
+    img_count = lax.axis_size("img")
+    quarters = img_count // 2
+    quarter_cols = head_cols // quarters
+    kv_stack = jnp.stack([cross_key, cross_value], 0).reshape(
+        2, feat_vis, parts, quarters, quarter_cols
+    )
+    my_kind = lax.dynamic_index_in_dim(kv_stack, my_shard % 2, 0, keepdims=False)
+    my_part = lax.dynamic_index_in_dim(my_kind, my_shard // 2, 2, keepdims=False)
+    my_part = lax.all_to_all(
+        jnp.transpose(my_part, (1, 0, 2)), "fsdp", split_axis=0, concat_axis=0, tiled=True
+    )
+    all_parts = gather_blocks(my_part, "img", img_count).reshape(
+        quarters, 2, parts, feat_vis, quarter_cols
+    )
+    kv_weights = jnp.transpose(all_parts, (2, 1, 3, 0, 4)).reshape(parts, 2, feat_vis, head_cols)
     text_f = text_states.astype(jnp.float32)
     gained = (text_f * text_gain).astype(jnp.bfloat16)
     after_weights = kv_weights[0, 0, 0, 0].astype(jnp.float32) * 0.0

time: 296 us -> 296 us (level)
  waiting for transfers between devices: 173 us -> 151 us
  blocking collectives: 0 us -> 16.9 us
  local copies, waits for them, and re-layouts: 17.4 us -> 28.8 us
  starting transfers between devices: 32.7 us -> 26.8 us
    all_to_all x1 -> x0, waiting for transfers between devices: 34.5 us -> none  [local(): lax.all_to_all(jnp.transpose(kv_weights, (2, 0, 1, 3)), 'fsdp', split_axi...]
    all_to_all x0 -> x1, blocking collectives: none -> 16.9 us  [local(): lax.all_to_all(jnp.transpose(my_part, (1, 0, 2)), 'fsdp', split_axis=0, c...]
    all_to_all x2 -> x3, waiting for transfers between devices: 26.1 us -> 42.7 us  [gather_blocks(): lax.all_to_all(spread, axis_name, split_axis=0, concat_axis=0, tiled=True)]
    all_to_all x1 -> x0, starting transfers between devices: 8.12 us -> none  [local(): lax.all_to_all(jnp.transpose(kv_weights, (2, 0, 1, 3)), 'fsdp', split_axi...]
    all_to_all x2 -> x3, starting transfers between devices: 8.05 us -> 12.6 us  [gather_blocks(): lax.all_to_all(spread, axis_name, split_axis=0, concat_axis=0, tiled=True)]
    transpose x0 -> x2, local copies, waits for them, and re-layouts: none -> 3.86 us  [the longest x1 3.64 us: local(): jnp.transpose(all_parts, (2, 1, 3, 0, 4))]
    reshape x0 -> x1, local copies, waits for them, and re-layouts: none -> 3.8 us  [local(): jnp.transpose(all_parts, (2, 1, 3, 0, 4))]
    all_to_all x1, waiting for transfers between devices: 14.6 us -> 11.6 us  [local(): lax.all_to_all(head_part.reshape(parts, row_part, vis_width), 'fsdp', spl...]
  transfers between devices with their start and end apart: 9 -> 9, of which waited for: 6 -> 6; matrix products, arithmetic and copies ran while one was open for 19% -> 23% of each run, Pallas kernels for 0% -> 0%
where the time goes in v11:
time: 296 us; the launch traced here: 294 us
  waiting for transfers between devices  151 us (51%)
  matrix products  42.4 us (14%)
  local copies, waits for them, and re-layouts  28.8 us (10%)
  starting transfers between devices  26.8 us (9%)
  blocking collectives  16.9 us (6%)
  between operations  15 us (5%)
  other arithmetic  13.7 us (5%)
    reduce_scatter x1, waiting for transfers between devices, local(): lax.psum_scatter(lax.dot_general(cross_out, attended, (((0,), (0,)), ((),...  81.4 us
    all_to_all x3, waiting for transfers between devices, gather_blocks(): lax.all_to_all(spread, axis_name, split_axis=0, concat_axis=0, tiled=True)  42.7 us
    all_to_all x1, blocking collectives, local(): lax.all_to_all(jnp.transpose(my_part, (1, 0, 2)), 'fsdp', split_axis=0, c...  16.9 us
    all_to_all x3, starting transfers between devices, gather_blocks(): lax.all_to_all(spread, axis_name, split_axis=0, concat_axis=0, tiled=True)  12.6 us
    all_to_all x1, waiting for transfers between devices, local(): lax.all_to_all(head_part.reshape(parts, row_part, vis_width), 'fsdp', spl...  11.6 us
    dot_general x1, matrix products, local(): lax.dot_general(cross_query, gained, contract_first, preferred_element_ty...  11.3 us
    all_to_all x1, waiting for transfers between devices, local(): lax.all_to_all(jnp.transpose(resampled_rows.reshape(row_part, parts, feat...  8.07 us
    dot_general x1, matrix products, local(): jnp.einsum('brk,bskc->brsc', slot_blocks, kv_weights, preferred_element_t...  7.37 us
  transfers between devices with their start and end apart: 9, of which 6 were waited for; matrix products, arithmetic and copies ran while one was open for 23% of the time, Pallas kernels for 0%

profile of v11, /device:TPU:0, one launch (start us, length us, event | category | flops | bytes accessed | tf_op | source)
XLA Modules:
  0.0 294.5 jit_solution(2827506118357460535)
XLA Ops:
  6.5 0.7 all-gather.2.cloned.1.call-update
  7.3 11.3 %fusion = bf16[8192,512]{0,1:T(8,128)(2,1)} fusion(bf16[512,8192]{1,0:T(8,128)(2,1)} %param.34, bf16[512,512]{1,0:T(8,128)(2,1)} %param.19, f32[512]{0:T(512)} %param.20), kind=kOutput, calls=%fused_computation.3 | convolution fusion | flops 4299948032 | bytes 17303552 | tf_op jit(solution)/shard_map/dot_general | solution.py:135
  18.7 1.3 copy-done.4
  20.0 0.9 stack.9
  20.9 3.2 %stack.10 = bf16[1,80,16,4,128]{4,3,2,1,0:T(4,128)(2,1)S(1)} reshape(bf16[80,8192]{1,0:T(8,128)(2,1)} %param.36) | data formatting | bytes 2621440 | tf_op jit(solution)/shard_map/stack | solution.py:115
  24.2 2.0 fusion.17
  26.2 0.2 copy.102
  26.4 16.9 %all_to_all.39 = bf16[16,80,128]{2,1,0:T(8,128)(2,1)S(1)} all-to-all(bf16[16,80,128]{2,1,0:T(8,128)(2,1)S(1)} %bitcast.105), channel_id=1, replica_groups=mesh['img'=8,'fsdp'=16] {'fsdp'}, dimensions={0} | all-to-all | bytes 655360 | tf_op jit(solution)/shard_map/all_to_all | solution.py:120
  43.4 2.0 broadcast_in_dim.14
  45.3 4.5 %all-to-all-start.2 = ((bf16[8,16,80,128]{3,2,1,0:T(8,128)(2,1)}), bf16[8,16,80,128]{3,2,1,0:T(8,128)(2,1)S(1)}, u32[]{:S(2)}, u32[]{:S(2)}) async-start(bf16[8,16,80,128]{3,2,1,0:T(8,128)(2,1)} %broadcast_in_dim.14), calls=%async_computation.2 | async-start | bytes 5242880 | tf_op jit(solution)/shard_map/all_to_all | solution.py:67
  50.0 0.5 copy-done.18
  50.6 1.8 convolution_convert_fusion.8
  52.4 1.4 copy.72
  53.8 1.8 convolution_convert_fusion.9
  55.7 1.4 copy.70
  57.1 0.8 fusion.15
  57.9 1.3 compare_convert_fusion
  59.2 1.3 add_select_fusion.1
  60.5 22.2 %all-to-all-done.2 = bf16[8,16,80,128]{3,2,1,0:T(8,128)(2,1)S(1)} async-done(((bf16[8,16,80,128]{3,2,1,0:T(8,128)(2,1)}), bf16[8,16,80,128]{3,2,1,0:T(8,128)(2,1)S(1)}, u32[]{:S(2)}, u32[]{:S(2)}) %all-to-all-start.2) | async-done | bytes 2621472 | tf_op jit(solution)/shard_map/all_to_all | solution.py:67
  82.6 3.6 %copy.74 = bf16[16,2,80,4,128]{4,3,2,1,0:T(4,128)(2,1)} copy(bf16[16,2,80,4,128]{4,2,0,1,3:T(8,128)(2,1)S(1)} %bitcast.100) | data formatting | bytes 5242880 | tf_op jit(solution)/shard_map/transpose | solution.py:126
  86.3 3.8 %reshape.229 = bf16[16,2,80,512]{3,2,1,0:T(8,128)(2,1)S(1)} reshape(bf16[16,2,80,4,128]{4,3,2,1,0:T(4,128)(2,1)} %copy.74) | data formatting | bytes 5242880 | tf_op jit(solution)/shard_map/reshape | solution.py:126
  90.1 0.5 slice.20
  91.3 0.6 broadcast_in_dim.15
  91.9 3.7 %all-to-all-start.3 = ((f32[16,1,592]{2,1,0:T(1,128)}), f32[16,1,592]{2,1,0:T(1,128)S(1)}, u32[]{:S(2)}, u32[]{:S(2)}) async-start(f32[16,1,592]{2,1,0:T(1,128)} %broadcast_in_dim.15), calls=%async_computation.3 | async-start | bytes 81920 | tf_op jit(solution)/shard_map/all_to_all | solution.py:67
  95.7 2.5 convert_reduce_fusion
  98.2 3.7 %convolution_convert_fusion.4 = bf16[4,256,96]{1,2,0:T(8,128)(2,1)} fusion(bf16[4,256,1280]{1,2,0:T(8,128)(2,1)} %all-gather.2.cloned.1.call-done, f32[1280]{0:T(1024)S(1)} %copy-done.24, f32[4,256]{1,0:T(4,128)S(1)} %get-tuple-element.16, f32[4,256]{1,0:T(4,128)S(1)} %get-tuple-element.15, bf16[1280,96]{0,1:T(8,128)(2,1)S(1)} %copy-done.22), kind=kOutput, calls=%fused_computation.32 | convolution fusion | flops 258310144 | bytes 3077120 | tf_op jit(solution)/shard_map/npv,vk->npk/dot_general | solution.py:149
  102.0 2.3 fusion.60
  104.4 3.0 %convolution_convert_fusion.5 = bf16[4,256,96]{1,2,0:T(8,128)(2,1)S(1)} fusion(bf16[4,256,1280]{1,2,0:T(8,128)(2,1)} %all-gather.2.cloned.1.call-done, f32[1280]{0:T(1024)S(1)} %copy-done.24, f32[4,256]{1,0:T(4,128)S(1)} %get-tuple-element.16, f32[4,256]{1,0:T(4,128)S(1)} %get-tuple-element.15, bf16[1280,96]{0,1:T(8,128)(2,1)} %param.31), kind=kOutput, calls=%fused_computation.33 | convolution fusion | flops 258310144 | bytes 3077120 | tf_op jit(solution)/shard_map/npv,vk->npk/dot_general | solution.py:152
  107.4 0.3 convolution_convert_fusion.6
  107.8 1.2 convolution_convert_fusion.3
  108.9 0.6 copy-done.6
  109.5 7.0 %all-to-all-start = ((bf16[16,16,1280]{2,1,0:T(8,128)(2,1)}), bf16[16,16,1280]{2,1,0:T(8,128)(2,1)S(1)}, u32[]{:S(2)}, u32[]{:S(2)}) async-start(bf16[16,16,1280]{2,1,0:T(8,128)(2,1)} %bitcast.12), calls=%async_computation | async-start | bytes 1310720 | tf_op jit(solution)/shard_map/all_to_all | solution.py:178
  116.6 0.3 convert_reduce_fusion.3
  117.0 0.8 copy.104
  117.9 0.5 copy-done.7
  118.4 11.6 %all-to-all-done = bf16[16,16,1280]{2,1,0:T(8,128)(2,1)S(1)} async-done(((bf16[16,16,1280]{2,1,0:T(8,128)(2,1)}), bf16[16,16,1280]{2,1,0:T(8,128)(2,1)S(1)}, u32[]{:S(2)}, u32[]{:S(2)}) %all-to-all-start) | async-done | bytes 655392 | tf_op jit(solution)/shard_map/all_to_all | solution.py:178
  130.1 0.9 fusion.36
  131.0 0.9 multiply_convert_fusion.1
  132.0 0.6 copy.103
  132.6 3.5 %all-to-all-start.4 = ((bf16[16,16,80]{2,1,0:T(8,128)(2,1)}), bf16[16,16,80]{2,1,0:T(8,128)(2,1)S(1)}, u32[]{:S(2)}, u32[]{:S(2)}) async-start(bf16[16,16,80]{2,1,0:T(8,128)(2,1)} %bitcast.97), calls=%async_computation.4 | async-start | bytes 131072 | tf_op jit(solution)/shard_map/all_to_all | solution.py:185
  136.2 8.1 %all-to-all-done.4 = bf16[16,16,80]{2,1,0:T(8,128)(2,1)S(1)} async-done(((bf16[16,16,80]{2,1,0:T(8,128)(2,1)}), bf16[16,16,80]{2,1,0:T(8,128)(2,1)S(1)}, u32[]{:S(2)}, u32[]{:S(2)}) %all-to-all-start.4) | async-done | bytes 40992 | tf_op jit(solution)/shard_map/all_to_all | solution.py:185
  144.3 0.2 reshape.237
  144.4 0.2 convolution_convert_fusion.2
  144.6 0.8 copy.77
  145.4 3.4 %all-to-all-start.5 = ((bf16[8,2,5120]{2,1,0:T(2,128)(2,1)}), bf16[8,2,5120]{2,1,0:T(2,128)(2,1)S(1)}, u32[]{:S(2)}, u32[]{:S(2)}) async-start(bf16[8,2,5120]{2,1,0:T(2,128)(2,1)} %copy.77), calls=%async_computation.5 | async-start | bytes 327680 | tf_op jit(solution)/shard_map/all_to_all | solution.py:194
  148.9 6.3 %all-to-all-done.5 = bf16[8,2,5120]{2,1,0:T(2,128)(2,1)S(1)} async-done(((bf16[8,2,5120]{2,1,0:T(2,128)(2,1)}), bf16[8,2,5120]{2,1,0:T(2,128)(2,1)S(1)}, u32[]{:S(2)}, u32[]{:S(2)}) %all-to-all-start.5) | async-done | bytes 163872 | tf_op jit(solution)/shard_map/all_to_all | solution.py:194
  155.2 0.3 fusion.2
  155.5 0.2 broadcast_in_dim.16
  155.8 1.2 broadcast_in_dim.17
  157.0 4.4 %all-to-all-start.6 = ((bf16[16,512,80]{1,2,0:T(8,128)(2,1)}), bf16[16,512,80]{1,2,0:T(8,128)(2,1)}, u32[]{:S(2)}, u32[]{:S(2)}) async-start(bf16[16,512,80]{1,2,0:T(8,128)(2,1)} %broadcast_in_dim.17), calls=%async_computation.6 | async-start | bytes 2621440 | tf_op jit(solution)/shard_map/all_to_all | solution.py:67
  161.4 0.3 reduce-scatter.5.cloned.1.call-start
  161.7 20.5 %all-to-all-done.6 = bf16[16,512,80]{1,2,0:T(8,128)(2,1)} async-done(((bf16[16,512,80]{1,2,0:T(8,128)(2,1)}), bf16[16,512,80]{1,2,0:T(8,128)(2,1)}, u32[]{:S(2)}, u32[]{:S(2)}) %all-to-all-start.6) | async-done | bytes 1310752 | tf_op jit(solution)/shard_map/all_to_all | solution.py:67
  182.2 7.4 %reduce-precision_reduce_fusion = bf16[512,2,512]{2,0,1:T(8,128)(2,1)} fusion(bf16[16,2,80,512]{3,2,1,0:T(8,128)(2,1)S(1)} %reshape.229, bf16[16,512,80]{1,2,0:T(8,128)(2,1)} %all-to-all-done.6), kind=kOutput, calls=%fused_computation | convolution fusion | flops 1358430208 | bytes 4980736 | tf_op jit(solution)/shard_map/brk,bskc->brsc/dot_general | solution.py:199
  189.6 1.3 convert_element_type.168
  190.9 0.4 fusion.59
  191.5 1.2 multiply_convert_fusion
  192.7 0.2 copy.87
  192.9 0.9 fusion.7
  193.8 1.0 fusion.11
  194.9 0.2 slice-done
  195.1 1.5 slice-done.1
  196.6 6.9 %fusion.1 = bf16[8192,512]{0,1:T(8,128)(2,1)} fusion(bf16[512,512]{1,0:T(8,128)(2,1)S(1)} %bitcast.106, bf16[512,8192]{1,0:T(8,128)(2,1)S(1)} %bitcast.102), kind=kOutput, calls=%fused_computation.4 | convolution fusion | flops 4299161600 | bytes 17301504 | tf_op jit(solution)/shard_map/dot_general | solution.py:220
  204.3 81.4 %reduce-scatter.5.cloned.1.call-done = bf16[512,512]{0,1:T(8,128)(2,1)} async-done(((bf16[8192,512]{0,1:T(8,128)(2,1)}), bf16[512,512]{0,1:T(8,128)(2,1)}) %reduce-scatter.5.cloned.1.call-update) | async-done | bytes 524304 | tf_op jit(solution)/shard_map/reduce_scatter | solution.py:219
  285.8 2.2 convert_add_fusion
  (82 shorter events, 1.3 us)
Async XLA Ops:
  6.5 101.2 %copy-start = (bf16[96,1280]{1,0:T(8,128)(2,1)S(1)}, bf16[96,1280]{1,0:T(8,128)(2,1)}, u32[]{:S(2)}) copy-start(bf16[96,1280]{1,0:T(8,128)(2,1)} %param.32) | copy-start | bytes 737284
  6.5 89.2 %all-gather.2.cloned.1.call-start = ((), (), s32[]{:S(2)}) async-start(), calls=%async_computation.9 | async-start | bytes 2785280 | tf_op jit(solution)/shard_map/all_gather | solution.py:142
  7.3 184.2 %reduce-scatter.3.cloned.1.call-start = ((), (), s32[]{:S(2)}) async-start(), calls=%async_computation.10 | async-start | bytes 8912896 | tf_op jit(solution)/shard_map/reduce_scatter | solution.py:134
  18.6 1.3 copy-start.4
  43.4 6.4 %copy-start.5 = (bf16[64,1280]{1,0:T(8,128)(2,1)S(1)}, bf16[64,1280]{1,0:T(8,128)(2,1)}, u32[]{:S(2)}) copy-start(bf16[64,1280]{1,0:T(8,128)(2,1)} %param.26) | copy-start | bytes 491524
  43.4 13.7 %copy-start.2 = (bf16[512,512]{1,0:T(8,128)(2,1)S(1)}, bf16[512,512]{1,0:T(8,128)(2,1)}, u32[]{:S(2)}) copy-start(bf16[512,512]{1,0:T(8,128)(2,1)} %param.19) | copy-start | bytes 1572868
  45.3 37.3 %all-to-all-start.2 = ((bf16[8,16,80,128]{3,2,1,0:T(8,128)(2,1)}), bf16[8,16,80,128]{3,2,1,0:T(8,128)(2,1)S(1)}, u32[]{:S(2)}, u32[]{:S(2)}) async-start(bf16[8,16,80,128]{3,2,1,0:T(8,128)(2,1)} %broadcast_in_dim.14), calls=%async_computation.2 | async-start | bytes 5242880 | tf_op jit(solution)/shard_map/all_to_all | solution.py:67
  50.0 0.5 copy-start.18
  50.0 0.6 copy-start.20
  82.6 8.6 %copy-start.12 = (f32[512]{0:T(512)S(1)}, f32[512]{0:T(512)}, u32[]{:S(2)}) copy-start(f32[512]{0:T(512)} %fusion.15) | copy-start | bytes 6148
  82.6 8.6 %copy-start.17 = (f32[80]{0:T(128)S(1)}, f32[80]{0:T(128)}, u32[]{:S(2)}) copy-start(f32[80]{0:T(128)} %param.33) | copy-start | bytes 964
  86.3 11.9 %copy-start.22 = (bf16[1280,96]{0,1:T(8,128)(2,1)S(1)}, bf16[1280,96]{0,1:T(8,128)(2,1)}, u32[]{:S(2)}) copy-start(bf16[1280,96]{0,1:T(8,128)(2,1)} %param.30) | copy-start | bytes 737284
  86.3 11.9 %copy-start.24 = (f32[1280]{0:T(1024)S(1)}, f32[1280]{0:T(1024)}, u32[]{:S(2)}) copy-start(f32[1280]{0:T(1024)} %param.27) | copy-start | bytes 15364
  91.9 17.0 %all-to-all-start.3 = ((f32[16,1,592]{2,1,0:T(1,128)}), f32[16,1,592]{2,1,0:T(1,128)S(1)}, u32[]{:S(2)}, u32[]{:S(2)}) async-start(f32[16,1,592]{2,1,0:T(1,128)} %broadcast_in_dim.15), calls=%async_computation.3 | async-start | bytes 81920 | tf_op jit(solution)/shard_map/all_to_all | solution.py:67
  95.6 6.3 %copy-start.10 = (bf16[64,96]{0,1:T(8,128)(2,1)S(1)}, bf16[64,96]{0,1:T(8,128)(2,1)}, u32[]{:S(2)}) copy-start(bf16[64,96]{0,1:T(8,128)(2,1)} %copy.72) | copy-start | bytes 36868
  95.6 6.3 %copy-start.19 = (f32[64]{0:T(128)S(1)}, f32[64]{0:T(128)}, u32[]{:S(2)}) copy-start(f32[64]{0:T(128)} %copy-done.18) | copy-start | bytes 772
  95.7 6.3 %copy-start.21 = (f32[64]{0:T(128)S(1)}, f32[64]{0:T(128)}, u32[]{:S(2)}) copy-start(f32[64]{0:T(128)} %copy-done.20) | copy-start | bytes 772
  95.7 6.3 %copy-start.23 = (f32[1280]{0:T(1024)S(1)}, f32[1280]{0:T(1024)}, u32[]{:S(2)}) copy-start(f32[1280]{0:T(1024)} %param.28) | copy-start | bytes 15364
  102.0 5.4 %copy-start.9 = (bf16[64,96]{0,1:T(8,128)(2,1)S(1)}, bf16[64,96]{0,1:T(8,128)(2,1)}, u32[]{:S(2)}) copy-start(bf16[64,96]{0,1:T(8,128)(2,1)} %copy.70) | copy-start | bytes 36868
  104.4 3.1 %copy-start.25 = (f32[4,1,64,320]{3,2,0,1:T(8,128)S(1)}, f32[4,1,64,320]{3,2,0,1:T(8,128)}, u32[]{:S(2)}) copy-start(f32[4,1,64,320]{3,2,0,1:T(8,128)} %get-tuple-element.22) | copy-start | bytes 983044
  104.4 12.2 %copy-start.11 = (s32[8,8]{1,0:T(8,128)S(1)}, s32[8,8]{1,0:T(8,128)}, u32[]{:S(2)}) copy-start(s32[8,8]{1,0:T(8,128)} %get-tuple-element.13) | copy-start | bytes 772
  104.4 12.5 %copy-start.13 = (s32[8,8]{1,0:T(8,128)S(1)}, s32[8,8]{1,0:T(8,128)}, u32[]{:S(2)}) copy-start(s32[8,8]{1,0:T(8,128)} %get-tuple-element.14) | copy-start | bytes 772
  104.4 12.5 %copy-start.16 = (bf16[8,8]{1,0:T(8,128)(2,1)S(1)}, bf16[8,8]{1,0:T(8,128)(2,1)}, u32[]{:S(2)}) copy-start(bf16[8,8]{1,0:T(8,128)(2,1)} %compare_convert_fusion) | copy-start | bytes 388
  108.9 0.6 copy-start.6
  108.9 52.7 %copy-start.14 = (s32[1,512]{1,0:T(1,128)S(1)}, s32[1,512]{1,0:T(1,128)}, u32[]{:S(2)}) copy-start(s32[1,512]{1,0:T(1,128)} %param.23) | copy-start | bytes 6148
  109.5 20.4 %all-to-all-start = ((bf16[16,16,1280]{2,1,0:T(8,128)(2,1)}), bf16[16,16,1280]{2,1,0:T(8,128)(2,1)S(1)}, u32[]{:S(2)}, u32[]{:S(2)}) async-start(bf16[16,16,1280]{2,1,0:T(8,128)(2,1)} %bitcast.12), calls=%async_computation | async-start | bytes 1310720 | tf_op jit(solution)/shard_map/all_to_all | solution.py:178
  117.8 0.6 copy-start.7
  130.1 31.6 %copy-start.8 = (f32[16,1,592]{2,0,1:T(8,128)S(1)}, f32[16,1,592]{2,0,1:T(8,128)}, u32[]{:S(2)}) copy-start(f32[16,1,592]{2,0,1:T(8,128)} %copy-done.7) | copy-start | bytes 113668
  132.6 11.6 %all-to-all-start.4 = ((bf16[16,16,80]{2,1,0:T(8,128)(2,1)}), bf16[16,16,80]{2,1,0:T(8,128)(2,1)S(1)}, u32[]{:S(2)}, u32[]{:S(2)}) async-start(bf16[16,16,80]{2,1,0:T(8,128)(2,1)} %bitcast.97), calls=%async_computation.4 | async-start | bytes 131072 | tf_op jit(solution)/shard_map/all_to_all | solution.py:185
  145.4 9.8 %all-to-all-start.5 = ((bf16[8,2,5120]{2,1,0:T(2,128)(2,1)}), bf16[8,2,5120]{2,1,0:T(2,128)(2,1)S(1)}, u32[]{:S(2)}, u32[]{:S(2)}) async-start(bf16[8,2,5120]{2,1,0:T(2,128)(2,1)} %copy.77), calls=%async_computation.5 | async-start | bytes 327680 | tf_op jit(solution)/shard_map/all_to_all | solution.py:194
  157.0 25.2 %all-to-all-start.6 = ((bf16[16,512,80]{1,2,0:T(8,128)(2,1)}), bf16[16,512,80]{1,2,0:T(8,128)(2,1)}, u32[]{:S(2)}, u32[]{:S(2)}) async-start(bf16[16,512,80]{1,2,0:T(8,128)(2,1)} %broadcast_in_dim.17), calls=%async_computation.6 | async-start | bytes 2621440 | tf_op jit(solution)/shard_map/all_to_all | solution.py:67
  161.4 124.4 %reduce-scatter.5.cloned.1.call-start = ((), (), s32[]{:S(2)}) async-start(), calls=%async_computation.11 | async-start | bytes 8912896 | tf_op jit(solution)/shard_map/reduce_scatter | solution.py:219
  192.9 2.2 slice-start
  193.8 2.8 slice-start.1
  203.5 84.4 %copy-start.1 = (bf16[96,1280]{1,0:T(8,128)(2,1)S(1)}, bf16[96,1280]{1,0:T(8,128)(2,1)}, u32[]{:S(2)}) copy-start(bf16[96,1280]{1,0:T(8,128)(2,1)} %param.32) | copy-start | bytes 737284
  203.5 0.7 copy-start.15
  203.6 82.2 %copy-start.3 = (bf16[512,512]{1,0:T(8,128)(2,1)S(1)}, bf16[512,512]{1,0:T(8,128)(2,1)}, u32[]{:S(2)}) copy-start(bf16[512,512]{1,0:T(8,128)(2,1)} %param.19) | copy-start | bytes 1572868
Sparse Core Ops, SparseCore 0:
  9.5 48.6 all-gather.1
  61.6 89.7 reduce-scatter.2
  203.7 82.0 reduce-scatter.4
